TPU v7x, 256 devices: a whole 4x4x8 slice. The times are simulated.
256 devices in a mesh: space: 64 (over z, x, core), head: 4 (over y).
Axes of the slice: x: 4, y: 4, z: 8, core: 2. Of those that a mesh axis runs over, the one named last changes fastest.
Arguments:
- features: bfloat16 [512, 16, 16, 128], P('space', None, None, 'head'), may hold values from -6 to 6
- mask: int32 [512, 16, 16], P('space'), may hold values from 0 to 1, as said below
- conv1_weight: bfloat16 [27, 128, 128], replicated, may hold values from -0.21875 to 0.21875
- conv2_weight: bfloat16 [27, 128, 128], replicated, may hold values from -0.21875 to 0.21875
- down_weight: bfloat16 [8, 128, 512], replicated, may hold values from -0.1875 to 0.1875
- norm_gain: float32 [512], replicated, may hold values from 0.1 to 1.9
- qkv_weight: bfloat16 [512, 3, 512], P(None, None, 'head'), may hold values from -2 to 2
- out_weight: bfloat16 [512, 512], P('head'), may hold values from -0.25 to 0.25
Outputs:
- refined: bfloat16 [512, 16, 16, 128], P('space', None, None, 'head')
- level_out: bfloat16 [16384, 512], P('space', 'head')
Inputs may be any that keep to these rules, and one draw needn't show every extreme that they name: `mask`: A voxel is occupied only inside an active brick of 8^3 aligned voxels; the first brick and its first voxel are always occupied.
All inputs are finite; a program needn't handle non-finite values.
Results may differ from a plain program's by a relative error of at most 0.012.
Values may be sent and summed in bfloat16 or wider, within the bound.
No kernel may reach another device: no remote copies, remote signals or barrier semaphores. Data moves between devices by JAX's collectives and lax.ppermute only.
A program may use at most 64 MiB of HBM per device.

v0:
```python
import jax
import jax.numpy as jnp
from jax import lax
from jax.sharding import PartitionSpec as P

HEADS = 8
KEY_BLOCK = 1024


def with_halo(cells, axis, width):
    count = lax.axis_size(axis)
    ends = count - 1
    head = lax.slice_in_dim(cells, 0, width, axis=0)
    tail = lax.slice_in_dim(cells, cells.shape[0] - width, cells.shape[0], axis=0)
    return jnp.concatenate(
        [
            lax.ppermute(tail, axis, [(i, i + 1) for i in range(ends)]),
            cells,
            lax.ppermute(head, axis, [(i + 1, i) for i in range(ends)]),
        ],
        axis=0,
    )


def convolve(rimmed, weight):
    chans = weight.shape[1]
    kernel = weight.reshape(3, 3, 3, chans, weight.shape[2])
    out = lax.conv_general_dilated(
        rimmed[None],
        kernel,
        window_strides=(1, 1, 1),
        padding=((0, 0), (1, 1), (1, 1)),
        dimension_numbers=("NDHWC", "DHWIO", "NDHWC"),
        preferred_element_type=jnp.float32,
    )
    return out[0]


def to_cells(field):
    nx, ny, nz, count = field.shape
    blocks = field.reshape(nx // 2, 2, ny // 2, 2, nz // 2, 2, count).transpose(0, 2, 4, 1, 3, 5, 6)
    return blocks.reshape(nx // 2 * (ny // 2) * (nz // 2), 8 * count)


def body(
    features, mask, conv1_weight, conv2_weight, down_weight, norm_gain, qkv_weight, out_weight
):
    member = lax.axis_index("head")
    nx, ny, nz, local = features.shape
    width = down_weight.shape[2]
    chans = conv1_weight.shape[1]
    tokens = nx // 2 * (ny // 2) * (nz // 2)
    occupied = mask.astype(jnp.float32)[..., None]
    masked = features * mask.astype(jnp.bfloat16)[..., None]
    rimmed = lax.all_gather(with_halo(masked, "space", 1), "head", axis=3, tiled=True)
    whole_masked = lax.slice_in_dim(rimmed, 1, nx + 1, axis=0)
    pre1 = convolve(rimmed, conv1_weight)
    hidden = (occupied * jax.nn.silu(pre1)).astype(jnp.bfloat16)
    pre2 = convolve(with_halo(hidden, "space", 1), conv2_weight)
    refined_all = (occupied * (whole_masked.astype(jnp.float32) + pre2)).astype(jnp.bfloat16)
    refined = lax.dynamic_slice_in_dim(refined_all, member * local, local, 3)
    coarse = jnp.dot(
        to_cells(refined_all),
        down_weight.reshape(8 * chans, width),
        preferred_element_type=jnp.float32,
    ).astype(jnp.bfloat16)
    wide = coarse.astype(jnp.float32)
    normed = (
        wide * lax.rsqrt(jnp.mean(wide * wide, axis=1, keepdims=True) + 1e-05) * norm_gain
    ).astype(jnp.bfloat16)
    local_cols = qkv_weight.shape[2]
    proj = jnp.dot(
        normed, qkv_weight.reshape(width, 3 * local_cols), preferred_element_type=jnp.float32
    )
    proj = proj.astype(jnp.bfloat16).reshape(tokens, 3, local_cols)
    head_size = width // HEADS
    heads_here = local_cols // head_size
    query = proj[:, 0].reshape(tokens, heads_here, head_size)
    live_cell = (
        mask.reshape(nx // 2, 2, ny // 2, 2, nz // 2, 2)
        .max(axis=(1, 3, 5))
        .reshape(1, -1)
        .astype(jnp.bfloat16)
    )
    span = 2 * local_cols
    live_len = -(-tokens // span) * span
    live_rows = jnp.pad(live_cell, ((0, 0), (0, live_len - tokens))).reshape(-1, span)
    live_count = live_rows.shape[0]
    live_rows = jnp.pad(live_rows, ((0, -(-live_count // 8) * 8 - live_count), (0, 0)))
    piece = jnp.concatenate([proj[:, 1], proj[:, 2]], axis=1)
    piece = jnp.concatenate([piece, live_rows], axis=0)
    rows = piece.shape[0]
    gathered = lax.all_gather(piece[None], "space", axis=0, tiled=True)
    parts = gathered.shape[0]
    count = parts * tokens
    piece_keys = gathered[:, :tokens, :local_cols].reshape(count, heads_here, head_size)
    piece_values = gathered[:, :tokens, local_cols:].reshape(count, heads_here, head_size)
    piece_live = gathered[:, tokens : tokens + live_count].reshape(parts, -1)[:, :tokens].reshape(count)
    bias = jnp.where(piece_live > 0, 0.0, -1e30).astype(jnp.float32)
    scale = head_size ** (-0.5)

    def one_block(carry, block):
        top_old, sums, accum = carry
        block_keys, block_values, block_bias = block
        scores = (
            jnp.einsum("qhd,khd->hqk", query, block_keys, preferred_element_type=jnp.float32)
            * scale
            + block_bias[None, None, :]
        )
        top_new = jnp.maximum(top_old, jnp.max(scores, axis=-1))
        expo = jnp.exp(scores - top_new[..., None])
        factor = jnp.exp(top_old - top_new)
        sums = sums * factor + jnp.sum(expo, axis=-1)
        accum = accum * factor[..., None] + jnp.einsum(
            "hqk,khd->hqd",
            expo.astype(jnp.bfloat16),
            block_values,
            preferred_element_type=jnp.float32,
        )
        return ((top_new, sums, accum), None)

    start_state = (
        jnp.full((heads_here, tokens), -1e30, jnp.float32),
        jnp.zeros((heads_here, tokens), jnp.float32),
        jnp.zeros((heads_here, tokens, head_size), jnp.float32),
    )
    size = KEY_BLOCK if count % KEY_BLOCK == 0 else tokens
    blocks = count // size
    stacked = (
        piece_keys.reshape(blocks, size, heads_here, head_size),
        piece_values.reshape(blocks, size, heads_here, head_size),
        bias.reshape(blocks, size),
    )
    carry, unused = lax.scan(one_block, start_state, stacked)
    top_final, sums, accum = carry
    attn = (
        (accum / sums[..., None])
        .transpose(1, 0, 2)
        .reshape(tokens, local_cols)
        .astype(jnp.bfloat16)
    )
    cols_w = lax.all_to_all(out_weight, "head", 1, 0, tiled=True)
    attn_all = lax.all_gather(attn, "head", axis=1, tiled=True)
    mixed = jnp.dot(attn_all, cols_w, preferred_element_type=jnp.float32)
    mine = lax.dynamic_slice_in_dim(wide, member * local_cols, local_cols, 1)
    level_out = (mine + mixed).astype(jnp.bfloat16)
    return (refined, level_out)


def solution(mesh):
    in_specs = (
        P("space", None, None, "head"),
        P("space", None, None),
        P(),
        P(),
        P(),
        P(),
        P(None, None, "head"),
        P("head", None),
    )
    out_specs = (P("space", None, None, "head"), P("space", "head"))
    return jax.shard_map(body, mesh=mesh, in_specs=in_specs, out_specs=out_specs, check_vma=False)
```

profile of v0, /device:TPU:1, one launch (start us, length us, event | category | flops | bytes accessed | tf_op | source)
XLA Modules:
  0.0 342.8 jit_solution(4440227885603397588)
XLA Ops:
  7.2 1.0 fusion.60
  8.2 2.7 copy.59
  11.1 4.5 %collective-permute-start = (bf16[1,16,16,32]{2,1,0,3:T(8,128)(2,1)S(1)}, bf16[1,16,16,32]{2,1,0,3:T(8,128)(2,1)S(1)}, u32[]{:S(2)}, u32[]{:S(2)}) collective-permute-start(bf16[1,16,16,32]{2,1,0,3:T(8,128)(2,1)S(1)} %get-tuple-element.126), channel_id=1, source_target_pairs={{0,4},{4,8},{8,12},{12,16},{16,20},{20,24},{24,28},{28,32},{32,36}... | collective-permute-start | bytes 49160 | tf_op jit(solution)/shard_map/ppermute | solution.py:17
  15.6 1.9 collective-permute-start.1
  17.6 4.3 %collective-permute-done.1 = bf16[1,16,16,32]{2,1,0,3:T(8,128)(2,1)S(1)} collective-permute-done((bf16[1,16,16,32]{2,1,0,3:T(8,128)(2,1)S(1)}, bf16[1,16,16,32]{2,1,0,3:T(8,128)(2,1)S(1)}, u32[]{:S(2)}, u32[]{:S(2)}) %collective-permute-start.1) | collective-permute-done | bytes 16416 | tf_op jit(solution)/shard_map/ppermute | solution.py:19
  22.1 44.5 %all_gather.9 = bf16[10,16,16,128]{2,1,0,3:T(8,128)(2,1)} all-gather(bf16[10,16,16,32]{2,1,0,3:T(8,128)(2,1)S(1)} %pad_maximum_fusion), channel_id=1, replica_groups=mesh['space'=64,'head'=4] {'head'}, dimensions={3}, use_global_device_ids=true | all-gather | bytes 819200 | tf_op jit(solution)/shard_map/all_gather | solution.py:55
  66.6 5.2 %copy.60 = bf16[10,16,16,128]{3,1,2,0:T(8,128)(2,1)S(1)} copy(bf16[10,16,16,128]{2,1,0,3:T(8,128)(2,1)} %all_gather.9) | data formatting | bytes 1310720 | tf_op jit(solution)/shard_map/all_gather | solution.py:55
  72.5 0.5 copy-done.5
  73.0 6.2 %fusion.35 = f32[8,16,8,3,128]{4,2,3,1,0:T(8,128)S(1)} fusion(bf16[3,3,3,128,128]{4,3,2,1,0:T(8,128)(2,1)S(1)} %bitcast.110, bf16[10,16,1,7,2,128]{5,3,4,1,0,2:T(8,128)(2,1)S(1)} %slice.51, bf16[10,16,1,8,3,128]{5,3,4,1,0,2:T(8,128)(2,1)S(1)} %copy.63, pred[8,3]{0,1:T(4,128)(4,1)S(1)} %copy-done.7), kind=kOutput, calls=%fused_computation.40 | convolution fusion | flops 2609971200 | bytes 4014104 | tf_op jit(solution)/shard_map/conv_general_dilated | solution.py:28
  79.8 4.7 %collective-permute-start.2 = (bf16[1,16,16,128]{3,1,2,0:T(8,128)(2,1)S(1)}, bf16[1,16,16,128]{3,1,2,0:T(8,128)(2,1)S(1)}, u32[]{:S(2)}, u32[]{:S(2)}) collective-permute-start(bf16[1,16,16,128]{3,1,2,0:T(8,128)(2,1)S(1)} %get-tuple-element.128), channel_id=1, source_target_pairs={{0,4},{4,8},{8,12},{12,16},{16,20},{20,24},{24,28},{28,32},{32,36}... | collective-permute-start | bytes 196616 | tf_op jit(solution)/shard_map/ppermute | solution.py:17
  84.6 2.1 collective-permute-start.3
  86.9 1.2 copy.69
  88.0 0.6 reduce_max.18
  88.8 1.4 collective-permute-done.3
  90.9 0.5 copy-done.6
  91.4 6.2 %fusion.32 = f32[8,16,8,3,128]{4,2,3,1,0:T(8,128)S(1)} fusion(bf16[3,3,3,128,128]{4,3,2,1,0:T(8,128)(2,1)S(1)} %bitcast.111, bf16[10,16,1,7,2,128]{5,3,4,1,0,2:T(8,128)(2,1)S(1)} %slice.55, bf16[10,16,1,8,3,128]{5,3,4,1,0,2:T(8,128)(2,1)S(1)} %copy.66, pred[8,3]{0,1:T(4,128)(4,1)S(1)} %copy-done.7), kind=kOutput, calls=%fused_computation.39 | convolution fusion | flops 2609971200 | bytes 4014104 | tf_op jit(solution)/shard_map/conv_general_dilated | solution.py:28
  98.7 0.5 multiply_reduce_fusion
  99.8 0.8 copy.74
  100.5 0.8 copy.79
  101.3 3.5 %all-to-all-start = ((bf16[128,4,128]{0,2,1:T(8,128)(2,1)}), bf16[128,4,128]{0,2,1:T(8,128)(2,1)S(1)}, u32[]{:S(2)}, u32[]{:S(2)}) async-start(bf16[128,4,128]{0,2,1:T(8,128)(2,1)} %bitcast.24), calls=%async_computation | async-start | bytes 262144 | tf_op jit(solution)/shard_map/all_to_all | solution.py:142
  105.1 0.9 copy.81
  106.0 3.6 %all-to-all-done = bf16[128,4,128]{0,2,1:T(8,128)(2,1)S(1)} async-done(((bf16[128,4,128]{0,2,1:T(8,128)(2,1)}), bf16[128,4,128]{0,2,1:T(8,128)(2,1)S(1)}, u32[]{:S(2)}, u32[]{:S(2)}) %all-to-all-start) | async-done | bytes 131104 | tf_op jit(solution)/shard_map/all_to_all | solution.py:142
  109.7 79.9 %all-gather.3.cloned.1.call-done = bf16[16896,256]{1,0:T(8,128)(2,1)} async-done(((bf16[264,256]{1,0:T(8,128)(2,1)}), bf16[16896,256]{1,0:T(8,128)(2,1)}) %all-gather.3.cloned.1.call-update) | async-done | bytes 8650768 | tf_op jit(solution)/shard_map/all_gather | solution.py:93
  189.7 1.1 fusion.49
  190.8 6.0 %fusion.56 = (bf16[64,256,128]{2,1,0:T(8,128)(2,1)}, bf16[64,256,128]{2,1,0:T(8,128)(2,1)}) fusion(bf16[64,264,256]{2,1,0:T(8,128)(2,1)} %bitcast.93), kind=kLoop, calls=%fused_computation.77 | loop fusion | bytes 16777216 | tf_op jit(solution)/shard_map/slice | solution.py:97
  196.8 14.7 %reshape.108 = bf16[16,1024,2,64]{3,2,1,0:T(2,128)(2,1)} reshape(bf16[64,256,128]{2,1,0:T(8,128)(2,1)} %get-tuple-element.124) | data formatting | bytes 8388608 | tf_op jit(solution)/shard_map/reshape;reshape | solution.py:131
  211.5 20.1 %copy.78 = bf16[16,1024,2,64]{1,3,2,0:T(8,128)(2,1)} copy(bf16[16,1024,2,64]{3,2,1,0:T(2,128)(2,1)} %reshape.108) | data formatting | bytes 8388608
  231.6 14.7 %reshape.107 = bf16[16,1024,2,64]{3,2,1,0:T(2,128)(2,1)} reshape(bf16[64,256,128]{2,1,0:T(8,128)(2,1)} %get-tuple-element.125) | data formatting | bytes 8388608 | tf_op jit(solution)/shard_map/reshape;reshape | solution.py:130
  246.3 20.1 %copy.77 = bf16[16,1024,2,64]{1,3,2,0:T(8,128)(2,1)} copy(bf16[16,1024,2,64]{3,2,1,0:T(2,128)(2,1)} %reshape.107) | data formatting | bytes 8388608
  266.4 58.0 %while.15 = (s32[]{:T(128)}, f32[2,256]{1,0:T(2,128)S(1)}, f32[2,256]{1,0:T(2,128)S(1)}, f32[2,256,64]{1,2,0:T(8,128)S(1)}, bf16[16,1024,2,64]{1,3,2,0:T(8,128)(...) while((s32[]{:T(128)}, f32[2,256]{1,0:T(2,128)S(1)}, ...), condition=%wide.region_5.6_spmd.clone, body=%wide.region_2.5_spmd.clone.sunk | while | flops 140085760 | bytes 7196805 | solution.py:134
  266.4 1.5 bitcast_reduce_fusion.2
  268.4 1.6 convolution_add_fusion.3
  270.1 1.5 bitcast_reduce_fusion.2
  272.1 1.6 convolution_add_fusion.3
  273.7 1.5 bitcast_reduce_fusion.2
  275.7 1.6 convolution_add_fusion.3
  277.3 1.5 bitcast_reduce_fusion.2
  279.3 1.6 convolution_add_fusion.3
  280.9 1.5 bitcast_reduce_fusion.2
  283.0 1.6 convolution_add_fusion.3
  284.6 1.5 bitcast_reduce_fusion.2
  286.6 1.6 convolution_add_fusion.3
  288.2 1.5 bitcast_reduce_fusion.2
  290.2 1.6 convolution_add_fusion.3
  291.8 1.5 bitcast_reduce_fusion.2
  293.8 1.6 convolution_add_fusion.3
  295.5 1.5 bitcast_reduce_fusion.2
  297.5 1.6 convolution_add_fusion.3
  299.1 1.5 bitcast_reduce_fusion.2
  301.1 1.6 convolution_add_fusion.3
  302.7 1.5 bitcast_reduce_fusion.2
  304.7 1.6 convolution_add_fusion.3
  306.4 1.5 bitcast_reduce_fusion.2
  308.4 1.6 convolution_add_fusion.3
  310.0 1.5 bitcast_reduce_fusion.2
  312.0 1.6 convolution_add_fusion.3
  313.6 1.5 bitcast_reduce_fusion.2
  315.6 1.6 convolution_add_fusion.3
  317.2 1.5 bitcast_reduce_fusion.2
  319.2 1.6 convolution_add_fusion.3
  320.9 1.5 bitcast_reduce_fusion.2
  322.9 1.6 convolution_add_fusion.3
  324.5 10.5 %all_gather.11 = bf16[256,512]{0,1:T(8,128)(2,1)S(1)} all-gather(bf16[256,128]{0,1:T(8,128)(2,1)S(1)} %bitcast.109), channel_id=1, replica_groups=mesh['space'=64,'head'=4] {'head'}, dimensions={1}, use_global_device_ids=true | all-gather | bytes 327680 | tf_op jit(solution)/shard_map/all_gather | solution.py:143
  335.0 0.9 fusion.39
  (130 shorter events, 13.2 us)
Async XLA Ops:
  7.2 91.5 %copy-start = (bf16[8,128,512]{2,1,0:T(8,128)(2,1)S(1)}, bf16[8,128,512]{2,1,0:T(8,128)(2,1)}, u32[]{:S(2)}) copy-start(bf16[8,128,512]{2,1,0:T(8,128)(2,1)} %param.14) | copy-start | bytes 3145732
  7.2 182.5 %all-gather.3.cloned.1.call-start = ((), (), s32[]{:S(2)}) async-start(), calls=%async_computation.1 | async-start | bytes 8785920 | tf_op jit(solution)/shard_map/all_gather | solution.py:93
  11.1 6.5 %collective-permute-start = (bf16[1,16,16,32]{2,1,0,3:T(8,128)(2,1)S(1)}, bf16[1,16,16,32]{2,1,0,3:T(8,128)(2,1)S(1)}, u32[]{:S(2)}, u32[]{:S(2)}) collective-permute-start(bf16[1,16,16,32]{2,1,0,3:T(8,128)(2,1)S(1)} %get-tuple-element.126), channel_id=1, source_target_pairs={{0,4},{4,8},{8,12},{12,16},{16,20},{20,24},{24,28},{28,32},{32,36}... | collective-permute-start | bytes 49160 | tf_op jit(solution)/shard_map/ppermute | solution.py:17
  15.6 6.3 %collective-permute-start.1 = (bf16[1,16,16,32]{2,1,0,3:T(8,128)(2,1)S(1)}, bf16[1,16,16,32]{2,1,0,3:T(8,128)(2,1)S(1)}, u32[]{:S(2)}, u32[]{:S(2)}) collective-permute-start(bf16[1,16,16,32]{2,1,0,3:T(8,128)(2,1)S(1)} %get-tuple-element.127), channel_id=1, source_target_pairs={{4,0},{8,4},{12,8},{16,12},{20,16},{24,20},{28,24},{32,28},{36,32}... | collective-permute-start | bytes 49160 | tf_op jit(solution)/shard_map/ppermute | solution.py:19
  71.8 1.2 copy-start.5
  71.8 1.2 copy-start.7
  79.2 7.5 %copy-start.2 = (s32[8,16,16]{2,1,0:T(8,128)S(1)}, s32[8,16,16]{2,1,0:T(8,128)}, u32[]{:S(2)}) copy-start(s32[8,16,16]{2,1,0:T(8,128)} %param.11) | copy-start | bytes 24580
  79.8 9.0 %collective-permute-start.2 = (bf16[1,16,16,128]{3,1,2,0:T(8,128)(2,1)S(1)}, bf16[1,16,16,128]{3,1,2,0:T(8,128)(2,1)S(1)}, u32[]{:S(2)}, u32[]{:S(2)}) collective-permute-start(bf16[1,16,16,128]{3,1,2,0:T(8,128)(2,1)S(1)} %get-tuple-element.128), channel_id=1, source_target_pairs={{0,4},{4,8},{8,12},{12,16},{16,20},{20,24},{24,28},{28,32},{32,36}... | collective-permute-start | bytes 196616 | tf_op jit(solution)/shard_map/ppermute | solution.py:17
  84.6 5.6 %collective-permute-start.3 = (bf16[1,16,16,128]{3,1,2,0:T(8,128)(2,1)S(1)}, bf16[1,16,16,128]{3,1,2,0:T(8,128)(2,1)S(1)}, u32[]{:S(2)}, u32[]{:S(2)}) collective-permute-start(bf16[1,16,16,128]{3,1,2,0:T(8,128)(2,1)S(1)} %get-tuple-element.129), channel_id=1, source_target_pairs={{4,0},{8,4},{12,8},{16,12},{20,16},{24,20},{28,24},{32,28},{36,32}... | collective-permute-start | bytes 196616 | tf_op jit(solution)/shard_map/ppermute | solution.py:19
  90.2 1.2 copy-start.6
  98.3 0.9 copy-start.4
  98.6 1.9 copy-start.3
  101.3 8.3 %all-to-all-start = ((bf16[128,4,128]{0,2,1:T(8,128)(2,1)}), bf16[128,4,128]{0,2,1:T(8,128)(2,1)S(1)}, u32[]{:S(2)}, u32[]{:S(2)}) async-start(bf16[128,4,128]{0,2,1:T(8,128)(2,1)} %bitcast.24), calls=%async_computation | async-start | bytes 262144 | tf_op jit(solution)/shard_map/all_to_all | solution.py:142
  324.5 11.4 %copy-start.1 = (bf16[8,128,512]{2,1,0:T(8,128)(2,1)S(1)}, bf16[8,128,512]{2,1,0:T(8,128)(2,1)}, u32[]{:S(2)}) copy-start(bf16[8,128,512]{2,1,0:T(8,128)(2,1)} %param.14) | copy-start | bytes 3145732
Sparse Core Ops, SparseCore 0:
  100.7 88.9 all-gather.2
where the time goes:
time: 347 us; the launch traced here: 343 us
  local copies, waits for them, and re-layouts  91.5 us (26%)
  waiting for transfers between devices  89.1 us (26%)
  matrix products  62.8 us (18%)
  blocking collectives  54.9 us (16%)
  starting transfers between devices  16.8 us (5%)
  between operations  14.5 us (4%)
  other arithmetic  12.2 us (4%)
    all_gather x1, waiting for transfers between devices, body(): gathered = lax.all_gather(piece[None], 'space', axis=0, tiled=True)  79.9 us
    unnamed x22, local copies, waits for them, and re-layouts  46.9 us
    all_gather x1, blocking collectives, body(): lax.all_gather(with_halo(masked, 'space', 1), 'head', axis=3, tiled=True)  44.5 us
    dot_general x16, matrix products, one_block(): jnp.einsum('hqk,khd->hqd', expo.astype(jnp.bfloat16), block_values, prefe...  25.1 us
    dot_general x16, matrix products, one_block(): jnp.einsum('qhd,khd->hqk', query, block_keys, preferred_element_type=jnp....  23.6 us
    another operation x1, local copies, waits for them, and re-layouts, body(): piece_values.reshape(blocks, size, heads_here, head_size)  14.7 us
    another operation x1, local copies, waits for them, and re-layouts, body(): piece_keys.reshape(blocks, size, heads_here, head_size)  14.7 us
    conv_general_dilated x2, matrix products, convolve(): lax.conv_general_dilated(rimmed[None], kernel, window_strides=(1, 1, 1),...  12.4 us
  transfers between devices with their start and end apart: 6, of which 4 were waited for; matrix products, arithmetic and copies ran while one was open for 1% of the time, Pallas kernels for 0%

commit v1 on v0

v1 whole, which is shorter than its diff:
```python
import jax
import jax.numpy as jnp
from jax import lax
from jax.experimental import pallas as pl
from jax.experimental.pallas import tpu as pltpu
from jax.sharding import PartitionSpec as P

HEADS = 8
CHUNKS_PER_STEP = 8


def gather_head(piece_for):
    count = lax.axis_size("head")
    member = lax.axis_index("head")
    got = [piece_for(0)]
    for shift in range(1, count):
        got.append(
            lax.ppermute(
                piece_for(shift), "head", [(i, (i + shift) % count) for i in range(count)]
            )
        )
    ring = jnp.stack([got[0]] + [got[count - t] for t in range(1, count)])
    twice = jnp.concatenate([ring, ring], axis=0)
    return lax.dynamic_slice_in_dim(twice, (count - member) % count, count, axis=0)


def attend_kernel(q_ref, kv_ref, o_ref, top_ref, sum_ref, acc_ref, *, tokens, cols, hd, scale):
    step = pl.program_id(0)
    heads = cols // hd

    @pl.when(step == 0)
    def _():
        top_ref[...] = jnp.full(top_ref.shape, -1e30, jnp.float32)
        sum_ref[...] = jnp.zeros(sum_ref.shape, jnp.float32)
        acc_ref[...] = jnp.zeros(acc_ref.shape, jnp.float32)

    q = q_ref[...]
    lanes = lax.broadcasted_iota(jnp.int32, q.shape, 1) // hd
    query = jnp.concatenate([jnp.where(lanes == h, q, jnp.zeros_like(q)) for h in range(heads)], 0)
    for chunk in range(kv_ref.shape[0]):
        keys = kv_ref[chunk, :tokens, :cols]
        values = kv_ref[chunk, :tokens, cols:]
        live = kv_ref[chunk, tokens : tokens + 1, :tokens]
        bias = jnp.where(live > 0, 0.0, -1e30).astype(jnp.float32)
        scores = (
            lax.dot_general(
                query, keys, (((1,), (1,)), ((), ())), preferred_element_type=jnp.float32
            )
            * scale
            + bias
        )
        top_old = top_ref[...]
        top_new = jnp.maximum(top_old, jnp.max(scores, axis=-1, keepdims=True))
        expo = jnp.exp(scores - top_new)
        factor = jnp.exp(top_old - top_new)
        sum_ref[...] = sum_ref[...] * factor + jnp.sum(expo, axis=-1, keepdims=True)
        acc_ref[...] = acc_ref[...] * factor + jnp.dot(
            expo.astype(jnp.bfloat16), values, preferred_element_type=jnp.float32
        )
        top_ref[...] = top_new

    @pl.when(step == pl.num_programs(0) - 1)
    def _():
        ratio = acc_ref[...] / sum_ref[...]
        out = jnp.zeros(q.shape, jnp.float32)
        for h in range(heads):
            out = jnp.where(lanes == h, ratio[h * tokens : (h + 1) * tokens], out)
        o_ref[...] = out.astype(o_ref.dtype)


def attend(query, gathered, tokens, cols, hd, scale):
    parts, rows, span = gathered.shape
    qrows = query.shape[0] * (cols // hd)
    per = CHUNKS_PER_STEP if parts % CHUNKS_PER_STEP == 0 else 1
    kernel = lambda *refs: attend_kernel(*refs, tokens=tokens, cols=cols, hd=hd, scale=scale)
    return pl.pallas_call(
        kernel,
        grid=(parts // per,),
        in_specs=[
            pl.BlockSpec(query.shape, lambda i: (0, 0)),
            pl.BlockSpec((per, rows, span), lambda i: (i, 0, 0)),
        ],
        out_specs=pl.BlockSpec(query.shape, lambda i: (0, 0)),
        out_shape=jax.ShapeDtypeStruct(query.shape, jnp.bfloat16),
        scratch_shapes=[
            pltpu.VMEM((qrows, 1), jnp.float32),
            pltpu.VMEM((qrows, 1), jnp.float32),
            pltpu.VMEM((qrows, span - cols), jnp.float32),
        ],
    )(query, gathered)


def with_halo(cells, axis, width):
    count = lax.axis_size(axis)
    ends = count - 1
    head = lax.slice_in_dim(cells, 0, width, axis=0)
    tail = lax.slice_in_dim(cells, cells.shape[0] - width, cells.shape[0], axis=0)
    return jnp.concatenate(
        [
            lax.ppermute(tail, axis, [(i, i + 1) for i in range(ends)]),
            cells,
            lax.ppermute(head, axis, [(i + 1, i) for i in range(ends)]),
        ],
        axis=0,
    )


def convolve(rimmed, weight):
    chans = weight.shape[1]
    kernel = weight.reshape(3, 3, 3, chans, weight.shape[2])
    out = lax.conv_general_dilated(
        rimmed[None],
        kernel,
        window_strides=(1, 1, 1),
        padding=((0, 0), (1, 1), (1, 1)),
        dimension_numbers=("NDHWC", "DHWIO", "NDHWC"),
        preferred_element_type=jnp.float32,
    )
    return out[0]


def to_cells(field):
    nx, ny, nz, count = field.shape
    blocks = field.reshape(nx // 2, 2, ny // 2, 2, nz // 2, 2, count).transpose(0, 2, 4, 1, 3, 5, 6)
    return blocks.reshape(nx // 2 * (ny // 2) * (nz // 2), 8 * count)


def body(
    features, mask, conv1_weight, conv2_weight, down_weight, norm_gain, qkv_weight, out_weight
):
    member = lax.axis_index("head")
    nx, ny, nz, local = features.shape
    width = down_weight.shape[2]
    chans = conv1_weight.shape[1]
    tokens = nx // 2 * (ny // 2) * (nz // 2)
    occupied = mask.astype(jnp.float32)[..., None]
    masked = features * mask.astype(jnp.bfloat16)[..., None]
    halo = with_halo(masked, "space", 1)
    rimmed = gather_head(lambda shift: halo)
    rimmed = jnp.moveaxis(rimmed, 0, 3).reshape(halo.shape[:3] + (-1,))
    whole_masked = lax.slice_in_dim(rimmed, 1, nx + 1, axis=0)
    pre1 = convolve(rimmed, conv1_weight)
    hidden = (occupied * jax.nn.silu(pre1)).astype(jnp.bfloat16)
    pre2 = convolve(with_halo(hidden, "space", 1), conv2_weight)
    refined_all = (occupied * (whole_masked.astype(jnp.float32) + pre2)).astype(jnp.bfloat16)
    refined = lax.dynamic_slice_in_dim(refined_all, member * local, local, 3)
    coarse = jnp.dot(
        to_cells(refined_all),
        down_weight.reshape(8 * chans, width),
        preferred_element_type=jnp.float32,
    ).astype(jnp.bfloat16)
    wide = coarse.astype(jnp.float32)
    normed = (
        wide * lax.rsqrt(jnp.mean(wide * wide, axis=1, keepdims=True) + 1e-05) * norm_gain
    ).astype(jnp.bfloat16)
    local_cols = qkv_weight.shape[2]
    proj = jnp.dot(
        normed, qkv_weight.reshape(width, 3 * local_cols), preferred_element_type=jnp.float32
    )
    proj = proj.astype(jnp.bfloat16).reshape(tokens, 3, local_cols)
    head_size = width // HEADS
    heads_here = local_cols // head_size
    query = proj[:, 0]
    live_cell = (
        mask.reshape(nx // 2, 2, ny // 2, 2, nz // 2, 2)
        .max(axis=(1, 3, 5))
        .reshape(1, -1)
        .astype(jnp.bfloat16)
    )
    span = 2 * local_cols
    live_rows = jnp.pad(live_cell, ((0, 0), (0, span - tokens)))
    live_rows = jnp.pad(live_rows, ((0, 15), (0, 0)))
    piece = jnp.concatenate([proj[:, 1], proj[:, 2]], axis=1)
    piece = jnp.concatenate([piece, live_rows], axis=0)
    gathered = lax.all_gather(piece[None], "space", axis=0, tiled=True)
    scale = head_size ** (-0.5)
    attn = attend(query, gathered, tokens, local_cols, head_size, scale)
    cols_w = gather_head(
        lambda shift: lax.dynamic_slice_in_dim(
            out_weight, (member + shift) % lax.axis_size("head") * local_cols, local_cols, 1
        )
    ).reshape(width, local_cols)
    attn_all = jnp.moveaxis(gather_head(lambda shift: attn), 0, 1).reshape(tokens, width)
    mixed = jnp.dot(attn_all, cols_w, preferred_element_type=jnp.float32)
    mine = lax.dynamic_slice_in_dim(wide, member * local_cols, local_cols, 1)
    level_out = (mine + mixed).astype(jnp.bfloat16)
    return (refined, level_out)


def solution(mesh):
    in_specs = (
        P("space", None, None, "head"),
        P("space", None, None),
        P(),
        P(),
        P(),
        P(),
        P(None, None, "head"),
        P("head", None),
    )
    out_specs = (P("space", None, None, "head"), P("space", "head"))
    return jax.shard_map(body, mesh=mesh, in_specs=in_specs, out_specs=out_specs, check_vma=False)
```

time: 347 us -> 253 us (0.73)
  local copies, waits for them, and re-layouts: 91.5 us -> 32.9 us
  blocking collectives: 54.9 us -> 0 us
  matrix products: 62.8 us -> 20.5 us
  Pallas kernels: 0 us -> 33.2 us
  waiting for transfers between devices: 89.1 us -> 117 us
  starting transfers between devices: 16.8 us -> 21.6 us
  other arithmetic: 12.2 us -> 8.46 us
    all_gather x2 -> x0, blocking collectives: 54.9 us -> none  [the longest x1 44.5 us: body(): lax.all_gather(with_halo(masked, 'space', 1), 'head', axis=3, tiled=True)]
    dot_general x32 -> x0, matrix products: 48.6 us -> none  [the longest x16 25.1 us: one_block(): jnp.einsum('hqk,khd->hqd', expo.astype(jnp.bfloat16), block_values, prefe...]
    ppermute x0 -> x9, waiting for transfers between devices: none -> 40.1 us  [gather_head(): lax.ppermute(piece_for(shift), 'head', [(i, (i + shift) % count) for i in...]
    pallas_call x0 -> x1, Pallas kernels: none -> 33.2 us  [attend(): pl.pallas_call(kernel, grid=(parts // per,), in_specs=[pl.BlockSpec(query...]
    unnamed x22 -> x47, local copies, waits for them, and re-layouts: 46.9 us -> 14.6 us
    another operation x2 -> x1, local copies, waits for them, and re-layouts: 29.4 us -> 0.18 us  [convolve(): rimmed[None]]
    convert_element_type x1 -> x3, local copies, waits for them, and re-layouts: 0.08 us -> 12.8 us  [body(): whole_masked.astype(jnp.float32) + pre2]
    ppermute x0 -> x9, starting transfers between devices: none -> 8.71 us  [gather_head(): lax.ppermute(piece_for(shift), 'head', [(i, (i + shift) % count) for i in...]
  transfers between devices with their start and end apart: 6 -> 14, of which waited for: 4 -> 9; matrix products, arithmetic and copies ran while one was open for 1% -> 9% of each run, Pallas kernels for 0% -> 0%
where the time goes in v1:
time: 253 us; the launch traced here: 249 us
  waiting for transfers between devices  117 us (46%)
  Pallas kernels  33.2 us (13%)
  local copies, waits for them, and re-layouts  32.9 us (13%)
  starting transfers between devices  21.6 us (9%)
  matrix products  20.5 us (8%)
  between operations  15 us (6%)
  other arithmetic  8.46 us (3%)
    all_gather x1, waiting for transfers between devices, body(): gathered = lax.all_gather(piece[None], 'space', axis=0, tiled=True)  75.9 us
    ppermute x9, waiting for transfers between devices, gather_head(): lax.ppermute(piece_for(shift), 'head', [(i, (i + shift) % count) for i in...  40.1 us
    pallas_call x1, Pallas kernels, attend(): pl.pallas_call(kernel, grid=(parts // per,), in_specs=[pl.BlockSpec(query...  33.2 us
    conv_general_dilated x2, matrix products, convolve(): lax.conv_general_dilated(rimmed[None], kernel, window_strides=(1, 1, 1),...  17.9 us
    unnamed x47, local copies, waits for them, and re-layouts  14.6 us
    convert_element_type x3, local copies, waits for them, and re-layouts, body(): whole_masked.astype(jnp.float32) + pre2  12.8 us
    ppermute x9, starting transfers between devices, gather_head(): lax.ppermute(piece_for(shift), 'head', [(i, (i + shift) % count) for i in...  8.71 us
    ppermute x2, starting transfers between devices, with_halo(): lax.ppermute(head, axis, [(i + 1, i) for i in range(ends)])  7.62 us
  transfers between devices with their start and end apart: 14, of which 9 were waited for; matrix products, arithmetic and copies ran while one was open for 9% of the time, Pallas kernels for 0%

profile of v1, /device:TPU:1, one launch (start us, length us, event | category | flops | bytes accessed | tf_op | source)
XLA Modules:
  0.0 249.0 jit_solution(6559491247317901369)
XLA Ops:
  7.2 1.0 fusion.33
  8.2 1.4 broadcast_multiply_fusion
  9.6 5.1 %collective-permute-start.1 = (bf16[1,16,16,32]{3,2,1,0:T(8,128)(2,1)S(1)}, bf16[1,16,16,32]{3,2,1,0:T(8,128)(2,1)S(1)}, u32[]{:S(2)}, u32[]{:S(2)}) collective-permute-start(bf16[1,16,16,32]{3,2,1,0:T(8,128)(2,1)S(1)} %get-tuple-element.5), channel_id=1, source_target_pairs={{4,0},{8,4},{12,8},{16,12},{20,16},{24,20},{28,24},{32,28},{36,32}... | collective-permute-start | bytes 49160 | tf_op jit(solution)/shard_map/ppermute | solution.py:102
  14.7 1.9 collective-permute-start
  16.7 1.3 collective-permute-done
  18.0 1.0 pad_maximum_fusion
  19.0 2.1 collective-permute-start.2
  21.1 1.0 reshape.68
  22.1 1.2 copy.50
  23.3 1.0 mul.77
  24.3 0.6 reduce_max.9
  24.9 0.7 convert_element_type.76
  25.7 0.3 collective-permute-start.3
  26.0 0.8 collective-permute-start.4
  27.0 22.5 %collective-permute-done.2 = bf16[10,16,16,32]{3,2,1,0:T(8,128)(2,1)S(1)} collective-permute-done((bf16[10,16,16,32]{3,2,1,0:T(8,128)(2,1)}, bf16[10,16,16,32]{3,2,1,0:T(8,128)(2,1)S(1)}, u32[]{:S(2)}, u32[]{:S(2)}) %collective-permute-start.2) | collective-permute-done | bytes 163872 | tf_op jit(solution)/shard_map/ppermute | solution.py:18
  49.5 0.2 bitcast_dynamic-update-slice_fusion.4
  49.6 0.2 bitcast_dynamic-update-slice_fusion.2
  49.8 8.1 %collective-permute-done.4 = bf16[10,16,16,32]{3,2,1,0:T(8,128)(2,1)S(1)} collective-permute-done((bf16[10,16,16,32]{3,2,1,0:T(8,128)(2,1)}, bf16[10,16,16,32]{3,2,1,0:T(8,128)(2,1)S(1)}, u32[]{:S(2)}, u32[]{:S(2)}) %collective-permute-start.4) | collective-permute-done | bytes 163872 | tf_op jit(solution)/shard_map/ppermute | solution.py:18
  57.9 0.2 bitcast_dynamic-update-slice_fusion
  58.0 0.2 bitcast_dynamic-update-slice_fusion.7
  58.3 0.2 bitcast_dynamic-update-slice_fusion.5
  58.4 0.2 bitcast_dynamic-update-slice_fusion.3
  58.6 0.2 bitcast_dynamic-update-slice_fusion.1
  58.8 0.5 dynamic-slice_bitcast_fusion
  59.3 1.5 copy-done.1
  60.7 3.6 %copy.58 = bf16[10,16,16,4,32]{4,3,1,2,0:T(4,128)(2,1)} copy(bf16[10,16,16,4,32]{4,2,1,0,3:T(8,128)(2,1)S(1)} %dynamic-slice_bitcast_fusion) | data formatting | bytes 1310720
  64.4 3.6 %reshape.87 = bf16[10,16,1,16,128]{4,1,3,0,2:T(8,128)(2,1)S(1)} reshape(bf16[10,16,16,4,32]{4,3,1,2,0:T(4,128)(2,1)} %copy.58) | data formatting | bytes 1310720
  68.0 0.2 pad.5.clone
  68.2 0.3 copy.44
  68.5 0.2 slice.38
  68.7 0.5 copy-done.10
  69.2 6.2 %fusion.8 = f32[8,16,8,3,128]{4,2,3,1,0:T(8,128)S(1)} fusion(bf16[3,3,3,128,128]{4,3,2,1,0:T(8,128)(2,1)S(1)} %bitcast.93, bf16[10,16,1,7,2,128]{5,3,4,1,0,2:T(8,128)(2,1)S(1)} %slice.38, bf16[10,16,1,8,3,128]{5,3,4,1,0,2:T(8,128)(2,1)S(1)} %copy.44, pred[8,3]{0,1:T(4,128)(4,1)S(1)} %copy-done.11), kind=kOutput, calls=%fused_computation.10 | convolution fusion | flops 2609971200 | bytes 4014104 | tf_op jit(solution)/shard_map/conv_general_dilated | solution.py:111
  75.4 0.3 copy.45
  75.8 0.5 multiply_convert_fusion.1
  76.3 2.5 %collective-permute-start.6 = (bf16[1,16,16,128]{3,2,1,0:T(8,128)(2,1)S(1)}, bf16[1,16,16,128]{3,2,1,0:T(8,128)(2,1)S(1)}, u32[]{:S(2)}, u32[]{:S(2)}) collective-permute-start(bf16[1,16,16,128]{3,2,1,0:T(8,128)(2,1)S(1)} %get-tuple-element.3), channel_id=1, source_target_pairs={{4,0},{8,4},{12,8},{16,12},{20,16},{24,20},{28,24},{32,28},{36,32}... | collective-permute-start | bytes 196616 | tf_op jit(solution)/shard_map/ppermute | solution.py:102
  78.8 3.3 %collective-permute-start.5 = (bf16[1,16,16,128]{3,2,1,0:T(8,128)(2,1)S(1)}, bf16[1,16,16,128]{3,2,1,0:T(8,128)(2,1)S(1)}, u32[]{:S(2)}, u32[]{:S(2)}) collective-permute-start(bf16[1,16,16,128]{3,2,1,0:T(8,128)(2,1)S(1)} %get-tuple-element.2), channel_id=1, source_target_pairs={{0,4},{4,8},{8,12},{12,16},{16,20},{20,24},{24,28},{28,32},{32,36}... | collective-permute-start | bytes 196616 | tf_op jit(solution)/shard_map/ppermute | solution.py:100
  82.2 0.5 slice_convert_fusion
  82.7 4.8 %copy.40 = f32[8,16,16,4,32]{4,3,2,1,0:T(4,128)} copy(f32[8,16,16,4,32]{4,2,1,0,3:T(8,128)S(1)} %slice_convert_fusion) | data formatting | bytes 2097152 | tf_op jit(solution)/shard_map/convert_element_type | solution.py:145
  87.5 4.3 %reshape.77 = f32[4,2,8,2,8,2,128]{6,5,4,3,2,1,0:T(2,128)S(1)} reshape(f32[8,16,16,4,32]{4,3,2,1,0:T(4,128)} %copy.40) | data formatting | bytes 2097152 | tf_op jit(solution)/shard_map/convert_element_type | solution.py:145
  91.9 11.7 %fusion.11 = f32[1,8,16,16,128]{4,0,3,2,1:T(1,128)S(1)} fusion(bf16[3,3,3,128,128]{4,3,2,1,0:T(8,128)(2,1)} %bitcast.94, bf16[1,10,16,16,128]{4,3,2,1,0:T(8,128)(2,1)S(1)} %maximum_bitcast_fusion), kind=kOutput, calls=%fused_computation.11 | convolution fusion | flops 1664090112 | bytes 2588672 | tf_op jit(solution)/shard_map/conv_general_dilated | solution.py:111
  103.6 1.3 fusion.19
  105.0 0.5 multiply_reduce_fusion
  105.6 0.8 copy-done.3
  106.4 0.3 convolution_convert_fusion.1
  106.9 0.8 copy.54
  107.8 0.7 collective-permute-start.10
  108.5 0.3 collective-permute-start.11
  108.8 0.8 collective-permute-start.12
  109.6 1.6 collective-permute-done.10
  111.2 1.6 collective-permute-done.11
  112.8 0.9 collective-permute-done.12
  113.7 3.7 %reshape.76 = f32[8,16,16,128]{3,2,1,0:T(8,128)S(1)} reshape(f32[8,16,16,4,32]{4,3,2,1,0:T(4,128)} %copy.40) | data formatting | bytes 2097152 | tf_op jit(solution)/shard_map/convert_element_type | solution.py:145
  117.5 0.7 copy.56
  118.2 1.7 fusion.17
  119.9 75.9 %all-gather.3.cloned.1.call-done = bf16[17408,256]{1,0:T(8,128)(2,1)} async-done(((bf16[272,256]{1,0:T(8,128)(2,1)}), bf16[17408,256]{1,0:T(8,128)(2,1)}) %all-gather.3.cloned.1.call-update) | async-done | bytes 8912912 | tf_op jit(solution)/shard_map/all_gather | solution.py:175
  195.8 33.2 %shard_map.95 = bf16[256,128]{1,0:T(8,128)(2,1)} custom-call(bf16[256,128]{1,0:T(8,128)(2,1)} %bitcast.92, bf16[64,272,256]{2,1,0:T(8,128)(2,1)} %bitcast.84), custom_call_target="tpu_custom_call" | custom-call | tf_op jit(solution)/shard_map/pallas_call | solution.py:76
  229.0 2.5 collective-permute-start.7
  231.4 0.9 bitcast_dynamic-update-slice_fusion.14
  232.3 0.5 collective-permute-start.8
  232.9 0.6 collective-permute-start.9
  233.5 3.7 %collective-permute-done.8 = bf16[256,128]{1,0:T(8,128)(2,1)S(1)} collective-permute-done((bf16[256,128]{1,0:T(8,128)(2,1)}, bf16[256,128]{1,0:T(8,128)(2,1)S(1)}, u32[]{:S(2)}, u32[]{:S(2)}) %collective-permute-start.8) | collective-permute-done | bytes 65568 | tf_op jit(solution)/shard_map/ppermute | solution.py:18
  237.2 1.8 collective-permute-done.9
  239.0 0.9 bitcast_dynamic-update-slice_fusion.15
  239.9 1.8 fusion.15
  (54 shorter events, 0.9 us)
Async XLA Ops:
  7.2 97.9 %copy-start = (bf16[8,128,512]{2,1,0:T(8,128)(2,1)S(1)}, bf16[8,128,512]{2,1,0:T(8,128)(2,1)}, u32[]{:S(2)}) copy-start(bf16[8,128,512]{2,1,0:T(8,128)(2,1)} %param.12) | copy-start | bytes 3145732
  7.2 188.6 %all-gather.3.cloned.1.call-start = ((), (), s32[]{:S(2)}) async-start(), calls=%async_computation | async-start | bytes 9052160 | tf_op jit(solution)/shard_map/all_gather | solution.py:175
  8.2 67.6 %copy-start.5 = (f32[8,16,16]{2,1,0:T(8,128)}, f32[8,16,16]{2,1,0:T(8,128)S(1)}, u32[]{:S(2)}) copy-start(f32[8,16,16]{2,1,0:T(8,128)S(1)} %get-tuple-element.12) | copy-start | bytes 24580
  9.6 7.0 %collective-permute-start.1 = (bf16[1,16,16,32]{3,2,1,0:T(8,128)(2,1)S(1)}, bf16[1,16,16,32]{3,2,1,0:T(8,128)(2,1)S(1)}, u32[]{:S(2)}, u32[]{:S(2)}) collective-permute-start(bf16[1,16,16,32]{3,2,1,0:T(8,128)(2,1)S(1)} %get-tuple-element.5), channel_id=1, source_target_pairs={{4,0},{8,4},{12,8},{16,12},{20,16},{24,20},{28,24},{32,28},{36,32}... | collective-permute-start | bytes 49160 | tf_op jit(solution)/shard_map/ppermute | solution.py:102
  14.7 3.2 %collective-permute-start = (bf16[1,16,16,32]{3,2,1,0:T(8,128)(2,1)S(1)}, bf16[1,16,16,32]{3,2,1,0:T(8,128)(2,1)S(1)}, u32[]{:S(2)}, u32[]{:S(2)}) collective-permute-start(bf16[1,16,16,32]{3,2,1,0:T(8,128)(2,1)S(1)} %get-tuple-element.4), channel_id=1, source_target_pairs={{0,4},{4,8},{8,12},{12,16},{16,20},{20,24},{24,28},{28,32},{32,36}... | collective-permute-start | bytes 49160 | tf_op jit(solution)/shard_map/ppermute | solution.py:100
  19.0 30.5 %collective-permute-start.2 = (bf16[10,16,16,32]{3,2,1,0:T(8,128)(2,1)}, bf16[10,16,16,32]{3,2,1,0:T(8,128)(2,1)S(1)}, u32[]{:S(2)}, u32[]{:S(2)}) collective-permute-start(bf16[10,16,16,32]{3,2,1,0:T(8,128)(2,1)} %pad_maximum_fusion), channel_id=1, source_target_pairs={{0,3},{1,0},{2,1},{3,2},{4,7},{5,4},{6,5},{7,6},{8,11},{9,8},{10,9... | collective-permute-start | bytes 491528 | tf_op jit(solution)/shard_map/ppermute | solution.py:18
  25.7 24.0 %collective-permute-start.3 = (bf16[10,16,16,32]{3,2,1,0:T(8,128)(2,1)}, bf16[10,16,16,32]{3,2,1,0:T(8,128)(2,1)S(1)}, u32[]{:S(2)}, u32[]{:S(2)}) collective-permute-start(bf16[10,16,16,32]{3,2,1,0:T(8,128)(2,1)} %pad_maximum_fusion), channel_id=1, source_target_pairs={{0,2},{1,3},{2,0},{3,1},{4,6},{5,7},{6,4},{7,5},{8,10},{9,11},{10,... | collective-permute-start | bytes 491528 | tf_op jit(solution)/shard_map/ppermute | solution.py:18
  26.0 31.9 %collective-permute-start.4 = (bf16[10,16,16,32]{3,2,1,0:T(8,128)(2,1)}, bf16[10,16,16,32]{3,2,1,0:T(8,128)(2,1)S(1)}, u32[]{:S(2)}, u32[]{:S(2)}) collective-permute-start(bf16[10,16,16,32]{3,2,1,0:T(8,128)(2,1)} %pad_maximum_fusion), channel_id=1, source_target_pairs={{0,1},{1,2},{2,3},{3,0},{4,5},{5,6},{6,7},{7,4},{8,9},{9,10},{10,1... | collective-permute-start | bytes 491528 | tf_op jit(solution)/shard_map/ppermute | solution.py:18
  59.2 1.5 copy-start.1
  68.0 1.2 copy-start.10
  68.0 1.2 copy-start.11
  75.4 6.8 %copy-start.2 = (bf16[10,16,16,4,32]{4,2,1,0,3:T(8,128)(2,1)S(1)}, bf16[10,16,16,4,32]{4,2,1,0,3:T(8,128)(2,1)}, u32[]{:S(2)}) copy-start(bf16[10,16,16,4,32]{4,2,1,0,3:T(8,128)(2,1)} %copy-done.1) | copy-start | bytes 1966084
  76.3 15.5 %collective-permute-start.6 = (bf16[1,16,16,128]{3,2,1,0:T(8,128)(2,1)S(1)}, bf16[1,16,16,128]{3,2,1,0:T(8,128)(2,1)S(1)}, u32[]{:S(2)}, u32[]{:S(2)}) collective-permute-start(bf16[1,16,16,128]{3,2,1,0:T(8,128)(2,1)S(1)} %get-tuple-element.3), channel_id=1, source_target_pairs={{4,0},{8,4},{12,8},{16,12},{20,16},{24,20},{28,24},{32,28},{36,32}... | collective-permute-start | bytes 196616 | tf_op jit(solution)/shard_map/ppermute | solution.py:102
  78.8 12.9 %collective-permute-start.5 = (bf16[1,16,16,128]{3,2,1,0:T(8,128)(2,1)S(1)}, bf16[1,16,16,128]{3,2,1,0:T(8,128)(2,1)S(1)}, u32[]{:S(2)}, u32[]{:S(2)}) collective-permute-start(bf16[1,16,16,128]{3,2,1,0:T(8,128)(2,1)S(1)} %get-tuple-element.2), channel_id=1, source_target_pairs={{0,4},{4,8},{8,12},{12,16},{16,20},{20,24},{24,28},{28,32},{32,36}... | collective-permute-start | bytes 196616 | tf_op jit(solution)/shard_map/ppermute | solution.py:100
  91.9 11.7 %copy-start.4 = (f32[4,2,8,2,8,2]{5,4,3,2,1,0:T(8,128)S(1)}, f32[4,2,8,2,8,2]{5,4,3,2,1,0:T(8,128)}, u32[]{:S(2)}) copy-start(f32[4,2,8,2,8,2]{5,4,3,2,1,0:T(8,128)} %mul.77) | copy-start | bytes 24580
  103.6 2.8 %copy-start.9 = (f32[512]{0:T(512)S(1)}, f32[512]{0:T(512)}, u32[]{:S(2)}) copy-start(f32[512]{0:T(512)} %param.13) | copy-start | bytes 6148
  104.9 2.0 copy-start.7
  104.9 2.9 %copy-start.8 = (bf16[128,512]{1,0:T(8,128)(2,1)S(1)}, bf16[128,512]{1,0:T(8,128)(2,1)}, u32[]{:S(2)}) copy-start(bf16[128,512]{1,0:T(8,128)(2,1)} %param.15) | copy-start | bytes 393220
  105.6 0.8 copy-start.3
  107.7 10.5 %copy-start.6 = (f32[8,16,16]{2,1,0:T(8,128)S(1)}, f32[8,16,16]{2,1,0:T(8,128)}, u32[]{:S(2)}) copy-start(f32[8,16,16]{2,1,0:T(8,128)} %copy-done.5) | copy-start | bytes 24580
  107.8 3.4 %collective-permute-start.10 = (bf16[128,128]{1,0:T(8,128)(2,1)S(1)}, bf16[128,128]{1,0:T(8,128)(2,1)S(1)}, u32[]{:S(2)}, u32[]{:S(2)}) collective-permute-start(bf16[128,128]{1,0:T(8,128)(2,1)S(1)} %get-tuple-element.10), channel_id=1, source_target_pairs={{0,3},{1,0},{2,1},{3,2},{4,7},{5,4},{6,5},{7,6},{8,11},{9,8},{10,9... | collective-permute-start | bytes 98312 | tf_op jit(solution)/shard_map/ppermute | solution.py:18
  108.5 4.3 %collective-permute-start.11 = (bf16[128,128]{1,0:T(8,128)(2,1)S(1)}, bf16[128,128]{1,0:T(8,128)(2,1)S(1)}, u32[]{:S(2)}, u32[]{:S(2)}) collective-permute-start(bf16[128,128]{1,0:T(8,128)(2,1)S(1)} %get-tuple-element.11), channel_id=1, source_target_pairs={{0,2},{1,3},{2,0},{3,1},{4,6},{5,7},{6,4},{7,5},{8,10},{9,11},{10,... | collective-permute-start | bytes 98312 | tf_op jit(solution)/shard_map/ppermute | solution.py:18
  108.8 4.8 %collective-permute-start.12 = (bf16[128,128]{1,0:T(8,128)(2,1)S(1)}, bf16[128,128]{1,0:T(8,128)(2,1)S(1)}, u32[]{:S(2)}, u32[]{:S(2)}) collective-permute-start(bf16[128,128]{1,0:T(8,128)(2,1)S(1)} %get-tuple-element.9), channel_id=1, source_target_pairs={{0,1},{1,2},{2,3},{3,0},{4,5},{5,6},{6,7},{7,4},{8,9},{9,10},{10,1... | collective-permute-start | bytes 98312 | tf_op jit(solution)/shard_map/ppermute | solution.py:18
  229.0 4.5 %collective-permute-start.7 = (bf16[256,128]{1,0:T(8,128)(2,1)}, bf16[256,128]{1,0:T(8,128)(2,1)S(1)}, u32[]{:S(2)}, u32[]{:S(2)}) collective-permute-start(bf16[256,128]{1,0:T(8,128)(2,1)} %shard_map.95), channel_id=1, source_target_pairs={{0,3},{1,0},{2,1},{3,2},{4,7},{5,4},{6,5},{7,6},{8,11},{9,8},{10,9... | collective-permute-start | bytes 196616 | tf_op jit(solution)/shard_map/ppermute | solution.py:18
  232.3 4.9 %collective-permute-start.8 = (bf16[256,128]{1,0:T(8,128)(2,1)}, bf16[256,128]{1,0:T(8,128)(2,1)S(1)}, u32[]{:S(2)}, u32[]{:S(2)}) collective-permute-start(bf16[256,128]{1,0:T(8,128)(2,1)} %shard_map.95), channel_id=1, source_target_pairs={{0,2},{1,3},{2,0},{3,1},{4,6},{5,7},{6,4},{7,5},{8,10},{9,11},{10,... | collective-permute-start | bytes 196616 | tf_op jit(solution)/shard_map/ppermute | solution.py:18
  232.9 6.2 %collective-permute-start.9 = (bf16[256,128]{1,0:T(8,128)(2,1)}, bf16[256,128]{1,0:T(8,128)(2,1)S(1)}, u32[]{:S(2)}, u32[]{:S(2)}) collective-permute-start(bf16[256,128]{1,0:T(8,128)(2,1)} %shard_map.95), channel_id=1, source_target_pairs={{0,1},{1,2},{2,3},{3,0},{4,5},{5,6},{6,7},{7,4},{8,9},{9,10},{10,1... | collective-permute-start | bytes 196616 | tf_op jit(solution)/shard_map/ppermute | solution.py:18
Sparse Core Ops, SparseCore 0:
  107.9 87.8 all-gather.2

commit v2 on v1

--- a/solution.py
+++ b/solution.py
@@ -24,23 +24,28 @@
     return lax.dynamic_slice_in_dim(twice, (count - member) % count, count, axis=0)
 
 
-def attend_kernel(q_ref, kv_ref, o_ref, top_ref, sum_ref, acc_ref, *, tokens, cols, hd, scale):
+def attend_kernel(q_ref, kv_ref, top_in, sum_in, acc_in, *rest, keys_per, cols, hd, scale, final):
+    if final:
+        o_ref, top_ref, sum_ref, acc_ref = rest
+    else:
+        top_ref, sum_ref, acc_ref = rest
     step = pl.program_id(0)
     heads = cols // hd
+    qt = q_ref.shape[0]
 
     @pl.when(step == 0)
     def _():
-        top_ref[...] = jnp.full(top_ref.shape, -1e30, jnp.float32)
-        sum_ref[...] = jnp.zeros(sum_ref.shape, jnp.float32)
-        acc_ref[...] = jnp.zeros(acc_ref.shape, jnp.float32)
+        top_ref[...] = top_in[...]
+        sum_ref[...] = sum_in[...]
+        acc_ref[...] = acc_in[...]
 
     q = q_ref[...]
     lanes = lax.broadcasted_iota(jnp.int32, q.shape, 1) // hd
     query = jnp.concatenate([jnp.where(lanes == h, q, jnp.zeros_like(q)) for h in range(heads)], 0)
     for chunk in range(kv_ref.shape[0]):
-        keys = kv_ref[chunk, :tokens, :cols]
-        values = kv_ref[chunk, :tokens, cols:]
-        live = kv_ref[chunk, tokens : tokens + 1, :tokens]
+        keys = kv_ref[chunk, :keys_per, :cols]
+        values = kv_ref[chunk, :keys_per, cols:]
+        live = kv_ref[chunk, keys_per : keys_per + 1, :keys_per]
         bias = jnp.where(live > 0, 0.0, -1e30).astype(jnp.float32)
         scores = (
             lax.dot_general(
@@ -59,35 +64,44 @@
         )
         top_ref[...] = top_new
 
-    @pl.when(step == pl.num_programs(0) - 1)
-    def _():
-        ratio = acc_ref[...] / sum_ref[...]
-        out = jnp.zeros(q.shape, jnp.float32)
-        for h in range(heads):
-            out = jnp.where(lanes == h, ratio[h * tokens : (h + 1) * tokens], out)
-        o_ref[...] = out.astype(o_ref.dtype)
-
-
-def attend(query, gathered, tokens, cols, hd, scale):
+    if final:
+
+        @pl.when(step == pl.num_programs(0) - 1)
+        def _():
+            ratio = acc_ref[...] / sum_ref[...]
+            out = jnp.zeros(q.shape, jnp.float32)
+            for h in range(heads):
+                out = jnp.where(lanes == h, ratio[h * qt : (h + 1) * qt], out)
+            o_ref[...] = out.astype(o_ref.dtype)
+
+
+def attend(query, gathered, state, keys_per, cols, hd, scale, final):
     parts, rows, span = gathered.shape
     qrows = query.shape[0] * (cols // hd)
     per = CHUNKS_PER_STEP if parts % CHUNKS_PER_STEP == 0 else 1
-    kernel = lambda *refs: attend_kernel(*refs, tokens=tokens, cols=cols, hd=hd, scale=scale)
+    kernel = lambda *refs: attend_kernel(
+        *refs, keys_per=keys_per, cols=cols, hd=hd, scale=scale, final=final
+    )
+    shapes = [(qrows, 1), (qrows, 1), (qrows, span - cols)]
+    fixed = lambda i: (0, 0)
+    state_specs = [pl.BlockSpec(shape, fixed) for shape in shapes]
+    if final:
+        out_specs = pl.BlockSpec(query.shape, fixed)
+        out_shape = jax.ShapeDtypeStruct(query.shape, jnp.bfloat16)
+        scratch = [pltpu.VMEM(shape, jnp.float32) for shape in shapes]
+    else:
+        out_specs = state_specs
+        out_shape = [jax.ShapeDtypeStruct(shape, jnp.float32) for shape in shapes]
+        scratch = []
     return pl.pallas_call(
         kernel,
         grid=(parts // per,),
-        in_specs=[
-            pl.BlockSpec(query.shape, lambda i: (0, 0)),
-            pl.BlockSpec((per, rows, span), lambda i: (i, 0, 0)),
-        ],
-        out_specs=pl.BlockSpec(query.shape, lambda i: (0, 0)),
-        out_shape=jax.ShapeDtypeStruct(query.shape, jnp.bfloat16),
-        scratch_shapes=[
-            pltpu.VMEM((qrows, 1), jnp.float32),
-            pltpu.VMEM((qrows, 1), jnp.float32),
-            pltpu.VMEM((qrows, span - cols), jnp.float32),
-        ],
-    )(query, gathered)
+        in_specs=[pl.BlockSpec(query.shape, fixed), pl.BlockSpec((per, rows, span), lambda i: (i, 0, 0))]
+        + state_specs,
+        out_specs=out_specs,
+        out_shape=out_shape,
+        scratch_shapes=scratch,
+    )(query, gathered, *state)
 
 
 def with_halo(cells, axis, width):
@@ -168,13 +182,22 @@
         .astype(jnp.bfloat16)
     )
     span = 2 * local_cols
-    live_rows = jnp.pad(live_cell, ((0, 0), (0, span - tokens)))
-    live_rows = jnp.pad(live_rows, ((0, 15), (0, 0)))
-    piece = jnp.concatenate([proj[:, 1], proj[:, 2]], axis=1)
-    piece = jnp.concatenate([piece, live_rows], axis=0)
-    gathered = lax.all_gather(piece[None], "space", axis=0, tiled=True)
+    half = tokens // 2
+    kv = jnp.concatenate([proj[:, 1], proj[:, 2]], axis=1)
+    halves = []
+    for part in range(2):
+        live_rows = jnp.pad(live_cell[:, part * half : (part + 1) * half], ((0, 15), (0, span - half)))
+        piece = jnp.concatenate([kv[part * half : (part + 1) * half], live_rows], axis=0)
+        halves.append(lax.all_gather(piece[None], "space", axis=0, tiled=True))
     scale = head_size ** (-0.5)
-    attn = attend(query, gathered, tokens, local_cols, head_size, scale)
+    qrows = tokens * heads_here
+    state = (
+        jnp.full((qrows, 1), -1e30, jnp.float32),
+        jnp.zeros((qrows, 1), jnp.float32),
+        jnp.zeros((qrows, local_cols), jnp.float32),
+    )
+    state = attend(query, halves[0], state, half, local_cols, head_size, scale, False)
+    attn = attend(query, halves[1], state, half, local_cols, head_size, scale, True)
     cols_w = gather_head(
         lambda shift: lax.dynamic_slice_in_dim(
             out_weight, (member + shift) % lax.axis_size("head") * local_cols, local_cols, 1

time: 253 us -> 321 us (1.27)
  waiting for transfers between devices: 117 us -> 159 us
  Pallas kernels: 33.2 us -> 58.5 us
    all_gather x1 -> x2, waiting for transfers between devices: 75.9 us -> 118 us  [body(): halves.append(lax.all_gather(piece[None], 'space', axis=0, tiled=True))]
    pallas_call x1 -> x2, Pallas kernels: 33.2 us -> 58.5 us  [attend(): pl.pallas_call(kernel, grid=(parts // per,), in_specs=[pl.BlockSpec(query...]
    unnamed x47 -> x51, local copies, waits for them, and re-layouts: 14.6 us -> 13.6 us
  transfers between devices with their start and end apart: 14 -> 15, of which waited for: 9 -> 9; matrix products, arithmetic and copies ran while one was open for 9% -> 7% of each run, Pallas kernels for 0% -> 9%
where the time goes in v2:
time: 321 us; the launch traced here: 317 us
  waiting for transfers between devices  159 us (50%)
  Pallas kernels  58.5 us (18%)
  local copies, waits for them, and re-layouts  34.7 us (11%)
  starting transfers between devices  21.6 us (7%)
  matrix products  20.5 us (6%)
  between operations  14.9 us (5%)
  other arithmetic  8.52 us (3%)
    all_gather x2, waiting for transfers between devices, body(): halves.append(lax.all_gather(piece[None], 'space', axis=0, tiled=True))  118 us
    pallas_call x2, Pallas kernels, attend(): pl.pallas_call(kernel, grid=(parts // per,), in_specs=[pl.BlockSpec(query...  58.5 us
    ppermute x9, waiting for transfers between devices, gather_head(): lax.ppermute(piece_for(shift), 'head', [(i, (i + shift) % count) for i in...  40.8 us
    conv_general_dilated x2, matrix products, convolve(): lax.conv_general_dilated(rimmed[None], kernel, window_strides=(1, 1, 1),...  17.9 us
    unnamed x51, local copies, waits for them, and re-layouts  13.6 us
    convert_element_type x3, local copies, waits for them, and re-layouts, body(): whole_masked.astype(jnp.float32) + pre2  12.8 us
    ppermute x9, starting transfers between devices, gather_head(): lax.ppermute(piece_for(shift), 'head', [(i, (i + shift) % count) for i in...  8.35 us
    ppermute x2, starting transfers between devices, with_halo(): lax.ppermute(head, axis, [(i + 1, i) for i in range(ends)])  7.86 us
  transfers between devices with their start and end apart: 15, of which 9 were waited for; matrix products, arithmetic and copies ran while one was open for 7% of the time, Pallas kernels for 9%

profile of v2, /device:TPU:1, one launch (start us, length us, event | category | flops | bytes accessed | tf_op | source)
XLA Modules:
  0.0 317.4 jit_solution(10498941982178506241)
XLA Ops:
  7.2 1.0 fusion.40
  8.3 1.4 broadcast_multiply_fusion
  9.7 5.1 %collective-permute-start.1 = (bf16[1,16,16,32]{3,2,1,0:T(8,128)(2,1)S(1)}, bf16[1,16,16,32]{3,2,1,0:T(8,128)(2,1)S(1)}, u32[]{:S(2)}, u32[]{:S(2)}) collective-permute-start(bf16[1,16,16,32]{3,2,1,0:T(8,128)(2,1)S(1)} %get-tuple-element.11), channel_id=1, source_target_pairs={{4,0},{8,4},{12,8},{16,12},{20,16},{24,20},{28,24},{32,28},{36,32}... | collective-permute-start | bytes 49160 | tf_op jit(solution)/shard_map/ppermute | solution.py:116
  14.8 1.9 collective-permute-start
  16.7 1.0 reshape.68
  17.8 0.6 reduce_max.9
  18.5 1.0 pad_maximum_fusion
  19.5 2.1 collective-permute-start.2
  21.6 0.6 fusion.39
  22.3 0.2 copy.53
  22.4 1.0 mul.77
  23.4 0.3 collective-permute-start.3
  23.8 0.8 collective-permute-start.4
  24.8 25.7 %collective-permute-done.2 = bf16[10,16,16,32]{3,2,1,0:T(8,128)(2,1)S(1)} collective-permute-done((bf16[10,16,16,32]{3,2,1,0:T(8,128)(2,1)}, bf16[10,16,16,32]{3,2,1,0:T(8,128)(2,1)S(1)}, u32[]{:S(2)}, u32[]{:S(2)}) %collective-permute-start.2) | collective-permute-done | bytes 163872 | tf_op jit(solution)/shard_map/ppermute | solution.py:18
  50.8 5.1 %collective-permute-done.4 = bf16[10,16,16,32]{3,2,1,0:T(8,128)(2,1)S(1)} collective-permute-done((bf16[10,16,16,32]{3,2,1,0:T(8,128)(2,1)}, bf16[10,16,16,32]{3,2,1,0:T(8,128)(2,1)S(1)}, u32[]{:S(2)}, u32[]{:S(2)}) %collective-permute-start.4) | collective-permute-done | bytes 163872 | tf_op jit(solution)/shard_map/ppermute | solution.py:18
  56.1 0.2 bitcast_dynamic-update-slice_fusion.7
  56.8 0.5 dynamic-slice_bitcast_fusion
  57.3 1.5 copy-done.1
  58.8 3.6 %copy.63 = bf16[10,16,16,4,32]{4,3,1,2,0:T(4,128)(2,1)} copy(bf16[10,16,16,4,32]{4,2,1,0,3:T(8,128)(2,1)S(1)} %dynamic-slice_bitcast_fusion) | data formatting | bytes 1310720
  62.4 3.6 %reshape.88 = bf16[10,16,1,16,128]{4,1,3,0,2:T(8,128)(2,1)S(1)} reshape(bf16[10,16,16,4,32]{4,3,1,2,0:T(4,128)(2,1)} %copy.63) | data formatting | bytes 1310720
  66.0 0.2 pad.9.clone
  66.2 0.3 copy.47
  66.5 0.2 slice.54
  66.7 0.5 copy-done.12
  67.2 6.2 %fusion.8 = f32[8,16,8,3,128]{4,2,3,1,0:T(8,128)S(1)} fusion(bf16[3,3,3,128,128]{4,3,2,1,0:T(8,128)(2,1)S(1)} %bitcast.96, bf16[10,16,1,7,2,128]{5,3,4,1,0,2:T(8,128)(2,1)S(1)} %slice.54, bf16[10,16,1,8,3,128]{5,3,4,1,0,2:T(8,128)(2,1)S(1)} %copy.47, pred[8,3]{0,1:T(4,128)(4,1)S(1)} %copy-done.13), kind=kOutput, calls=%fused_computation.10 | convolution fusion | flops 2609971200 | bytes 4014104 | tf_op jit(solution)/shard_map/conv_general_dilated | solution.py:125
  73.4 0.3 copy.48
  73.8 0.5 multiply_convert_fusion.1
  74.3 2.7 collective-permute-start.6
  77.1 3.2 %collective-permute-start.5 = (bf16[1,16,16,128]{3,2,1,0:T(8,128)(2,1)S(1)}, bf16[1,16,16,128]{3,2,1,0:T(8,128)(2,1)S(1)}, u32[]{:S(2)}, u32[]{:S(2)}) collective-permute-start(bf16[1,16,16,128]{3,2,1,0:T(8,128)(2,1)S(1)} %get-tuple-element.8), channel_id=1, source_target_pairs={{0,4},{4,8},{8,12},{12,16},{16,20},{20,24},{24,28},{28,32},{32,36}... | collective-permute-start | bytes 196616 | tf_op jit(solution)/shard_map/ppermute | solution.py:114
  80.3 0.5 slice_convert_fusion
  80.8 4.8 %copy.43 = f32[8,16,16,4,32]{4,3,2,1,0:T(4,128)} copy(f32[8,16,16,4,32]{4,2,1,0,3:T(8,128)S(1)} %slice_convert_fusion) | data formatting | bytes 2097152 | tf_op jit(solution)/shard_map/convert_element_type | solution.py:159
  85.6 4.3 %reshape.77 = f32[4,2,8,2,8,2,128]{6,5,4,3,2,1,0:T(2,128)S(1)} reshape(f32[8,16,16,4,32]{4,3,2,1,0:T(4,128)} %copy.43) | data formatting | bytes 2097152 | tf_op jit(solution)/shard_map/convert_element_type | solution.py:159
  90.1 11.7 %fusion.11 = f32[1,8,16,16,128]{4,0,3,2,1:T(1,128)S(1)} fusion(bf16[3,3,3,128,128]{4,3,2,1,0:T(8,128)(2,1)} %bitcast.97, bf16[1,10,16,16,128]{4,3,2,1,0:T(8,128)(2,1)S(1)} %maximum_bitcast_fusion), kind=kOutput, calls=%fused_computation.11 | convolution fusion | flops 1664090112 | bytes 2588672 | tf_op jit(solution)/shard_map/conv_general_dilated | solution.py:125
  101.8 1.3 fusion.19
  103.2 0.5 multiply_reduce_fusion
  103.8 0.8 copy-done.3
  104.5 0.3 convolution_convert_fusion.1
  105.1 0.7 copy.59
  105.9 0.2 all-gather.5.cloned.1.call-start
  106.1 0.7 copy.57
  107.0 0.3 collective-permute-start.10
  107.3 0.3 collective-permute-start.11
  107.6 0.9 collective-permute-start.12
  108.5 1.6 collective-permute-done.10
  110.2 2.0 collective-permute-done.11
  112.2 0.7 collective-permute-done.12
  113.0 3.7 %reshape.76 = f32[8,16,16,128]{3,2,1,0:T(8,128)S(1)} reshape(f32[8,16,16,4,32]{4,3,2,1,0:T(4,128)} %copy.43) | data formatting | bytes 2097152 | tf_op jit(solution)/shard_map/convert_element_type | solution.py:159
  116.7 0.7 copy.61
  117.4 1.7 fusion.17
  119.1 69.9 %all-gather.7.cloned.1.call-done = bf16[9216,256]{1,0:T(8,128)(2,1)} async-done(((bf16[144,256]{1,0:T(8,128)(2,1)}), bf16[9216,256]{1,0:T(8,128)(2,1)}) %all-gather.7.cloned.1.call-update) | async-done | bytes 4718608 | tf_op jit(solution)/shard_map/all_gather | solution.py:191
  189.0 0.7 broadcast_in_dim.25.refs_2_
  189.7 0.7 broadcast_in_dim.26.refs_3_
  190.4 0.7 broadcast_in_dim.27.refs_4_
  191.1 29.2 %shard_map.95 = (f32[512,1]{1,0:T(8,128)}, f32[512,1]{1,0:T(8,128)}, f32[512,128]{1,0:T(8,128)}) custom-call(bf16[256,128]{1,0:T(8,128)(2,1)} %bitcast.94, bf16[64,144,256]{2,1,0:T(8,128)(2,1)} %bitcast.85, f32[512,1]{1,0:T(8,128)} %broadcast_in_dim.25.refs_2_, f32[512,1]{1,0:T(8,128)} %broadcast_in_dim.26.refs_3_, f32[512,128]{1,0:T(8,128)} %broadcast_in_dim.27.refs_4_), custom_call_target="tpu_custom_call" | custom-call | tf_op jit(solution)/shard_map/pallas_call | solution.py:96
  220.4 47.9 %all-gather.5.cloned.1.call-done = bf16[9216,256]{1,0:T(8,128)(2,1)} async-done(((bf16[144,256]{1,0:T(8,128)(2,1)}), bf16[9216,256]{1,0:T(8,128)(2,1)}) %all-gather.5.cloned.1.call-update) | async-done | bytes 4718608 | tf_op jit(solution)/shard_map/all_gather | solution.py:191
  268.3 29.3 %shard_map.96 = bf16[256,128]{1,0:T(8,128)(2,1)} custom-call(bf16[256,128]{1,0:T(8,128)(2,1)} %bitcast.95, bf16[64,144,256]{2,1,0:T(8,128)(2,1)} %bitcast.86, f32[512,1]{1,0:T(8,128)} %get-tuple-element.5.refs_2_, f32[512,1]{1,0:T(8,128)} %get-tuple-element.6.refs_3_, f32[512,128]{1,0:T(8,128)} %get-tuple-element.7.refs_4_), custom_call_target="tpu_custom_call" | custom-call | tf_op jit(solution)/shard_map/pallas_call | solution.py:96
  297.6 2.5 collective-permute-start.7
  300.1 0.9 bitcast_dynamic-update-slice_fusion.14
  301.0 0.5 collective-permute-start.8
  301.4 0.5 collective-permute-start.9
  301.9 3.9 %collective-permute-done.8 = bf16[256,128]{1,0:T(8,128)(2,1)S(1)} collective-permute-done((bf16[256,128]{1,0:T(8,128)(2,1)}, bf16[256,128]{1,0:T(8,128)(2,1)S(1)}, u32[]{:S(2)}, u32[]{:S(2)}) %collective-permute-start.8) | collective-permute-done | bytes 65568 | tf_op jit(solution)/shard_map/ppermute | solution.py:18
  305.9 1.8 collective-permute-done.9
  307.7 0.9 bitcast_dynamic-update-slice_fusion.15
  308.6 1.8 fusion.15
  (69 shorter events, 2.0 us)
Async XLA Ops:
  7.2 96.1 %copy-start = (bf16[8,128,512]{2,1,0:T(8,128)(2,1)S(1)}, bf16[8,128,512]{2,1,0:T(8,128)(2,1)}, u32[]{:S(2)}) copy-start(bf16[8,128,512]{2,1,0:T(8,128)(2,1)} %param.12) | copy-start | bytes 3145732
  7.2 15.1 %copy-start.7 = (bf16[512,3,128]{2,0,1:T(8,128)(2,1)S(1)}, bf16[512,3,128]{2,0,1:T(8,128)(2,1)}, u32[]{:S(2)}) copy-start(bf16[512,3,128]{2,0,1:T(8,128)(2,1)} %param.14) | copy-start | bytes 1179652
  7.2 181.8 %all-gather.7.cloned.1.call-start = ((), (), s32[]{:S(2)}) async-start(), calls=%async_computation.1 | async-start | bytes 4792320 | tf_op jit(solution)/shard_map/all_gather | solution.py:191
  8.2 65.5 %copy-start.5 = (f32[8,16,16]{2,1,0:T(8,128)}, f32[8,16,16]{2,1,0:T(8,128)S(1)}, u32[]{:S(2)}) copy-start(f32[8,16,16]{2,1,0:T(8,128)S(1)} %get-tuple-element.20) | copy-start | bytes 24580
  9.7 8.8 %collective-permute-start.1 = (bf16[1,16,16,32]{3,2,1,0:T(8,128)(2,1)S(1)}, bf16[1,16,16,32]{3,2,1,0:T(8,128)(2,1)S(1)}, u32[]{:S(2)}, u32[]{:S(2)}) collective-permute-start(bf16[1,16,16,32]{3,2,1,0:T(8,128)(2,1)S(1)} %get-tuple-element.11), channel_id=1, source_target_pairs={{4,0},{8,4},{12,8},{16,12},{20,16},{24,20},{28,24},{32,28},{36,32}... | collective-permute-start | bytes 49160 | tf_op jit(solution)/shard_map/ppermute | solution.py:116
  14.8 3.7 %collective-permute-start = (bf16[1,16,16,32]{3,2,1,0:T(8,128)(2,1)S(1)}, bf16[1,16,16,32]{3,2,1,0:T(8,128)(2,1)S(1)}, u32[]{:S(2)}, u32[]{:S(2)}) collective-permute-start(bf16[1,16,16,32]{3,2,1,0:T(8,128)(2,1)S(1)} %get-tuple-element.10), channel_id=1, source_target_pairs={{0,4},{4,8},{8,12},{12,16},{16,20},{20,24},{24,28},{28,32},{32,36}... | collective-permute-start | bytes 49160 | tf_op jit(solution)/shard_map/ppermute | solution.py:114
  19.5 30.9 %collective-permute-start.2 = (bf16[10,16,16,32]{3,2,1,0:T(8,128)(2,1)}, bf16[10,16,16,32]{3,2,1,0:T(8,128)(2,1)S(1)}, u32[]{:S(2)}, u32[]{:S(2)}) collective-permute-start(bf16[10,16,16,32]{3,2,1,0:T(8,128)(2,1)} %pad_maximum_fusion), channel_id=1, source_target_pairs={{0,3},{1,0},{2,1},{3,2},{4,7},{5,4},{6,5},{7,6},{8,11},{9,8},{10,9... | collective-permute-start | bytes 491528 | tf_op jit(solution)/shard_map/ppermute | solution.py:18
  23.4 27.2 %collective-permute-start.3 = (bf16[10,16,16,32]{3,2,1,0:T(8,128)(2,1)}, bf16[10,16,16,32]{3,2,1,0:T(8,128)(2,1)S(1)}, u32[]{:S(2)}, u32[]{:S(2)}) collective-permute-start(bf16[10,16,16,32]{3,2,1,0:T(8,128)(2,1)} %pad_maximum_fusion), channel_id=1, source_target_pairs={{0,2},{1,3},{2,0},{3,1},{4,6},{5,7},{6,4},{7,5},{8,10},{9,11},{10,... | collective-permute-start | bytes 491528 | tf_op jit(solution)/shard_map/ppermute | solution.py:18
  23.8 32.1 %collective-permute-start.4 = (bf16[10,16,16,32]{3,2,1,0:T(8,128)(2,1)}, bf16[10,16,16,32]{3,2,1,0:T(8,128)(2,1)S(1)}, u32[]{:S(2)}, u32[]{:S(2)}) collective-permute-start(bf16[10,16,16,32]{3,2,1,0:T(8,128)(2,1)} %pad_maximum_fusion), channel_id=1, source_target_pairs={{0,1},{1,2},{2,3},{3,0},{4,5},{5,6},{6,7},{7,4},{8,9},{9,10},{10,1... | collective-permute-start | bytes 491528 | tf_op jit(solution)/shard_map/ppermute | solution.py:18
  57.3 1.5 copy-start.1
  66.0 1.2 copy-start.12
  66.0 1.2 copy-start.13
  73.4 6.9 %copy-start.2 = (bf16[10,16,16,4,32]{4,2,1,0,3:T(8,128)(2,1)S(1)}, bf16[10,16,16,4,32]{4,2,1,0,3:T(8,128)(2,1)}, u32[]{:S(2)}) copy-start(bf16[10,16,16,4,32]{4,2,1,0,3:T(8,128)(2,1)} %copy-done.1) | copy-start | bytes 1966084
  74.3 15.6 %collective-permute-start.6 = (bf16[1,16,16,128]{3,2,1,0:T(8,128)(2,1)S(1)}, bf16[1,16,16,128]{3,2,1,0:T(8,128)(2,1)S(1)}, u32[]{:S(2)}, u32[]{:S(2)}) collective-permute-start(bf16[1,16,16,128]{3,2,1,0:T(8,128)(2,1)S(1)} %get-tuple-element.9), channel_id=1, source_target_pairs={{4,0},{8,4},{12,8},{16,12},{20,16},{24,20},{28,24},{32,28},{36,32}... | collective-permute-start | bytes 196616 | tf_op jit(solution)/shard_map/ppermute | solution.py:116
  77.1 12.9 %collective-permute-start.5 = (bf16[1,16,16,128]{3,2,1,0:T(8,128)(2,1)S(1)}, bf16[1,16,16,128]{3,2,1,0:T(8,128)(2,1)S(1)}, u32[]{:S(2)}, u32[]{:S(2)}) collective-permute-start(bf16[1,16,16,128]{3,2,1,0:T(8,128)(2,1)S(1)} %get-tuple-element.8), channel_id=1, source_target_pairs={{0,4},{4,8},{8,12},{12,16},{16,20},{20,24},{24,28},{28,32},{32,36}... | collective-permute-start | bytes 196616 | tf_op jit(solution)/shard_map/ppermute | solution.py:114
  90.0 11.7 %copy-start.4 = (f32[4,2,8,2,8,2]{5,4,3,2,1,0:T(8,128)S(1)}, f32[4,2,8,2,8,2]{5,4,3,2,1,0:T(8,128)}, u32[]{:S(2)}) copy-start(f32[4,2,8,2,8,2]{5,4,3,2,1,0:T(8,128)} %mul.77) | copy-start | bytes 24580
  101.7 2.8 copy-start.11
  103.1 2.0 copy-start.10
  103.1 3.0 copy-start.9
  103.1 3.9 %copy-start.8 = (bf16[128,512]{1,0:T(8,128)(2,1)S(1)}, bf16[128,512]{1,0:T(8,128)(2,1)}, u32[]{:S(2)}) copy-start(bf16[128,512]{1,0:T(8,128)(2,1)} %param.15) | copy-start | bytes 393220
  103.8 0.8 copy-start.3
  105.9 162.4 %all-gather.5.cloned.1.call-start = ((), (), s32[]{:S(2)}) async-start(), calls=%async_computation | async-start | bytes 4792320 | tf_op jit(solution)/shard_map/all_gather | solution.py:191
  106.1 11.3 %copy-start.6 = (f32[8,16,16]{2,1,0:T(8,128)S(1)}, f32[8,16,16]{2,1,0:T(8,128)}, u32[]{:S(2)}) copy-start(f32[8,16,16]{2,1,0:T(8,128)} %copy-done.5) | copy-start | bytes 24580
  107.0 3.2 %collective-permute-start.10 = (bf16[128,128]{1,0:T(8,128)(2,1)S(1)}, bf16[128,128]{1,0:T(8,128)(2,1)S(1)}, u32[]{:S(2)}, u32[]{:S(2)}) collective-permute-start(bf16[128,128]{1,0:T(8,128)(2,1)S(1)} %get-tuple-element.16), channel_id=1, source_target_pairs={{0,3},{1,0},{2,1},{3,2},{4,7},{5,4},{6,5},{7,6},{8,11},{9,8},{10,9... | collective-permute-start | bytes 98312 | tf_op jit(solution)/shard_map/ppermute | solution.py:18
  107.3 4.9 %collective-permute-start.11 = (bf16[128,128]{1,0:T(8,128)(2,1)S(1)}, bf16[128,128]{1,0:T(8,128)(2,1)S(1)}, u32[]{:S(2)}, u32[]{:S(2)}) collective-permute-start(bf16[128,128]{1,0:T(8,128)(2,1)S(1)} %get-tuple-element.17), channel_id=1, source_target_pairs={{0,2},{1,3},{2,0},{3,1},{4,6},{5,7},{6,4},{7,5},{8,10},{9,11},{10,... | collective-permute-start | bytes 98312 | tf_op jit(solution)/shard_map/ppermute | solution.py:18
  107.6 5.3 %collective-permute-start.12 = (bf16[128,128]{1,0:T(8,128)(2,1)S(1)}, bf16[128,128]{1,0:T(8,128)(2,1)S(1)}, u32[]{:S(2)}, u32[]{:S(2)}) collective-permute-start(bf16[128,128]{1,0:T(8,128)(2,1)S(1)} %get-tuple-element.15), channel_id=1, source_target_pairs={{0,1},{1,2},{2,3},{3,0},{4,5},{5,6},{6,7},{7,4},{8,9},{9,10},{10,1... | collective-permute-start | bytes 98312 | tf_op jit(solution)/shard_map/ppermute | solution.py:18
  297.6 4.4 %collective-permute-start.7 = (bf16[256,128]{1,0:T(8,128)(2,1)}, bf16[256,128]{1,0:T(8,128)(2,1)S(1)}, u32[]{:S(2)}, u32[]{:S(2)}) collective-permute-start(bf16[256,128]{1,0:T(8,128)(2,1)} %shard_map.96), channel_id=1, source_target_pairs={{0,3},{1,0},{2,1},{3,2},{4,7},{5,4},{6,5},{7,6},{8,11},{9,8},{10,9... | collective-permute-start | bytes 196616 | tf_op jit(solution)/shard_map/ppermute | solution.py:18
  301.0 4.9 %collective-permute-start.8 = (bf16[256,128]{1,0:T(8,128)(2,1)}, bf16[256,128]{1,0:T(8,128)(2,1)S(1)}, u32[]{:S(2)}, u32[]{:S(2)}) collective-permute-start(bf16[256,128]{1,0:T(8,128)(2,1)} %shard_map.96), channel_id=1, source_target_pairs={{0,2},{1,3},{2,0},{3,1},{4,6},{5,7},{6,4},{7,5},{8,10},{9,11},{10,... | collective-permute-start | bytes 196616 | tf_op jit(solution)/shard_map/ppermute | solution.py:18
  301.4 6.2 %collective-permute-start.9 = (bf16[256,128]{1,0:T(8,128)(2,1)}, bf16[256,128]{1,0:T(8,128)(2,1)S(1)}, u32[]{:S(2)}, u32[]{:S(2)}) collective-permute-start(bf16[256,128]{1,0:T(8,128)(2,1)} %shard_map.96), channel_id=1, source_target_pairs={{0,1},{1,2},{2,3},{3,0},{4,5},{5,6},{6,7},{7,4},{8,9},{9,10},{10,1... | collective-permute-start | bytes 196616 | tf_op jit(solution)/shard_map/ppermute | solution.py:18
Sparse Core Ops, SparseCore 0:
  106.0 82.9 all-gather.6
  191.7 76.5 all-gather.4

commit v3 on v1

--- a/solution.py
+++ b/solution.py
@@ -7,6 +7,7 @@
 
 HEADS = 8
 CHUNKS_PER_STEP = 8
+GROUP = 4
 
 
 def gather_head(piece_for):
@@ -37,26 +38,36 @@
     q = q_ref[...]
     lanes = lax.broadcasted_iota(jnp.int32, q.shape, 1) // hd
     query = jnp.concatenate([jnp.where(lanes == h, q, jnp.zeros_like(q)) for h in range(heads)], 0)
-    for chunk in range(kv_ref.shape[0]):
-        keys = kv_ref[chunk, :tokens, :cols]
-        values = kv_ref[chunk, :tokens, cols:]
-        live = kv_ref[chunk, tokens : tokens + 1, :tokens]
-        bias = jnp.where(live > 0, 0.0, -1e30).astype(jnp.float32)
-        scores = (
-            lax.dot_general(
-                query, keys, (((1,), (1,)), ((), ())), preferred_element_type=jnp.float32
+    group = GROUP if kv_ref.shape[0] % GROUP == 0 else 1
+    for first in range(0, kv_ref.shape[0], group):
+        scores, values = [], []
+        for chunk in range(first, first + group):
+            keys = kv_ref[chunk, :tokens, :cols]
+            values.append(kv_ref[chunk, :tokens, cols:])
+            live = kv_ref[chunk, tokens : tokens + 1, :tokens]
+            bias = jnp.where(live > 0, 0.0, -1e30).astype(jnp.float32)
+            scores.append(
+                lax.dot_general(
+                    query, keys, (((1,), (1,)), ((), ())), preferred_element_type=jnp.float32
+                )
+                * scale
+                + bias
             )
-            * scale
-            + bias
-        )
         top_old = top_ref[...]
-        top_new = jnp.maximum(top_old, jnp.max(scores, axis=-1, keepdims=True))
-        expo = jnp.exp(scores - top_new)
+        top_new = top_old
+        for block in scores:
+            top_new = jnp.maximum(top_new, jnp.max(block, axis=-1, keepdims=True))
         factor = jnp.exp(top_old - top_new)
-        sum_ref[...] = sum_ref[...] * factor + jnp.sum(expo, axis=-1, keepdims=True)
-        acc_ref[...] = acc_ref[...] * factor + jnp.dot(
-            expo.astype(jnp.bfloat16), values, preferred_element_type=jnp.float32
-        )
+        total = sum_ref[...] * factor
+        accum = acc_ref[...] * factor
+        for block, value in zip(scores, values):
+            expo = jnp.exp(block - top_new)
+            total = total + jnp.sum(expo, axis=-1, keepdims=True)
+            accum = accum + jnp.dot(
+                expo.astype(jnp.bfloat16), value, preferred_element_type=jnp.float32
+            )
+        sum_ref[...] = total
+        acc_ref[...] = accum
         top_ref[...] = top_new
 
     @pl.when(step == pl.num_programs(0) - 1)

time: 253 us -> 249 us (0.984)
  Pallas kernels: 33.2 us -> 29.2 us
    pallas_call x1, Pallas kernels: 33.2 us -> 29.2 us  [attend(): pl.pallas_call(kernel, grid=(parts // per,), in_specs=[pl.BlockSpec(query...]
where the time goes in v3:
time: 249 us; the launch traced here: 245 us
  waiting for transfers between devices  117 us (47%)
  local copies, waits for them, and re-layouts  32.9 us (13%)
  Pallas kernels  29.2 us (12%)
  starting transfers between devices  21.6 us (9%)
  matrix products  20.5 us (8%)
  between operations  15 us (6%)
  other arithmetic  8.46 us (3%)
    all_gather x1, waiting for transfers between devices, body(): gathered = lax.all_gather(piece[None], 'space', axis=0, tiled=True)  75.9 us
    ppermute x9, waiting for transfers between devices, gather_head(): lax.ppermute(piece_for(shift), 'head', [(i, (i + shift) % count) for i in...  40.1 us
    pallas_call x1, Pallas kernels, attend(): pl.pallas_call(kernel, grid=(parts // per,), in_specs=[pl.BlockSpec(query...  29.2 us
    conv_general_dilated x2, matrix products, convolve(): lax.conv_general_dilated(rimmed[None], kernel, window_strides=(1, 1, 1),...  17.9 us
    unnamed x47, local copies, waits for them, and re-layouts  14.6 us
    convert_element_type x3, local copies, waits for them, and re-layouts, body(): whole_masked.astype(jnp.float32) + pre2  12.8 us
    ppermute x9, starting transfers between devices, gather_head(): lax.ppermute(piece_for(shift), 'head', [(i, (i + shift) % count) for i in...  8.71 us
    ppermute x2, starting transfers between devices, with_halo(): lax.ppermute(head, axis, [(i + 1, i) for i in range(ends)])  7.62 us
  transfers between devices with their start and end apart: 14, of which 9 were waited for; matrix products, arithmetic and copies ran while one was open for 9% of the time, Pallas kernels for 0%

profile of v3, /device:TPU:1, one launch (start us, length us, event | category | flops | bytes accessed | tf_op | source)
XLA Modules:
  0.0 244.9 jit_solution(17383697334964557604)
XLA Ops:
  7.2 1.0 fusion.33
  8.2 1.4 broadcast_multiply_fusion
  9.6 5.1 %collective-permute-start.1 = (bf16[1,16,16,32]{3,2,1,0:T(8,128)(2,1)S(1)}, bf16[1,16,16,32]{3,2,1,0:T(8,128)(2,1)S(1)}, u32[]{:S(2)}, u32[]{:S(2)}) collective-permute-start(bf16[1,16,16,32]{3,2,1,0:T(8,128)(2,1)S(1)} %get-tuple-element.5), channel_id=1, source_target_pairs={{4,0},{8,4},{12,8},{16,12},{20,16},{24,20},{28,24},{32,28},{36,32}... | collective-permute-start | bytes 49160 | tf_op jit(solution)/shard_map/ppermute | solution.py:113
  14.7 1.9 collective-permute-start
  16.7 1.3 collective-permute-done
  18.0 1.0 pad_maximum_fusion
  19.0 2.1 collective-permute-start.2
  21.1 1.0 reshape.68
  22.1 1.2 copy.50
  23.3 1.0 mul.77
  24.3 0.6 reduce_max.9
  24.9 0.7 convert_element_type.76
  25.7 0.3 collective-permute-start.3
  26.0 0.8 collective-permute-start.4
  27.0 22.5 %collective-permute-done.2 = bf16[10,16,16,32]{3,2,1,0:T(8,128)(2,1)S(1)} collective-permute-done((bf16[10,16,16,32]{3,2,1,0:T(8,128)(2,1)}, bf16[10,16,16,32]{3,2,1,0:T(8,128)(2,1)S(1)}, u32[]{:S(2)}, u32[]{:S(2)}) %collective-permute-start.2) | collective-permute-done | bytes 163872 | tf_op jit(solution)/shard_map/ppermute | solution.py:19
  49.5 0.2 bitcast_dynamic-update-slice_fusion.4
  49.6 0.2 bitcast_dynamic-update-slice_fusion.2
  49.8 8.1 %collective-permute-done.4 = bf16[10,16,16,32]{3,2,1,0:T(8,128)(2,1)S(1)} collective-permute-done((bf16[10,16,16,32]{3,2,1,0:T(8,128)(2,1)}, bf16[10,16,16,32]{3,2,1,0:T(8,128)(2,1)S(1)}, u32[]{:S(2)}, u32[]{:S(2)}) %collective-permute-start.4) | collective-permute-done | bytes 163872 | tf_op jit(solution)/shard_map/ppermute | solution.py:19
  57.9 0.2 bitcast_dynamic-update-slice_fusion
  58.0 0.2 bitcast_dynamic-update-slice_fusion.7
  58.3 0.2 bitcast_dynamic-update-slice_fusion.5
  58.4 0.2 bitcast_dynamic-update-slice_fusion.3
  58.6 0.2 bitcast_dynamic-update-slice_fusion.1
  58.8 0.5 dynamic-slice_bitcast_fusion
  59.3 1.5 copy-done.1
  60.7 3.6 %copy.58 = bf16[10,16,16,4,32]{4,3,1,2,0:T(4,128)(2,1)} copy(bf16[10,16,16,4,32]{4,2,1,0,3:T(8,128)(2,1)S(1)} %dynamic-slice_bitcast_fusion) | data formatting | bytes 1310720
  64.4 3.6 %reshape.87 = bf16[10,16,1,16,128]{4,1,3,0,2:T(8,128)(2,1)S(1)} reshape(bf16[10,16,16,4,32]{4,3,1,2,0:T(4,128)(2,1)} %copy.58) | data formatting | bytes 1310720
  68.0 0.2 pad.5.clone
  68.2 0.3 copy.44
  68.5 0.2 slice.38
  68.7 0.5 copy-done.10
  69.2 6.2 %fusion.8 = f32[8,16,8,3,128]{4,2,3,1,0:T(8,128)S(1)} fusion(bf16[3,3,3,128,128]{4,3,2,1,0:T(8,128)(2,1)S(1)} %bitcast.93, bf16[10,16,1,7,2,128]{5,3,4,1,0,2:T(8,128)(2,1)S(1)} %slice.38, bf16[10,16,1,8,3,128]{5,3,4,1,0,2:T(8,128)(2,1)S(1)} %copy.44, pred[8,3]{0,1:T(4,128)(4,1)S(1)} %copy-done.11), kind=kOutput, calls=%fused_computation.10 | convolution fusion | flops 2609971200 | bytes 4014104 | tf_op jit(solution)/shard_map/conv_general_dilated | solution.py:122
  75.4 0.3 copy.45
  75.8 0.5 multiply_convert_fusion.1
  76.3 2.5 %collective-permute-start.6 = (bf16[1,16,16,128]{3,2,1,0:T(8,128)(2,1)S(1)}, bf16[1,16,16,128]{3,2,1,0:T(8,128)(2,1)S(1)}, u32[]{:S(2)}, u32[]{:S(2)}) collective-permute-start(bf16[1,16,16,128]{3,2,1,0:T(8,128)(2,1)S(1)} %get-tuple-element.3), channel_id=1, source_target_pairs={{4,0},{8,4},{12,8},{16,12},{20,16},{24,20},{28,24},{32,28},{36,32}... | collective-permute-start | bytes 196616 | tf_op jit(solution)/shard_map/ppermute | solution.py:113
  78.8 3.3 %collective-permute-start.5 = (bf16[1,16,16,128]{3,2,1,0:T(8,128)(2,1)S(1)}, bf16[1,16,16,128]{3,2,1,0:T(8,128)(2,1)S(1)}, u32[]{:S(2)}, u32[]{:S(2)}) collective-permute-start(bf16[1,16,16,128]{3,2,1,0:T(8,128)(2,1)S(1)} %get-tuple-element.2), channel_id=1, source_target_pairs={{0,4},{4,8},{8,12},{12,16},{16,20},{20,24},{24,28},{28,32},{32,36}... | collective-permute-start | bytes 196616 | tf_op jit(solution)/shard_map/ppermute | solution.py:111
  82.2 0.5 slice_convert_fusion
  82.7 4.8 %copy.40 = f32[8,16,16,4,32]{4,3,2,1,0:T(4,128)} copy(f32[8,16,16,4,32]{4,2,1,0,3:T(8,128)S(1)} %slice_convert_fusion) | data formatting | bytes 2097152 | tf_op jit(solution)/shard_map/convert_element_type | solution.py:156
  87.5 4.3 %reshape.77 = f32[4,2,8,2,8,2,128]{6,5,4,3,2,1,0:T(2,128)S(1)} reshape(f32[8,16,16,4,32]{4,3,2,1,0:T(4,128)} %copy.40) | data formatting | bytes 2097152 | tf_op jit(solution)/shard_map/convert_element_type | solution.py:156
  91.9 11.7 %fusion.11 = f32[1,8,16,16,128]{4,0,3,2,1:T(1,128)S(1)} fusion(bf16[3,3,3,128,128]{4,3,2,1,0:T(8,128)(2,1)} %bitcast.94, bf16[1,10,16,16,128]{4,3,2,1,0:T(8,128)(2,1)S(1)} %maximum_bitcast_fusion), kind=kOutput, calls=%fused_computation.11 | convolution fusion | flops 1664090112 | bytes 2588672 | tf_op jit(solution)/shard_map/conv_general_dilated | solution.py:122
  103.6 1.3 fusion.19
  105.0 0.5 multiply_reduce_fusion
  105.6 0.8 copy-done.3
  106.4 0.3 convolution_convert_fusion.1
  106.9 0.8 copy.54
  107.8 0.7 collective-permute-start.10
  108.5 0.3 collective-permute-start.11
  108.8 0.8 collective-permute-start.12
  109.6 1.6 collective-permute-done.10
  111.2 1.6 collective-permute-done.11
  112.8 0.9 collective-permute-done.12
  113.7 3.7 %reshape.76 = f32[8,16,16,128]{3,2,1,0:T(8,128)S(1)} reshape(f32[8,16,16,4,32]{4,3,2,1,0:T(4,128)} %copy.40) | data formatting | bytes 2097152 | tf_op jit(solution)/shard_map/convert_element_type | solution.py:156
  117.5 0.7 copy.56
  118.2 1.7 fusion.17
  119.9 75.9 %all-gather.3.cloned.1.call-done = bf16[17408,256]{1,0:T(8,128)(2,1)} async-done(((bf16[272,256]{1,0:T(8,128)(2,1)}), bf16[17408,256]{1,0:T(8,128)(2,1)}) %all-gather.3.cloned.1.call-update) | async-done | bytes 8912912 | tf_op jit(solution)/shard_map/all_gather | solution.py:186
  195.8 29.2 %shard_map.95 = bf16[256,128]{1,0:T(8,128)(2,1)} custom-call(bf16[256,128]{1,0:T(8,128)(2,1)} %bitcast.92, bf16[64,272,256]{2,1,0:T(8,128)(2,1)} %bitcast.84), custom_call_target="tpu_custom_call" | custom-call | tf_op jit(solution)/shard_map/pallas_call | solution.py:87
  225.0 2.5 %collective-permute-start.7 = (bf16[256,128]{1,0:T(8,128)(2,1)}, bf16[256,128]{1,0:T(8,128)(2,1)S(1)}, u32[]{:S(2)}, u32[]{:S(2)}) collective-permute-start(bf16[256,128]{1,0:T(8,128)(2,1)} %shard_map.95), channel_id=1, source_target_pairs={{0,3},{1,0},{2,1},{3,2},{4,7},{5,4},{6,5},{7,6},{8,11},{9,8},{10,9... | collective-permute-start | bytes 196616 | tf_op jit(solution)/shard_map/ppermute | solution.py:19
  227.4 0.9 bitcast_dynamic-update-slice_fusion.14
  228.3 0.5 collective-permute-start.8
  228.8 0.6 collective-permute-start.9
  229.5 3.7 %collective-permute-done.8 = bf16[256,128]{1,0:T(8,128)(2,1)S(1)} collective-permute-done((bf16[256,128]{1,0:T(8,128)(2,1)}, bf16[256,128]{1,0:T(8,128)(2,1)S(1)}, u32[]{:S(2)}, u32[]{:S(2)}) %collective-permute-start.8) | collective-permute-done | bytes 65568 | tf_op jit(solution)/shard_map/ppermute | solution.py:19
  233.2 1.8 collective-permute-done.9
  235.0 0.9 bitcast_dynamic-update-slice_fusion.15
  235.9 1.8 fusion.15
  (54 shorter events, 0.9 us)
Async XLA Ops:
  7.2 97.9 %copy-start = (bf16[8,128,512]{2,1,0:T(8,128)(2,1)S(1)}, bf16[8,128,512]{2,1,0:T(8,128)(2,1)}, u32[]{:S(2)}) copy-start(bf16[8,128,512]{2,1,0:T(8,128)(2,1)} %param.12) | copy-start | bytes 3145732
  7.2 188.6 %all-gather.3.cloned.1.call-start = ((), (), s32[]{:S(2)}) async-start(), calls=%async_computation | async-start | bytes 9052160 | tf_op jit(solution)/shard_map/all_gather | solution.py:186
  8.2 67.6 %copy-start.5 = (f32[8,16,16]{2,1,0:T(8,128)}, f32[8,16,16]{2,1,0:T(8,128)S(1)}, u32[]{:S(2)}) copy-start(f32[8,16,16]{2,1,0:T(8,128)S(1)} %get-tuple-element.12) | copy-start | bytes 24580
  9.6 7.0 %collective-permute-start.1 = (bf16[1,16,16,32]{3,2,1,0:T(8,128)(2,1)S(1)}, bf16[1,16,16,32]{3,2,1,0:T(8,128)(2,1)S(1)}, u32[]{:S(2)}, u32[]{:S(2)}) collective-permute-start(bf16[1,16,16,32]{3,2,1,0:T(8,128)(2,1)S(1)} %get-tuple-element.5), channel_id=1, source_target_pairs={{4,0},{8,4},{12,8},{16,12},{20,16},{24,20},{28,24},{32,28},{36,32}... | collective-permute-start | bytes 49160 | tf_op jit(solution)/shard_map/ppermute | solution.py:113
  14.7 3.2 %collective-permute-start = (bf16[1,16,16,32]{3,2,1,0:T(8,128)(2,1)S(1)}, bf16[1,16,16,32]{3,2,1,0:T(8,128)(2,1)S(1)}, u32[]{:S(2)}, u32[]{:S(2)}) collective-permute-start(bf16[1,16,16,32]{3,2,1,0:T(8,128)(2,1)S(1)} %get-tuple-element.4), channel_id=1, source_target_pairs={{0,4},{4,8},{8,12},{12,16},{16,20},{20,24},{24,28},{28,32},{32,36}... | collective-permute-start | bytes 49160 | tf_op jit(solution)/shard_map/ppermute | solution.py:111
  19.0 30.5 %collective-permute-start.2 = (bf16[10,16,16,32]{3,2,1,0:T(8,128)(2,1)}, bf16[10,16,16,32]{3,2,1,0:T(8,128)(2,1)S(1)}, u32[]{:S(2)}, u32[]{:S(2)}) collective-permute-start(bf16[10,16,16,32]{3,2,1,0:T(8,128)(2,1)} %pad_maximum_fusion), channel_id=1, source_target_pairs={{0,3},{1,0},{2,1},{3,2},{4,7},{5,4},{6,5},{7,6},{8,11},{9,8},{10,9... | collective-permute-start | bytes 491528 | tf_op jit(solution)/shard_map/ppermute | solution.py:19
  25.7 24.0 %collective-permute-start.3 = (bf16[10,16,16,32]{3,2,1,0:T(8,128)(2,1)}, bf16[10,16,16,32]{3,2,1,0:T(8,128)(2,1)S(1)}, u32[]{:S(2)}, u32[]{:S(2)}) collective-permute-start(bf16[10,16,16,32]{3,2,1,0:T(8,128)(2,1)} %pad_maximum_fusion), channel_id=1, source_target_pairs={{0,2},{1,3},{2,0},{3,1},{4,6},{5,7},{6,4},{7,5},{8,10},{9,11},{10,... | collective-permute-start | bytes 491528 | tf_op jit(solution)/shard_map/ppermute | solution.py:19
  26.0 31.9 %collective-permute-start.4 = (bf16[10,16,16,32]{3,2,1,0:T(8,128)(2,1)}, bf16[10,16,16,32]{3,2,1,0:T(8,128)(2,1)S(1)}, u32[]{:S(2)}, u32[]{:S(2)}) collective-permute-start(bf16[10,16,16,32]{3,2,1,0:T(8,128)(2,1)} %pad_maximum_fusion), channel_id=1, source_target_pairs={{0,1},{1,2},{2,3},{3,0},{4,5},{5,6},{6,7},{7,4},{8,9},{9,10},{10,1... | collective-permute-start | bytes 491528 | tf_op jit(solution)/shard_map/ppermute | solution.py:19
  59.2 1.5 copy-start.1
  68.0 1.2 copy-start.10
  68.0 1.2 copy-start.11
  75.4 6.8 %copy-start.2 = (bf16[10,16,16,4,32]{4,2,1,0,3:T(8,128)(2,1)S(1)}, bf16[10,16,16,4,32]{4,2,1,0,3:T(8,128)(2,1)}, u32[]{:S(2)}) copy-start(bf16[10,16,16,4,32]{4,2,1,0,3:T(8,128)(2,1)} %copy-done.1) | copy-start | bytes 1966084
  76.3 15.5 %collective-permute-start.6 = (bf16[1,16,16,128]{3,2,1,0:T(8,128)(2,1)S(1)}, bf16[1,16,16,128]{3,2,1,0:T(8,128)(2,1)S(1)}, u32[]{:S(2)}, u32[]{:S(2)}) collective-permute-start(bf16[1,16,16,128]{3,2,1,0:T(8,128)(2,1)S(1)} %get-tuple-element.3), channel_id=1, source_target_pairs={{4,0},{8,4},{12,8},{16,12},{20,16},{24,20},{28,24},{32,28},{36,32}... | collective-permute-start | bytes 196616 | tf_op jit(solution)/shard_map/ppermute | solution.py:113
  78.8 12.9 %collective-permute-start.5 = (bf16[1,16,16,128]{3,2,1,0:T(8,128)(2,1)S(1)}, bf16[1,16,16,128]{3,2,1,0:T(8,128)(2,1)S(1)}, u32[]{:S(2)}, u32[]{:S(2)}) collective-permute-start(bf16[1,16,16,128]{3,2,1,0:T(8,128)(2,1)S(1)} %get-tuple-element.2), channel_id=1, source_target_pairs={{0,4},{4,8},{8,12},{12,16},{16,20},{20,24},{24,28},{28,32},{32,36}... | collective-permute-start | bytes 196616 | tf_op jit(solution)/shard_map/ppermute | solution.py:111
  91.9 11.7 %copy-start.4 = (f32[4,2,8,2,8,2]{5,4,3,2,1,0:T(8,128)S(1)}, f32[4,2,8,2,8,2]{5,4,3,2,1,0:T(8,128)}, u32[]{:S(2)}) copy-start(f32[4,2,8,2,8,2]{5,4,3,2,1,0:T(8,128)} %mul.77) | copy-start | bytes 24580
  103.6 2.8 %copy-start.9 = (f32[512]{0:T(512)S(1)}, f32[512]{0:T(512)}, u32[]{:S(2)}) copy-start(f32[512]{0:T(512)} %param.13) | copy-start | bytes 6148
  104.9 2.0 copy-start.7
  104.9 2.9 %copy-start.8 = (bf16[128,512]{1,0:T(8,128)(2,1)S(1)}, bf16[128,512]{1,0:T(8,128)(2,1)}, u32[]{:S(2)}) copy-start(bf16[128,512]{1,0:T(8,128)(2,1)} %param.15) | copy-start | bytes 393220
  105.6 0.8 copy-start.3
  107.7 10.5 %copy-start.6 = (f32[8,16,16]{2,1,0:T(8,128)S(1)}, f32[8,16,16]{2,1,0:T(8,128)}, u32[]{:S(2)}) copy-start(f32[8,16,16]{2,1,0:T(8,128)} %copy-done.5) | copy-start | bytes 24580
  107.8 3.4 %collective-permute-start.10 = (bf16[128,128]{1,0:T(8,128)(2,1)S(1)}, bf16[128,128]{1,0:T(8,128)(2,1)S(1)}, u32[]{:S(2)}, u32[]{:S(2)}) collective-permute-start(bf16[128,128]{1,0:T(8,128)(2,1)S(1)} %get-tuple-element.10), channel_id=1, source_target_pairs={{0,3},{1,0},{2,1},{3,2},{4,7},{5,4},{6,5},{7,6},{8,11},{9,8},{10,9... | collective-permute-start | bytes 98312 | tf_op jit(solution)/shard_map/ppermute | solution.py:19
  108.5 4.3 %collective-permute-start.11 = (bf16[128,128]{1,0:T(8,128)(2,1)S(1)}, bf16[128,128]{1,0:T(8,128)(2,1)S(1)}, u32[]{:S(2)}, u32[]{:S(2)}) collective-permute-start(bf16[128,128]{1,0:T(8,128)(2,1)S(1)} %get-tuple-element.11), channel_id=1, source_target_pairs={{0,2},{1,3},{2,0},{3,1},{4,6},{5,7},{6,4},{7,5},{8,10},{9,11},{10,... | collective-permute-start | bytes 98312 | tf_op jit(solution)/shard_map/ppermute | solution.py:19
  108.8 4.8 %collective-permute-start.12 = (bf16[128,128]{1,0:T(8,128)(2,1)S(1)}, bf16[128,128]{1,0:T(8,128)(2,1)S(1)}, u32[]{:S(2)}, u32[]{:S(2)}) collective-permute-start(bf16[128,128]{1,0:T(8,128)(2,1)S(1)} %get-tuple-element.9), channel_id=1, source_target_pairs={{0,1},{1,2},{2,3},{3,0},{4,5},{5,6},{6,7},{7,4},{8,9},{9,10},{10,1... | collective-permute-start | bytes 98312 | tf_op jit(solution)/shard_map/ppermute | solution.py:19
  225.0 4.5 %collective-permute-start.7 = (bf16[256,128]{1,0:T(8,128)(2,1)}, bf16[256,128]{1,0:T(8,128)(2,1)S(1)}, u32[]{:S(2)}, u32[]{:S(2)}) collective-permute-start(bf16[256,128]{1,0:T(8,128)(2,1)} %shard_map.95), channel_id=1, source_target_pairs={{0,3},{1,0},{2,1},{3,2},{4,7},{5,4},{6,5},{7,6},{8,11},{9,8},{10,9... | collective-permute-start | bytes 196616 | tf_op jit(solution)/shard_map/ppermute | solution.py:19
  228.3 4.9 %collective-permute-start.8 = (bf16[256,128]{1,0:T(8,128)(2,1)}, bf16[256,128]{1,0:T(8,128)(2,1)S(1)}, u32[]{:S(2)}, u32[]{:S(2)}) collective-permute-start(bf16[256,128]{1,0:T(8,128)(2,1)} %shard_map.95), channel_id=1, source_target_pairs={{0,2},{1,3},{2,0},{3,1},{4,6},{5,7},{6,4},{7,5},{8,10},{9,11},{10,... | collective-permute-start | bytes 196616 | tf_op jit(solution)/shard_map/ppermute | solution.py:19
  228.8 6.1 %collective-permute-start.9 = (bf16[256,128]{1,0:T(8,128)(2,1)}, bf16[256,128]{1,0:T(8,128)(2,1)S(1)}, u32[]{:S(2)}, u32[]{:S(2)}) collective-permute-start(bf16[256,128]{1,0:T(8,128)(2,1)} %shard_map.95), channel_id=1, source_target_pairs={{0,1},{1,2},{2,3},{3,0},{4,5},{5,6},{6,7},{7,4},{8,9},{9,10},{10,1... | collective-permute-start | bytes 196616 | tf_op jit(solution)/shard_map/ppermute | solution.py:19
Sparse Core Ops, SparseCore 0:
  107.9 87.8 all-gather.2

commit v4 on v3

--- a/solution.py
+++ b/solution.py
@@ -6,6 +6,7 @@
 from jax.sharding import PartitionSpec as P
 
 HEADS = 8
+SPACE = ("chip", "core")
 CHUNKS_PER_STEP = 8
 GROUP = 4
 
@@ -25,7 +26,7 @@
     return lax.dynamic_slice_in_dim(twice, (count - member) % count, count, axis=0)
 
 
-def attend_kernel(q_ref, kv_ref, o_ref, top_ref, sum_ref, acc_ref, *, tokens, cols, hd, scale):
+def attend_kernel(q_ref, kv_ref, o_ref, top_ref, sum_ref, acc_ref, *, tokens, cols, hd, scale, sub):
     step = pl.program_id(0)
     heads = cols // hd
 
@@ -36,23 +37,24 @@
         acc_ref[...] = jnp.zeros(acc_ref.shape, jnp.float32)
 
     q = q_ref[...]
-    lanes = lax.broadcasted_iota(jnp.int32, q.shape, 1) // hd
-    query = jnp.concatenate([jnp.where(lanes == h, q, jnp.zeros_like(q)) for h in range(heads)], 0)
+    lanes = lax.broadcasted_iota(jnp.int32, q.shape, 1)
+    query = jnp.where(lanes < hd, q, jnp.zeros_like(q))
     group = GROUP if kv_ref.shape[0] % GROUP == 0 else 1
     for first in range(0, kv_ref.shape[0], group):
         scores, values = [], []
         for chunk in range(first, first + group):
-            keys = kv_ref[chunk, :tokens, :cols]
-            values.append(kv_ref[chunk, :tokens, cols:])
-            live = kv_ref[chunk, tokens : tokens + 1, :tokens]
-            bias = jnp.where(live > 0, 0.0, -1e30).astype(jnp.float32)
-            scores.append(
-                lax.dot_general(
-                    query, keys, (((1,), (1,)), ((), ())), preferred_element_type=jnp.float32
+            for part in range(tokens // sub):
+                keys = kv_ref[chunk, part * sub : (part + 1) * sub, :]
+                values.append(keys)
+                live = kv_ref[chunk, tokens + part : tokens + part + 1, :sub]
+                bias = jnp.where(live > 0, 0.0, -1e30).astype(jnp.float32)
+                scores.append(
+                    lax.dot_general(
+                        query, keys, (((1,), (1,)), ((), ())), preferred_element_type=jnp.float32
+                    )
+                    * scale
+                    + bias
                 )
-                * scale
-                + bias
-            )
         top_old = top_ref[...]
         top_new = top_old
         for block in scores:
@@ -73,17 +75,16 @@
     @pl.when(step == pl.num_programs(0) - 1)
     def _():
         ratio = acc_ref[...] / sum_ref[...]
-        out = jnp.zeros(q.shape, jnp.float32)
-        for h in range(heads):
-            out = jnp.where(lanes == h, ratio[h * tokens : (h + 1) * tokens], out)
-        o_ref[...] = out.astype(o_ref.dtype)
-
-
-def attend(query, gathered, tokens, cols, hd, scale):
+        o_ref[...] = ratio[:, hd:].astype(o_ref.dtype)
+
+
+def attend(query, gathered, tokens, hd, scale, sub):
     parts, rows, span = gathered.shape
-    qrows = query.shape[0] * (cols // hd)
+    qrows = query.shape[0]
     per = CHUNKS_PER_STEP if parts % CHUNKS_PER_STEP == 0 else 1
-    kernel = lambda *refs: attend_kernel(*refs, tokens=tokens, cols=cols, hd=hd, scale=scale)
+    kernel = lambda *refs: attend_kernel(
+        *refs, tokens=tokens, cols=span, hd=hd, scale=scale, sub=sub
+    )
     return pl.pallas_call(
         kernel,
         grid=(parts // per,),
@@ -91,18 +92,18 @@
             pl.BlockSpec(query.shape, lambda i: (0, 0)),
             pl.BlockSpec((per, rows, span), lambda i: (i, 0, 0)),
         ],
-        out_specs=pl.BlockSpec(query.shape, lambda i: (0, 0)),
-        out_shape=jax.ShapeDtypeStruct(query.shape, jnp.bfloat16),
+        out_specs=pl.BlockSpec((qrows, span - hd), lambda i: (0, 0)),
+        out_shape=jax.ShapeDtypeStruct((qrows, span - hd), jnp.bfloat16),
         scratch_shapes=[
             pltpu.VMEM((qrows, 1), jnp.float32),
             pltpu.VMEM((qrows, 1), jnp.float32),
-            pltpu.VMEM((qrows, span - cols), jnp.float32),
+            pltpu.VMEM((qrows, span), jnp.float32),
         ],
     )(query, gathered)
 
 
 def with_halo(cells, axis, width):
-    count = lax.axis_size(axis)
+    count = lax.axis_size(axis[0]) * lax.axis_size(axis[1])
     ends = count - 1
     head = lax.slice_in_dim(cells, 0, width, axis=0)
     tail = lax.slice_in_dim(cells, cells.shape[0] - width, cells.shape[0], axis=0)
@@ -146,13 +147,13 @@
     tokens = nx // 2 * (ny // 2) * (nz // 2)
     occupied = mask.astype(jnp.float32)[..., None]
     masked = features * mask.astype(jnp.bfloat16)[..., None]
-    halo = with_halo(masked, "space", 1)
+    halo = with_halo(masked, SPACE, 1)
     rimmed = gather_head(lambda shift: halo)
     rimmed = jnp.moveaxis(rimmed, 0, 3).reshape(halo.shape[:3] + (-1,))
     whole_masked = lax.slice_in_dim(rimmed, 1, nx + 1, axis=0)
     pre1 = convolve(rimmed, conv1_weight)
     hidden = (occupied * jax.nn.silu(pre1)).astype(jnp.bfloat16)
-    pre2 = convolve(with_halo(hidden, "space", 1), conv2_weight)
+    pre2 = convolve(with_halo(hidden, SPACE, 1), conv2_weight)
     refined_all = (occupied * (whole_masked.astype(jnp.float32) + pre2)).astype(jnp.bfloat16)
     refined = lax.dynamic_slice_in_dim(refined_all, member * local, local, 3)
     coarse = jnp.dot(
@@ -178,14 +179,27 @@
         .reshape(1, -1)
         .astype(jnp.bfloat16)
     )
-    span = 2 * local_cols
-    live_rows = jnp.pad(live_cell, ((0, 0), (0, span - tokens)))
-    live_rows = jnp.pad(live_rows, ((0, 15), (0, 0)))
-    piece = jnp.concatenate([proj[:, 1], proj[:, 2]], axis=1)
-    piece = jnp.concatenate([piece, live_rows], axis=0)
-    gathered = lax.all_gather(piece[None], "space", axis=0, tiled=True)
+    core = lax.axis_index("core")
+    swap = [(0, 1), (1, 0)]
+    qkv = proj.reshape(tokens, 3, heads_here, head_size)
+    keep = lax.dynamic_index_in_dim(qkv, core, 2, keepdims=False)
+    send = lax.dynamic_index_in_dim(qkv, 1 - core, 2, keepdims=False)
+    both = jnp.concatenate([send.reshape(tokens, 3 * head_size), live_cell.reshape(tokens, 1).astype(jnp.bfloat16)], 1)
+    got = lax.ppermute(both, "core", swap)
+    mine = jnp.concatenate([keep.reshape(tokens, 3 * head_size), live_cell.reshape(tokens, 1).astype(jnp.bfloat16)], 1)
+    chip = jnp.where(core == 0, jnp.concatenate([mine, got], 0), jnp.concatenate([got, mine], 0))
+    chip_tokens = 2 * tokens
+    sub = 2 * head_size
+    query = jnp.pad(chip[:, :head_size], ((0, 0), (0, head_size)))
+    live_rows = chip[:, 3 * head_size].reshape(chip_tokens // sub, sub)
+    live_rows = jnp.pad(live_rows, ((0, (-live_rows.shape[0]) % 16), (0, 0)))
+    piece = jnp.concatenate([chip[:, head_size : 3 * head_size], live_rows], axis=0)
+    gathered = lax.all_gather(piece[None], "chip", axis=0, tiled=True)
     scale = head_size ** (-0.5)
-    attn = attend(query, gathered, tokens, local_cols, head_size, scale)
+    half = attend(query, gathered, chip_tokens, head_size, scale, sub)
+    own = lax.dynamic_slice_in_dim(half, core * tokens, tokens, 0)
+    other = lax.ppermute(lax.dynamic_slice_in_dim(half, (1 - core) * tokens, tokens, 0), "core", swap)
+    attn = jnp.where(core == 0, jnp.concatenate([own, other], 1), jnp.concatenate([other, own], 1))
     cols_w = gather_head(
         lambda shift: lax.dynamic_slice_in_dim(
             out_weight, (member + shift) % lax.axis_size("head") * local_cols, local_cols, 1
@@ -199,9 +213,12 @@
 
 
 def solution(mesh):
+    space = mesh.shape["space"]
+    devices = mesh.devices.reshape(space // 2, 2, mesh.shape["head"])
+    split = jax.sharding.Mesh(devices, ("chip", "core", "head"))
     in_specs = (
-        P("space", None, None, "head"),
-        P("space", None, None),
+        P(SPACE, None, None, "head"),
+        P(SPACE, None, None),
         P(),
         P(),
         P(),
@@ -209,5 +226,5 @@
         P(None, None, "head"),
         P("head", None),
     )
-    out_specs = (P("space", None, None, "head"), P("space", "head"))
-    return jax.shard_map(body, mesh=mesh, in_specs=in_specs, out_specs=out_specs, check_vma=False)
+    out_specs = (P(SPACE, None, None, "head"), P(SPACE, "head"))
+    return jax.shard_map(body, mesh=split, in_specs=in_specs, out_specs=out_specs, check_vma=False)

time: 249 us -> 243 us (0.976)
  Pallas kernels: 29.2 us -> 22 us
  starting transfers between devices: 21.6 us -> 25.9 us
  local copies, waits for them, and re-layouts: 32.9 us -> 29.9 us
    pallas_call x1, Pallas kernels: 29.2 us -> 22 us  [attend(): pl.pallas_call(kernel, grid=(parts // per,), in_specs=[pl.BlockSpec(query...]
    ppermute x0 -> x2, starting transfers between devices: none -> 4.32 us  [the longest x1 4.05 us: body(): lax.ppermute(lax.dynamic_slice_in_dim(half, (1 - core) * tokens, tokens,...]
    unnamed x47 -> x48, local copies, waits for them, and re-layouts: 14.6 us -> 11.2 us
  transfers between devices with their start and end apart: 14 -> 16, of which waited for: 9 -> 11; matrix products, arithmetic and copies ran while one was open for 9% -> 8% of each run, Pallas kernels for 0% -> 0%
where the time goes in v4:
time: 243 us; the launch traced here: 240 us
  waiting for transfers between devices  116 us (48%)
  local copies, waits for them, and re-layouts  29.9 us (12%)
  starting transfers between devices  25.9 us (11%)
  Pallas kernels  22 us (9%)
  matrix products  20.5 us (8%)
  between operations  14.9 us (6%)
  other arithmetic  10.4 us (4%)
    all_gather x1, waiting for transfers between devices, body(): gathered = lax.all_gather(piece[None], 'chip', axis=0, tiled=True)  73.6 us
    ppermute x9, waiting for transfers between devices, gather_head(): lax.ppermute(piece_for(shift), 'head', [(i, (i + shift) % count) for i in...  39.9 us
    pallas_call x1, Pallas kernels, attend(): pl.pallas_call(kernel, grid=(parts // per,), in_specs=[pl.BlockSpec(query...  22 us
    conv_general_dilated x2, matrix products, convolve(): lax.conv_general_dilated(rimmed[None], kernel, window_strides=(1, 1, 1),...  17.9 us
    convert_element_type x3, local copies, waits for them, and re-layouts, body(): whole_masked.astype(jnp.float32) + pre2  12.8 us
    unnamed x48, local copies, waits for them, and re-layouts  11.2 us
    ppermute x9, starting transfers between devices, gather_head(): lax.ppermute(piece_for(shift), 'head', [(i, (i + shift) % count) for i in...  8.54 us
    ppermute x2, starting transfers between devices, with_halo(): lax.ppermute(head, axis, [(i + 1, i) for i in range(ends)])  7.82 us
  transfers between devices with their start and end apart: 16, of which 11 were waited for; matrix products, arithmetic and copies ran while one was open for 8% of the time, Pallas kernels for 0%

profile of v4, /device:TPU:1, one launch (start us, length us, event | category | flops | bytes accessed | tf_op | source)
XLA Modules:
  0.0 239.7 jit_solution(10171421153540756662)
XLA Ops:
  7.2 1.0 fusion.34
  8.3 1.4 broadcast_multiply_fusion
  9.7 5.1 %collective-permute-start.1 = (bf16[1,16,16,32]{3,2,1,0:T(8,128)(2,1)S(1)}, bf16[1,16,16,32]{3,2,1,0:T(8,128)(2,1)S(1)}, u32[]{:S(2)}, u32[]{:S(2)}) collective-permute-start(bf16[1,16,16,32]{3,2,1,0:T(8,128)(2,1)S(1)} %get-tuple-element.5), channel_id=1, source_target_pairs={{4,0},{8,4},{12,8},{16,12},{20,16},{24,20},{28,24},{32,28},{36,32}... | collective-permute-start | bytes 49160 | tf_op jit(solution)/shard_map/ppermute | solution.py:114
  14.8 1.9 collective-permute-start
  16.7 1.3 collective-permute-done
  18.0 1.0 pad_maximum_fusion
  19.0 2.1 collective-permute-start.2
  21.1 1.0 reshape.131
  22.2 0.6 reduce_max.9
  22.8 0.7 convert_element_type.79
  23.5 0.2 copy.23
  23.7 1.0 mul.83
  24.7 0.3 collective-permute-start.3
  25.1 0.8 collective-permute-start.4
  26.1 23.5 %collective-permute-done.2 = bf16[10,16,16,32]{3,2,1,0:T(8,128)(2,1)S(1)} collective-permute-done((bf16[10,16,16,32]{3,2,1,0:T(8,128)(2,1)}, bf16[10,16,16,32]{3,2,1,0:T(8,128)(2,1)S(1)}, u32[]{:S(2)}, u32[]{:S(2)}) %collective-permute-start.2) | collective-permute-done | bytes 163872 | tf_op jit(solution)/shard_map/ppermute | solution.py:20
  49.7 0.2 bitcast_dynamic-update-slice_fusion.2
  49.9 7.1 %collective-permute-done.4 = bf16[10,16,16,32]{3,2,1,0:T(8,128)(2,1)S(1)} collective-permute-done((bf16[10,16,16,32]{3,2,1,0:T(8,128)(2,1)}, bf16[10,16,16,32]{3,2,1,0:T(8,128)(2,1)S(1)}, u32[]{:S(2)}, u32[]{:S(2)}) %collective-permute-start.4) | collective-permute-done | bytes 163872 | tf_op jit(solution)/shard_map/ppermute | solution.py:20
  57.1 0.2 bitcast_dynamic-update-slice_fusion.7
  57.3 0.2 bitcast_dynamic-update-slice_fusion.5
  57.5 0.2 bitcast_dynamic-update-slice_fusion.3
  57.8 0.5 dynamic-slice_bitcast_fusion
  58.3 1.5 copy-done.1
  59.8 3.6 %copy.31 = bf16[10,16,16,4,32]{4,3,1,2,0:T(4,128)(2,1)} copy(bf16[10,16,16,4,32]{4,2,1,0,3:T(8,128)(2,1)S(1)} %dynamic-slice_bitcast_fusion) | data formatting | bytes 1310720
  63.4 3.6 %reshape.151 = bf16[10,16,1,16,128]{4,1,3,0,2:T(8,128)(2,1)S(1)} reshape(bf16[10,16,16,4,32]{4,3,1,2,0:T(4,128)(2,1)} %copy.31) | data formatting | bytes 1310720
  67.1 0.2 pad.10.clone
  67.3 0.3 copy.17
  67.5 0.2 slice.39
  67.7 0.5 copy-done.12
  68.2 6.2 %fusion.8 = f32[8,16,8,3,128]{4,2,3,1,0:T(8,128)S(1)} fusion(bf16[3,3,3,128,128]{4,3,2,1,0:T(8,128)(2,1)S(1)} %bitcast.96, bf16[10,16,1,7,2,128]{5,3,4,1,0,2:T(8,128)(2,1)S(1)} %slice.39, bf16[10,16,1,8,3,128]{5,3,4,1,0,2:T(8,128)(2,1)S(1)} %copy.17, pred[8,3]{0,1:T(4,128)(4,1)S(1)} %copy-done.13), kind=kOutput, calls=%fused_computation.10 | convolution fusion | flops 2609971200 | bytes 4014104 | tf_op jit(solution)/shard_map/conv_general_dilated | solution.py:123
  74.4 0.3 copy.18
  74.8 0.5 multiply_convert_fusion.1
  75.3 2.7 %collective-permute-start.6 = (bf16[1,16,16,128]{3,2,1,0:T(8,128)(2,1)S(1)}, bf16[1,16,16,128]{3,2,1,0:T(8,128)(2,1)S(1)}, u32[]{:S(2)}, u32[]{:S(2)}) collective-permute-start(bf16[1,16,16,128]{3,2,1,0:T(8,128)(2,1)S(1)} %get-tuple-element.3), channel_id=1, source_target_pairs={{4,0},{8,4},{12,8},{16,12},{20,16},{24,20},{28,24},{32,28},{36,32}... | collective-permute-start | bytes 196616 | tf_op jit(solution)/shard_map/ppermute | solution.py:114
  78.1 3.3 %collective-permute-start.5 = (bf16[1,16,16,128]{3,2,1,0:T(8,128)(2,1)S(1)}, bf16[1,16,16,128]{3,2,1,0:T(8,128)(2,1)S(1)}, u32[]{:S(2)}, u32[]{:S(2)}) collective-permute-start(bf16[1,16,16,128]{3,2,1,0:T(8,128)(2,1)S(1)} %get-tuple-element.2), channel_id=1, source_target_pairs={{0,4},{4,8},{8,12},{12,16},{16,20},{20,24},{24,28},{28,32},{32,36}... | collective-permute-start | bytes 196616 | tf_op jit(solution)/shard_map/ppermute | solution.py:112
  81.4 0.5 slice_convert_fusion
  81.9 4.8 %copy.13 = f32[8,16,16,4,32]{4,3,2,1,0:T(4,128)} copy(f32[8,16,16,4,32]{4,2,1,0,3:T(8,128)S(1)} %slice_convert_fusion) | data formatting | bytes 2097152 | tf_op jit(solution)/shard_map/convert_element_type | solution.py:157
  86.7 4.3 %reshape.141 = f32[4,2,8,2,8,2,128]{6,5,4,3,2,1,0:T(2,128)S(1)} reshape(f32[8,16,16,4,32]{4,3,2,1,0:T(4,128)} %copy.13) | data formatting | bytes 2097152 | tf_op jit(solution)/shard_map/convert_element_type | solution.py:157
  91.1 11.7 %fusion.11 = f32[1,8,16,16,128]{4,0,3,2,1:T(1,128)S(1)} fusion(bf16[3,3,3,128,128]{4,3,2,1,0:T(8,128)(2,1)} %bitcast.97, bf16[1,10,16,16,128]{4,3,2,1,0:T(8,128)(2,1)S(1)} %maximum_bitcast_fusion), kind=kOutput, calls=%fused_computation.11 | convolution fusion | flops 1664090112 | bytes 2588672 | tf_op jit(solution)/shard_map/conv_general_dilated | solution.py:123
  102.8 1.3 fusion.19
  104.3 0.5 multiply_reduce_fusion
  104.8 0.8 copy-done.3
  105.6 0.3 convolution_convert_fusion.1
  106.4 0.3 collective-permute-start.7
  106.8 1.2 collective-permute-done.7
  108.1 0.2 slice_reduce_fusion
  108.3 0.7 fusion.33
  109.0 0.7 fusion.25
  109.8 0.4 collective-permute-start.12
  110.2 0.3 collective-permute-start.13
  110.5 0.8 collective-permute-start.14
  111.3 1.3 collective-permute-done.12
  112.6 1.8 collective-permute-done.13
  114.5 0.9 collective-permute-done.14
  115.4 3.7 %reshape.140 = f32[8,16,16,128]{3,2,1,0:T(8,128)S(1)} reshape(f32[8,16,16,4,32]{4,3,2,1,0:T(4,128)} %copy.13) | data formatting | bytes 2097152 | tf_op jit(solution)/shard_map/convert_element_type | solution.py:157
  119.1 73.6 %all-gather.3.cloned.1.call-done = bf16[16896,128]{1,0:T(8,128)(2,1)} async-done(((bf16[528,128]{1,0:T(8,128)(2,1)}), bf16[16896,128]{1,0:T(8,128)(2,1)}) %all-gather.3.cloned.1.call-update) | async-done | bytes 4325392 | tf_op jit(solution)/shard_map/all_gather | solution.py:197
  192.7 22.0 %shard_map.95 = bf16[512,64]{1,0:T(8,128)(2,1)} custom-call(bf16[512,128]{1,0:T(8,128)(2,1)} %get-tuple-element.7.refs_0_, bf16[32,528,128]{2,1,0:T(8,128)(2,1)} %bitcast.82), custom_call_target="tpu_custom_call" | custom-call | tf_op jit(solution)/shard_map/pallas_call | solution.py:88
  214.7 0.9 constant_dynamic-slice_fusion.2
  215.6 4.1 %collective-permute-start.8 = (bf16[256,64]{1,0:T(8,128)(2,1)S(1)}, bf16[256,64]{1,0:T(8,128)(2,1)S(1)}, u32[]{:S(2)}, u32[]{:S(2)}) collective-permute-start(bf16[256,64]{1,0:T(8,128)(2,1)S(1)} %get-tuple-element.13), channel_id=1, source_target_pairs={{0,4},{4,0},{1,5},{5,1},{2,6},{6,2},{3,7},{7,3},{8,12},{12,8},{9,1... | collective-permute-start | bytes 98312 | tf_op jit(solution)/shard_map/ppermute | solution.py:201
  219.6 1.7 fusion.17
  221.4 2.5 %collective-permute-start.9 = (bf16[256,128]{1,0:T(8,128)(2,1)S(1)}, bf16[256,128]{1,0:T(8,128)(2,1)S(1)}, u32[]{:S(2)}, u32[]{:S(2)}) collective-permute-start(bf16[256,128]{1,0:T(8,128)(2,1)S(1)} %maximum_select_fusion.2), channel_id=1, source_target_pairs={{0,3},{1,0},{2,1},{3,2},{4,7},{5,4},{6,5},{7,6},{8,11},{9,8},{10,9... | collective-permute-start | bytes 196616 | tf_op jit(solution)/shard_map/ppermute | solution.py:20
  224.0 0.5 collective-permute-start.10
  224.5 0.6 collective-permute-start.11
  225.3 3.3 %collective-permute-done.10 = bf16[256,128]{1,0:T(8,128)(2,1)S(1)} collective-permute-done((bf16[256,128]{1,0:T(8,128)(2,1)S(1)}, bf16[256,128]{1,0:T(8,128)(2,1)S(1)}, u32[]{:S(2)}, u32[]{:S(2)}) %collective-permute-start.10) | collective-permute-done | bytes 65568 | tf_op jit(solution)/shard_map/ppermute | solution.py:20
  228.7 2.0 collective-permute-done.11
  230.9 1.8 fusion.15
  (68 shorter events, 2.3 us)
Async XLA Ops:
  7.2 97.1 %copy-start = (bf16[8,128,512]{2,1,0:T(8,128)(2,1)S(1)}, bf16[8,128,512]{2,1,0:T(8,128)(2,1)}, u32[]{:S(2)}) copy-start(bf16[8,128,512]{2,1,0:T(8,128)(2,1)} %param.12) | copy-start | bytes 3145732
  7.2 16.4 %copy-start.8 = (bf16[512,3,128]{2,0,1:T(8,128)(2,1)S(1)}, bf16[512,3,128]{2,0,1:T(8,128)(2,1)}, u32[]{:S(2)}) copy-start(bf16[512,3,128]{2,0,1:T(8,128)(2,1)} %param.14) | copy-start | bytes 1179652
  7.2 185.5 %all-gather.3.cloned.1.call-start = ((), (), s32[]{:S(2)}) async-start(), calls=%async_computation | async-start | bytes 4460544 | tf_op jit(solution)/shard_map/all_gather | solution.py:197
  8.2 66.5 %copy-start.5 = (f32[8,16,16]{2,1,0:T(8,128)}, f32[8,16,16]{2,1,0:T(8,128)S(1)}, u32[]{:S(2)}) copy-start(f32[8,16,16]{2,1,0:T(8,128)S(1)} %get-tuple-element.15) | copy-start | bytes 24580
  9.7 7.0 %collective-permute-start.1 = (bf16[1,16,16,32]{3,2,1,0:T(8,128)(2,1)S(1)}, bf16[1,16,16,32]{3,2,1,0:T(8,128)(2,1)S(1)}, u32[]{:S(2)}, u32[]{:S(2)}) collective-permute-start(bf16[1,16,16,32]{3,2,1,0:T(8,128)(2,1)S(1)} %get-tuple-element.5), channel_id=1, source_target_pairs={{4,0},{8,4},{12,8},{16,12},{20,16},{24,20},{28,24},{32,28},{36,32}... | collective-permute-start | bytes 49160 | tf_op jit(solution)/shard_map/ppermute | solution.py:114
  14.8 3.2 %collective-permute-start = (bf16[1,16,16,32]{3,2,1,0:T(8,128)(2,1)S(1)}, bf16[1,16,16,32]{3,2,1,0:T(8,128)(2,1)S(1)}, u32[]{:S(2)}, u32[]{:S(2)}) collective-permute-start(bf16[1,16,16,32]{3,2,1,0:T(8,128)(2,1)S(1)} %get-tuple-element.4), channel_id=1, source_target_pairs={{0,4},{4,8},{8,12},{12,16},{16,20},{20,24},{24,28},{28,32},{32,36}... | collective-permute-start | bytes 49160 | tf_op jit(solution)/shard_map/ppermute | solution.py:112
  19.0 30.5 %collective-permute-start.2 = (bf16[10,16,16,32]{3,2,1,0:T(8,128)(2,1)}, bf16[10,16,16,32]{3,2,1,0:T(8,128)(2,1)S(1)}, u32[]{:S(2)}, u32[]{:S(2)}) collective-permute-start(bf16[10,16,16,32]{3,2,1,0:T(8,128)(2,1)} %pad_maximum_fusion), channel_id=1, source_target_pairs={{0,3},{1,0},{2,1},{3,2},{4,7},{5,4},{6,5},{7,6},{8,11},{9,8},{10,9... | collective-permute-start | bytes 491528 | tf_op jit(solution)/shard_map/ppermute | solution.py:20
  24.7 25.0 %collective-permute-start.3 = (bf16[10,16,16,32]{3,2,1,0:T(8,128)(2,1)}, bf16[10,16,16,32]{3,2,1,0:T(8,128)(2,1)S(1)}, u32[]{:S(2)}, u32[]{:S(2)}) collective-permute-start(bf16[10,16,16,32]{3,2,1,0:T(8,128)(2,1)} %pad_maximum_fusion), channel_id=1, source_target_pairs={{0,2},{1,3},{2,0},{3,1},{4,6},{5,7},{6,4},{7,5},{8,10},{9,11},{10,... | collective-permute-start | bytes 491528 | tf_op jit(solution)/shard_map/ppermute | solution.py:20
  25.1 31.9 %collective-permute-start.4 = (bf16[10,16,16,32]{3,2,1,0:T(8,128)(2,1)}, bf16[10,16,16,32]{3,2,1,0:T(8,128)(2,1)S(1)}, u32[]{:S(2)}, u32[]{:S(2)}) collective-permute-start(bf16[10,16,16,32]{3,2,1,0:T(8,128)(2,1)} %pad_maximum_fusion), channel_id=1, source_target_pairs={{0,1},{1,2},{2,3},{3,0},{4,5},{5,6},{6,7},{7,4},{8,9},{9,10},{10,1... | collective-permute-start | bytes 491528 | tf_op jit(solution)/shard_map/ppermute | solution.py:20
  58.3 1.5 copy-start.1
  67.0 1.2 copy-start.12
  67.0 1.2 copy-start.13
  74.4 7.0 %copy-start.2 = (bf16[10,16,16,4,32]{4,2,1,0,3:T(8,128)(2,1)S(1)}, bf16[10,16,16,4,32]{4,2,1,0,3:T(8,128)(2,1)}, u32[]{:S(2)}) copy-start(bf16[10,16,16,4,32]{4,2,1,0,3:T(8,128)(2,1)} %copy-done.1) | copy-start | bytes 1966084
  75.3 15.6 %collective-permute-start.6 = (bf16[1,16,16,128]{3,2,1,0:T(8,128)(2,1)S(1)}, bf16[1,16,16,128]{3,2,1,0:T(8,128)(2,1)S(1)}, u32[]{:S(2)}, u32[]{:S(2)}) collective-permute-start(bf16[1,16,16,128]{3,2,1,0:T(8,128)(2,1)S(1)} %get-tuple-element.3), channel_id=1, source_target_pairs={{4,0},{8,4},{12,8},{16,12},{20,16},{24,20},{28,24},{32,28},{36,32}... | collective-permute-start | bytes 196616 | tf_op jit(solution)/shard_map/ppermute | solution.py:114
  78.1 12.9 %collective-permute-start.5 = (bf16[1,16,16,128]{3,2,1,0:T(8,128)(2,1)S(1)}, bf16[1,16,16,128]{3,2,1,0:T(8,128)(2,1)S(1)}, u32[]{:S(2)}, u32[]{:S(2)}) collective-permute-start(bf16[1,16,16,128]{3,2,1,0:T(8,128)(2,1)S(1)} %get-tuple-element.2), channel_id=1, source_target_pairs={{0,4},{4,8},{8,12},{12,16},{16,20},{20,24},{24,28},{28,32},{32,36}... | collective-permute-start | bytes 196616 | tf_op jit(solution)/shard_map/ppermute | solution.py:112
  91.1 11.7 %copy-start.4 = (f32[4,2,8,2,8,2]{5,4,3,2,1,0:T(8,128)S(1)}, f32[4,2,8,2,8,2]{5,4,3,2,1,0:T(8,128)}, u32[]{:S(2)}) copy-start(f32[4,2,8,2,8,2]{5,4,3,2,1,0:T(8,128)} %mul.83) | copy-start | bytes 24580
  102.8 2.9 %copy-start.10 = (f32[512]{0:T(512)S(1)}, f32[512]{0:T(512)}, u32[]{:S(2)}) copy-start(f32[512]{0:T(512)} %param.13) | copy-start | bytes 6148
  104.1 2.2 copy-start.7
  104.1 4.2 %copy-start.11 = (pred[128]{0:T(512)(128)(4,1)S(1)}, pred[128]{0:T(512)(128)(4,1)}, u32[]{:S(2)}) copy-start(pred[128]{0:T(512)(128)(4,1)} %constant.72.clone.1) | copy-start | bytes 388
  104.2 5.5 %copy-start.9 = (bf16[128,512]{1,0:T(8,128)(2,1)S(1)}, bf16[128,512]{1,0:T(8,128)(2,1)}, u32[]{:S(2)}) copy-start(bf16[128,512]{1,0:T(8,128)(2,1)} %param.15) | copy-start | bytes 393220
  104.8 0.8 copy-start.3
  106.4 1.6 collective-permute-start.7
  109.8 2.8 %collective-permute-start.12 = (bf16[128,128]{1,0:T(8,128)(2,1)S(1)}, bf16[128,128]{1,0:T(8,128)(2,1)S(1)}, u32[]{:S(2)}, u32[]{:S(2)}) collective-permute-start(bf16[128,128]{1,0:T(8,128)(2,1)S(1)} %get-tuple-element.11), channel_id=1, source_target_pairs={{0,3},{1,0},{2,1},{3,2},{4,7},{5,4},{6,5},{7,6},{8,11},{9,8},{10,9... | collective-permute-start | bytes 98312 | tf_op jit(solution)/shard_map/ppermute | solution.py:20
  110.2 4.3 %collective-permute-start.13 = (bf16[128,128]{1,0:T(8,128)(2,1)S(1)}, bf16[128,128]{1,0:T(8,128)(2,1)S(1)}, u32[]{:S(2)}, u32[]{:S(2)}) collective-permute-start(bf16[128,128]{1,0:T(8,128)(2,1)S(1)} %get-tuple-element.12), channel_id=1, source_target_pairs={{0,2},{1,3},{2,0},{3,1},{4,6},{5,7},{6,4},{7,5},{8,10},{9,11},{10,... | collective-permute-start | bytes 98312 | tf_op jit(solution)/shard_map/ppermute | solution.py:20
  110.5 4.8 %collective-permute-start.14 = (bf16[128,128]{1,0:T(8,128)(2,1)S(1)}, bf16[128,128]{1,0:T(8,128)(2,1)S(1)}, u32[]{:S(2)}, u32[]{:S(2)}) collective-permute-start(bf16[128,128]{1,0:T(8,128)(2,1)S(1)} %get-tuple-element.10), channel_id=1, source_target_pairs={{0,1},{1,2},{2,3},{3,0},{4,5},{5,6},{6,7},{7,4},{8,9},{9,10},{10,1... | collective-permute-start | bytes 98312 | tf_op jit(solution)/shard_map/ppermute | solution.py:20
  119.1 100.5 %copy-start.6 = (f32[8,16,16]{2,1,0:T(8,128)S(1)}, f32[8,16,16]{2,1,0:T(8,128)}, u32[]{:S(2)}) copy-start(f32[8,16,16]{2,1,0:T(8,128)} %copy-done.5) | copy-start | bytes 24580
  215.6 5.7 %collective-permute-start.8 = (bf16[256,64]{1,0:T(8,128)(2,1)S(1)}, bf16[256,64]{1,0:T(8,128)(2,1)S(1)}, u32[]{:S(2)}, u32[]{:S(2)}) collective-permute-start(bf16[256,64]{1,0:T(8,128)(2,1)S(1)} %get-tuple-element.13), channel_id=1, source_target_pairs={{0,4},{4,0},{1,5},{5,1},{2,6},{6,2},{3,7},{7,3},{8,12},{12,8},{9,1... | collective-permute-start | bytes 98312 | tf_op jit(solution)/shard_map/ppermute | solution.py:201
  221.4 3.9 %collective-permute-start.9 = (bf16[256,128]{1,0:T(8,128)(2,1)S(1)}, bf16[256,128]{1,0:T(8,128)(2,1)S(1)}, u32[]{:S(2)}, u32[]{:S(2)}) collective-permute-start(bf16[256,128]{1,0:T(8,128)(2,1)S(1)} %maximum_select_fusion.2), channel_id=1, source_target_pairs={{0,3},{1,0},{2,1},{3,2},{4,7},{5,4},{6,5},{7,6},{8,11},{9,8},{10,9... | collective-permute-start | bytes 196616 | tf_op jit(solution)/shard_map/ppermute | solution.py:20
  224.0 4.7 %collective-permute-start.10 = (bf16[256,128]{1,0:T(8,128)(2,1)S(1)}, bf16[256,128]{1,0:T(8,128)(2,1)S(1)}, u32[]{:S(2)}, u32[]{:S(2)}) collective-permute-start(bf16[256,128]{1,0:T(8,128)(2,1)S(1)} %maximum_select_fusion.2), channel_id=1, source_target_pairs={{0,2},{1,3},{2,0},{3,1},{4,6},{5,7},{6,4},{7,5},{8,10},{9,11},{10,... | collective-permute-start | bytes 196616 | tf_op jit(solution)/shard_map/ppermute | solution.py:20
  224.5 6.2 %collective-permute-start.11 = (bf16[256,128]{1,0:T(8,128)(2,1)S(1)}, bf16[256,128]{1,0:T(8,128)(2,1)S(1)}, u32[]{:S(2)}, u32[]{:S(2)}) collective-permute-start(bf16[256,128]{1,0:T(8,128)(2,1)S(1)} %maximum_select_fusion.2), channel_id=1, source_target_pairs={{0,1},{1,2},{2,3},{3,0},{4,5},{5,6},{6,7},{7,4},{8,9},{9,10},{10,1... | collective-permute-start | bytes 196616 | tf_op jit(solution)/shard_map/ppermute | solution.py:20
Sparse Core Ops, SparseCore 0:
  109.8 82.8 all-gather.2

commit v5 on v4

--- a/solution.py
+++ b/solution.py
@@ -147,10 +147,10 @@
     tokens = nx // 2 * (ny // 2) * (nz // 2)
     occupied = mask.astype(jnp.float32)[..., None]
     masked = features * mask.astype(jnp.bfloat16)[..., None]
-    halo = with_halo(masked, SPACE, 1)
-    rimmed = gather_head(lambda shift: halo)
-    rimmed = jnp.moveaxis(rimmed, 0, 3).reshape(halo.shape[:3] + (-1,))
-    whole_masked = lax.slice_in_dim(rimmed, 1, nx + 1, axis=0)
+    whole = gather_head(lambda shift: features)
+    whole = jnp.moveaxis(whole, 0, 3).reshape(features.shape[:3] + (-1,))
+    whole_masked = whole * mask.astype(jnp.bfloat16)[..., None]
+    rimmed = with_halo(whole_masked, SPACE, 1)
     pre1 = convolve(rimmed, conv1_weight)
     hidden = (occupied * jax.nn.silu(pre1)).astype(jnp.bfloat16)
     pre2 = convolve(with_halo(hidden, SPACE, 1), conv2_weight)

time: 243 us -> 233 us (0.959); the launches traced: 240 us -> 232 us
  waiting for transfers between devices: 116 us -> 103 us
  other arithmetic: 10.4 us -> 14.3 us
    convert_element_type x3 -> x0, local copies, waits for them, and re-layouts: 12.8 us -> none  [body(): whole_masked.astype(jnp.float32) + pre2]
    ppermute x9, waiting for transfers between devices: 39.9 us -> 28.3 us  [gather_head(): lax.ppermute(piece_for(shift), 'head', [(i, (i + shift) % count) for i in...]
    transpose x1 -> x2, local copies, waits for them, and re-layouts: 0.46 us -> 4.66 us  [body(): whole = jnp.moveaxis(whole, 0, 3).reshape(features.shape[:3] + (-1,))]
    unnamed x48 -> x53, local copies, waits for them, and re-layouts: 11.2 us -> 14.9 us
    reshape x0 -> x2, local copies, waits for them, and re-layouts: none -> 3.52 us  [body(): whole = jnp.moveaxis(whole, 0, 3).reshape(features.shape[:3] + (-1,))]
    ppermute x2, starting transfers between devices: 7.82 us -> 4.31 us  [with_halo(): lax.ppermute(head, axis, [(i + 1, i) for i in range(ends)])]
    ppermute x2, starting transfers between devices: 5.23 us -> 7.83 us  [with_halo(): lax.ppermute(tail, axis, [(i, i + 1) for i in range(ends)])]
  transfers between devices with their start and end apart: 16 -> 16, of which waited for: 11 -> 9; matrix products, arithmetic and copies ran while one was open for 8% -> 9% of each run, Pallas kernels for 0% -> 0%
where the time goes in v5:
time: 233 us; the launch traced here: 232 us
  waiting for transfers between devices  103 us (44%)
  local copies, waits for them, and re-layouts  32.2 us (14%)
  starting transfers between devices  26.6 us (11%)
  Pallas kernels  22 us (9%)
  matrix products  19.6 us (8%)
  between operations  14.5 us (6%)
  other arithmetic  14.3 us (6%)
    all_gather x1, waiting for transfers between devices, body(): gathered = lax.all_gather(piece[None], 'chip', axis=0, tiled=True)  72 us
    ppermute x9, waiting for transfers between devices, gather_head(): lax.ppermute(piece_for(shift), 'head', [(i, (i + shift) % count) for i in...  28.3 us
    pallas_call x1, Pallas kernels, attend(): pl.pallas_call(kernel, grid=(parts // per,), in_specs=[pl.BlockSpec(query...  22 us
    conv_general_dilated x2, matrix products, convolve(): lax.conv_general_dilated(rimmed[None], kernel, window_strides=(1, 1, 1),...  17.9 us
    unnamed x53, local copies, waits for them, and re-layouts  14.9 us
    ppermute x9, starting transfers between devices, gather_head(): lax.ppermute(piece_for(shift), 'head', [(i, (i + shift) % count) for i in...  10.3 us
    ppermute x2, starting transfers between devices, with_halo(): lax.ppermute(tail, axis, [(i, i + 1) for i in range(ends)])  7.83 us
    transpose x2, local copies, waits for them, and re-layouts, body(): whole = jnp.moveaxis(whole, 0, 3).reshape(features.shape[:3] + (-1,))  4.66 us
  transfers between devices with their start and end apart: 16, of which 9 were waited for; matrix products, arithmetic and copies ran while one was open for 9% of the time, Pallas kernels for 0%

profile of v5, /device:TPU:1, one launch (start us, length us, event | category | flops | bytes accessed | tf_op | source)
XLA Modules:
  0.0 232.3 jit_solution(11782810367171122720)
XLA Ops:
  7.2 3.6 %collective-permute-start = (bf16[8,16,16,32]{3,2,1,0:T(8,128)(2,1)}, bf16[8,16,16,32]{3,2,1,0:T(8,128)(2,1)S(1)}, u32[]{:S(2)}, u32[]{:S(2)}) collective-permute-start(bf16[8,16,16,32]{3,2,1,0:T(8,128)(2,1)} %param.8), channel_id=1, source_target_pairs={{0,3},{1,0},{2,1},{3,2},{4,7},{5,4},{6,5},{7,6},{8,11},{9,8},{10,9... | collective-permute-start | bytes 393224 | tf_op jit(solution)/shard_map/ppermute | solution.py:20
  11.2 0.7 collective-permute-start.2
  11.9 1.9 bitcast_dynamic-update-slice_fusion.6
  13.8 0.9 fusion.34
  14.7 18.1 %collective-permute-done = bf16[8,16,16,32]{3,2,1,0:T(8,128)(2,1)S(1)} collective-permute-done((bf16[8,16,16,32]{3,2,1,0:T(8,128)(2,1)}, bf16[8,16,16,32]{3,2,1,0:T(8,128)(2,1)S(1)}, u32[]{:S(2)}, u32[]{:S(2)}) %collective-permute-start) | collective-permute-done | bytes 131104 | tf_op jit(solution)/shard_map/ppermute | solution.py:20
  32.9 0.8 bitcast_dynamic-update-slice_fusion.4
  33.7 0.8 bitcast_dynamic-update-slice_fusion.2
  34.6 3.1 %collective-permute-done.2 = bf16[8,16,16,32]{3,2,1,0:T(8,128)(2,1)S(1)} collective-permute-done((bf16[8,16,16,32]{3,2,1,0:T(8,128)(2,1)}, bf16[8,16,16,32]{3,2,1,0:T(8,128)(2,1)S(1)}, u32[]{:S(2)}, u32[]{:S(2)}) %collective-permute-start.2) | collective-permute-done | bytes 131104 | tf_op jit(solution)/shard_map/ppermute | solution.py:20
  37.7 0.8 bitcast_dynamic-update-slice_fusion
  38.5 0.8 bitcast_dynamic-update-slice_fusion.7
  39.3 0.8 bitcast_dynamic-update-slice_fusion.5
  40.2 0.8 bitcast_dynamic-update-slice_fusion.3
  41.0 0.8 bitcast_dynamic-update-slice_fusion.1
  41.8 2.0 dynamic-slice_bitcast_fusion
  43.8 2.7 %copy.13 = bf16[8,16,16,4,32]{4,3,2,1,0:T(4,128)(2,1)S(1)} copy(bf16[8,16,16,4,32]{4,2,1,0,3:T(8,128)(2,1)S(1)} %dynamic-slice_bitcast_fusion) | data formatting | bytes 1048576 | tf_op jit(solution)/shard_map/transpose | solution.py:151
  46.5 1.8 reshape.125
  48.2 1.5 broadcast_multiply_fusion
  49.7 2.4 %collective-permute-start.4 = (bf16[1,16,16,128]{3,2,1,0:T(8,128)(2,1)S(1)}, bf16[1,16,16,128]{3,2,1,0:T(8,128)(2,1)S(1)}, u32[]{:S(2)}, u32[]{:S(2)}) collective-permute-start(bf16[1,16,16,128]{3,2,1,0:T(8,128)(2,1)S(1)} %get-tuple-element.5), channel_id=1, source_target_pairs={{4,0},{8,4},{12,8},{16,12},{20,16},{24,20},{28,24},{32,28},{36,32}... | collective-permute-start | bytes 196616 | tf_op jit(solution)/shard_map/ppermute | solution.py:114
  52.1 3.3 %collective-permute-start.3 = (bf16[1,16,16,128]{3,2,1,0:T(8,128)(2,1)S(1)}, bf16[1,16,16,128]{3,2,1,0:T(8,128)(2,1)S(1)}, u32[]{:S(2)}, u32[]{:S(2)}) collective-permute-start(bf16[1,16,16,128]{3,2,1,0:T(8,128)(2,1)S(1)} %get-tuple-element.4), channel_id=1, source_target_pairs={{0,4},{4,8},{8,12},{12,16},{16,20},{20,24},{24,28},{28,32},{32,36}... | collective-permute-start | bytes 196616 | tf_op jit(solution)/shard_map/ppermute | solution.py:112
  55.5 1.1 collective-permute-done.3
  57.6 6.2 %fusion.8 = f32[8,16,8,3,128]{4,2,3,1,0:T(8,128)S(1)} fusion(bf16[3,3,3,128,128]{4,3,2,1,0:T(8,128)(2,1)S(1)} %bitcast.96, bf16[10,16,1,7,2,128]{5,3,4,1,0,2:T(8,128)(2,1)S(1)} %slice.33, bf16[10,16,1,8,3,128]{5,3,4,1,0,2:T(8,128)(2,1)S(1)} %copy.16, pred[8,3]{0,1:T(4,128)(4,1)S(1)} %copy-done.15), kind=kOutput, calls=%fused_computation.9 | convolution fusion | flops 2609971200 | bytes 4014104 | tf_op jit(solution)/shard_map/conv_general_dilated | solution.py:123
  64.1 0.5 multiply_convert_fusion.1
  64.7 0.8 copy-done.3
  65.5 0.6 fusion.31
  66.1 1.9 collective-permute-start.6
  68.0 4.5 %collective-permute-start.5 = (bf16[1,16,16,128]{3,2,1,0:T(8,128)(2,1)}, bf16[1,16,16,128]{3,2,1,0:T(8,128)(2,1)}, u32[]{:S(2)}, u32[]{:S(2)}) collective-permute-start(bf16[1,16,16,128]{3,2,1,0:T(8,128)(2,1)} %get-tuple-element.2), channel_id=1, source_target_pairs={{0,4},{4,8},{8,12},{12,16},{16,20},{20,24},{24,28},{28,32},{32,36}... | collective-permute-start | bytes 196616 | tf_op jit(solution)/shard_map/ppermute | solution.py:112
  72.5 1.0 reshape.133
  73.5 1.0 mul.90
  74.5 0.9 mul.92
  75.4 1.7 reduce_max.9
  77.1 0.7 convert_element_type.69
  77.8 1.2 copy.22
  79.0 1.8 reshape.128
  80.8 1.2 maximum_bitcast_fusion.1
  82.0 11.7 %fusion.11 = f32[1,8,16,16,128]{4,0,3,2,1:T(1,128)S(1)} fusion(bf16[3,3,3,128,128]{4,3,2,1,0:T(8,128)(2,1)} %bitcast.97, bf16[1,10,16,16,128]{4,3,2,1,0:T(8,128)(2,1)S(1)} %maximum_bitcast_fusion.1), kind=kOutput, calls=%fused_computation.10 | convolution fusion | flops 1664090112 | bytes 2588672 | tf_op jit(solution)/shard_map/conv_general_dilated | solution.py:123
  93.7 2.5 %fusion.19 = bf16[4,8,8,2,2,2,128]{6,5,2,4,1,3,0:T(2,128)(2,1)S(1)} fusion(f32[4,2,8,2,8,2,128]{6,5,4,3,2,1,0:T(2,128)S(1)} %bitcast.83, bf16[4,2,8,2,8,2,128]{6,5,4,3,2,1,0:T(2,128)(2,1)S(1)} %copy-done.5, f32[4,2,8,2,8,2]{5,4,3,2,1,0:T(8,128)S(1)} %copy-done.6, bf16[4,2,8,2,8,2]{5,4,3,2,1,0:T(8,128)(2,1)S(1)} %copy-done.9), kind=kLoop, calls=%fused_computation.27 | loop fusion | flops 1310720 | bytes 2109440 | tf_op jit(solution)/shard_map/transpose | solution.py:136
  97.6 1.6 pad_maximum_fusion
  99.3 1.6 collective-permute-done.7
  100.9 1.1 maximum_select_fusion
  102.2 0.7 fusion.33
  102.9 0.7 fusion.25
  103.7 0.8 constant_dynamic-slice_fusion.6
  104.5 1.3 collective-permute-start.12
  105.8 0.7 collective-permute-start.14
  106.5 1.4 constant_dynamic-update-slice_fusion.9
  107.8 0.6 constant_dynamic-update-slice_fusion.8
  108.5 1.7 collective-permute-done.13
  110.1 0.6 constant_dynamic-update-slice_fusion.7
  110.7 0.6 constant_dynamic-update-slice_fusion.6
  111.4 1.4 constant_dynamic-update-slice_fusion.5
  112.7 0.6 constant_dynamic-update-slice_fusion.4
  113.3 0.6 constant_dynamic-update-slice_fusion.3
  113.9 0.6 constant_dynamic-update-slice_fusion.2
  114.6 72.0 %all-gather.3.cloned.1.call-done = bf16[16896,128]{1,0:T(8,128)(2,1)} async-done(((bf16[528,128]{1,0:T(8,128)(2,1)}), bf16[16896,128]{1,0:T(8,128)(2,1)}) %all-gather.3.cloned.1.call-update) | async-done | bytes 4325392 | tf_op jit(solution)/shard_map/all_gather | solution.py:197
  186.5 22.0 %shard_map.95 = bf16[512,64]{1,0:T(8,128)(2,1)} custom-call(bf16[512,128]{1,0:T(8,128)(2,1)} %get-tuple-element.7.refs_0_, bf16[32,528,128]{2,1,0:T(8,128)(2,1)} %bitcast.82), custom_call_target="tpu_custom_call" | custom-call | tf_op jit(solution)/shard_map/pallas_call | solution.py:88
  208.5 0.9 constant_dynamic-slice_fusion.2
  209.4 4.1 %collective-permute-start.8 = (bf16[256,64]{1,0:T(8,128)(2,1)S(1)}, bf16[256,64]{1,0:T(8,128)(2,1)S(1)}, u32[]{:S(2)}, u32[]{:S(2)}) collective-permute-start(bf16[256,64]{1,0:T(8,128)(2,1)S(1)} %get-tuple-element.13), channel_id=1, source_target_pairs={{0,4},{4,0},{1,5},{5,1},{2,6},{6,2},{3,7},{7,3},{8,12},{12,8},{9,1... | collective-permute-start | bytes 98312 | tf_op jit(solution)/shard_map/ppermute | solution.py:201
  213.5 1.5 fusion.17
  215.2 2.5 %collective-permute-start.9 = (bf16[256,128]{1,0:T(8,128)(2,1)S(1)}, bf16[256,128]{1,0:T(8,128)(2,1)S(1)}, u32[]{:S(2)}, u32[]{:S(2)}) collective-permute-start(bf16[256,128]{1,0:T(8,128)(2,1)S(1)} %maximum_select_fusion.2), channel_id=1, source_target_pairs={{0,3},{1,0},{2,1},{3,2},{4,7},{5,4},{6,5},{7,6},{8,11},{9,8},{10,9... | collective-permute-start | bytes 196616 | tf_op jit(solution)/shard_map/ppermute | solution.py:20
  217.7 0.5 collective-permute-start.10
  218.2 0.6 collective-permute-start.11
  219.0 3.3 %collective-permute-done.10 = bf16[256,128]{1,0:T(8,128)(2,1)S(1)} collective-permute-done((bf16[256,128]{1,0:T(8,128)(2,1)S(1)}, bf16[256,128]{1,0:T(8,128)(2,1)S(1)}, u32[]{:S(2)}, u32[]{:S(2)}) %collective-permute-start.10) | collective-permute-done | bytes 65568 | tf_op jit(solution)/shard_map/ppermute | solution.py:20
  222.4 2.0 collective-permute-done.11
  224.6 0.9 fusion.15
  (71 shorter events, 3.8 us)
Async XLA Ops:
  7.2 89.2 %copy-start = (bf16[8,128,512]{2,1,0:T(8,128)(2,1)S(1)}, bf16[8,128,512]{2,1,0:T(8,128)(2,1)}, u32[]{:S(2)}) copy-start(bf16[8,128,512]{2,1,0:T(8,128)(2,1)} %param.12) | copy-start | bytes 3145732
  7.2 31.3 %copy-start.4 = (bf16[8,16,16,32]{3,2,1,0:T(8,128)(2,1)S(1)}, bf16[8,16,16,32]{3,2,1,0:T(8,128)(2,1)}, u32[]{:S(2)}) copy-start(bf16[8,16,16,32]{3,2,1,0:T(8,128)(2,1)} %param.8) | copy-start | bytes 393220
  7.2 179.3 %all-gather.3.cloned.1.call-start = ((), (), s32[]{:S(2)}) async-start(), calls=%async_computation | async-start | bytes 4460544 | tf_op jit(solution)/shard_map/all_gather | solution.py:197
  7.2 25.6 %collective-permute-start = (bf16[8,16,16,32]{3,2,1,0:T(8,128)(2,1)}, bf16[8,16,16,32]{3,2,1,0:T(8,128)(2,1)S(1)}, u32[]{:S(2)}, u32[]{:S(2)}) collective-permute-start(bf16[8,16,16,32]{3,2,1,0:T(8,128)(2,1)} %param.8), channel_id=1, source_target_pairs={{0,3},{1,0},{2,1},{3,2},{4,7},{5,4},{6,5},{7,6},{8,11},{9,8},{10,9... | collective-permute-start | bytes 393224 | tf_op jit(solution)/shard_map/ppermute | solution.py:20
  10.9 22.9 %collective-permute-start.1 = (bf16[8,16,16,32]{3,2,1,0:T(8,128)(2,1)}, bf16[8,16,16,32]{3,2,1,0:T(8,128)(2,1)S(1)}, u32[]{:S(2)}, u32[]{:S(2)}) collective-permute-start(bf16[8,16,16,32]{3,2,1,0:T(8,128)(2,1)} %param.8), channel_id=1, source_target_pairs={{0,2},{1,3},{2,0},{3,1},{4,6},{5,7},{6,4},{7,5},{8,10},{9,11},{10,... | collective-permute-start | bytes 393224 | tf_op jit(solution)/shard_map/ppermute | solution.py:20
  11.2 26.4 %collective-permute-start.2 = (bf16[8,16,16,32]{3,2,1,0:T(8,128)(2,1)}, bf16[8,16,16,32]{3,2,1,0:T(8,128)(2,1)S(1)}, u32[]{:S(2)}, u32[]{:S(2)}) collective-permute-start(bf16[8,16,16,32]{3,2,1,0:T(8,128)(2,1)} %param.8), channel_id=1, source_target_pairs={{0,1},{1,2},{2,3},{3,0},{4,5},{5,6},{6,7},{7,4},{8,9},{9,10},{10,1... | collective-permute-start | bytes 393224 | tf_op jit(solution)/shard_map/ppermute | solution.py:20
  14.7 58.8 %copy-start.7 = (f32[8,16,16]{2,1,0:T(8,128)}, f32[8,16,16]{2,1,0:T(8,128)S(1)}, u32[]{:S(2)}) copy-start(f32[8,16,16]{2,1,0:T(8,128)S(1)} %get-tuple-element.15) | copy-start | bytes 24580
  48.2 9.3 %copy-start.14 = (bf16[27,128,128]{2,1,0:T(8,128)(2,1)S(1)}, bf16[27,128,128]{2,1,0:T(8,128)(2,1)}, u32[]{:S(2)}) copy-start(bf16[27,128,128]{2,1,0:T(8,128)(2,1)} %param.10) | copy-start | bytes 2654212
  48.2 9.3 %copy-start.15 = (pred[8,3]{0,1:T(4,128)(4,1)S(1)}, pred[8,3]{0,1:T(4,128)(4,1)}, u32[]{:S(2)}) copy-start(pred[8,3]{0,1:T(4,128)(4,1)} %constant.89) | copy-start | bytes 76
  49.7 6.9 %copy-start.1 = (bf16[8,16,16,128]{3,2,1,0:T(8,128)(2,1)}, bf16[8,16,16,128]{3,2,1,0:T(8,128)(2,1)S(1)}, u32[]{:S(2)}) copy-start(bf16[8,16,16,128]{3,2,1,0:T(8,128)(2,1)S(1)} %broadcast_multiply_fusion) | copy-start | bytes 1572868
  49.7 5.8 %collective-permute-start.4 = (bf16[1,16,16,128]{3,2,1,0:T(8,128)(2,1)S(1)}, bf16[1,16,16,128]{3,2,1,0:T(8,128)(2,1)S(1)}, u32[]{:S(2)}, u32[]{:S(2)}) collective-permute-start(bf16[1,16,16,128]{3,2,1,0:T(8,128)(2,1)S(1)} %get-tuple-element.5), channel_id=1, source_target_pairs={{4,0},{8,4},{12,8},{16,12},{20,16},{24,20},{28,24},{32,28},{36,32}... | collective-permute-start | bytes 196616 | tf_op jit(solution)/shard_map/ppermute | solution.py:114
  52.1 4.5 %collective-permute-start.3 = (bf16[1,16,16,128]{3,2,1,0:T(8,128)(2,1)S(1)}, bf16[1,16,16,128]{3,2,1,0:T(8,128)(2,1)S(1)}, u32[]{:S(2)}, u32[]{:S(2)}) collective-permute-start(bf16[1,16,16,128]{3,2,1,0:T(8,128)(2,1)S(1)} %get-tuple-element.4), channel_id=1, source_target_pairs={{0,4},{4,8},{8,12},{12,16},{16,20},{20,24},{24,28},{28,32},{32,36}... | collective-permute-start | bytes 196616 | tf_op jit(solution)/shard_map/ppermute | solution.py:112
  63.8 8.8 %copy-start.10 = (s32[8,16,16]{2,1,0:T(8,128)S(1)}, s32[8,16,16]{2,1,0:T(8,128)}, u32[]{:S(2)}) copy-start(s32[8,16,16]{2,1,0:T(8,128)} %param.9) | copy-start | bytes 24580
  64.7 0.8 copy-start.3
  66.1 14.7 %collective-permute-start.6 = (bf16[1,16,16,128]{3,2,1,0:T(8,128)(2,1)}, bf16[1,16,16,128]{3,2,1,0:T(8,128)(2,1)}, u32[]{:S(2)}, u32[]{:S(2)}) collective-permute-start(bf16[1,16,16,128]{3,2,1,0:T(8,128)(2,1)} %get-tuple-element.3), channel_id=1, source_target_pairs={{4,0},{8,4},{12,8},{16,12},{20,16},{24,20},{28,24},{32,28},{36,32}... | collective-permute-start | bytes 196616 | tf_op jit(solution)/shard_map/ppermute | solution.py:114
  68.0 12.7 %collective-permute-start.5 = (bf16[1,16,16,128]{3,2,1,0:T(8,128)(2,1)}, bf16[1,16,16,128]{3,2,1,0:T(8,128)(2,1)}, u32[]{:S(2)}, u32[]{:S(2)}) collective-permute-start(bf16[1,16,16,128]{3,2,1,0:T(8,128)(2,1)} %get-tuple-element.2), channel_id=1, source_target_pairs={{0,4},{4,8},{8,12},{12,16},{16,20},{20,24},{24,28},{28,32},{32,36}... | collective-permute-start | bytes 196616 | tf_op jit(solution)/shard_map/ppermute | solution.py:112
  81.9 11.8 %copy-start.5 = (bf16[4,2,8,2,8,2,128]{6,5,4,3,2,1,0:T(2,128)(2,1)S(1)}, bf16[4,2,8,2,8,2,128]{6,5,4,3,2,1,0:T(2,128)(2,1)}, u32[]{:S(2)}) copy-start(bf16[4,2,8,2,8,2,128]{6,5,4,3,2,1,0:T(2,128)(2,1)} %reshape.128) | copy-start | bytes 1572868
  81.9 11.8 %copy-start.6 = (f32[4,2,8,2,8,2]{5,4,3,2,1,0:T(8,128)S(1)}, f32[4,2,8,2,8,2]{5,4,3,2,1,0:T(8,128)}, u32[]{:S(2)}) copy-start(f32[4,2,8,2,8,2]{5,4,3,2,1,0:T(8,128)} %mul.90) | copy-start | bytes 24580
  82.0 11.8 %copy-start.9 = (bf16[4,2,8,2,8,2]{5,4,3,2,1,0:T(8,128)(2,1)S(1)}, bf16[4,2,8,2,8,2]{5,4,3,2,1,0:T(8,128)(2,1)}, u32[]{:S(2)}) copy-start(bf16[4,2,8,2,8,2]{5,4,3,2,1,0:T(8,128)(2,1)} %mul.92) | copy-start | bytes 12292
  93.7 3.2 %copy-start.12 = (f32[512]{0:T(512)S(1)}, f32[512]{0:T(512)}, u32[]{:S(2)}) copy-start(f32[512]{0:T(512)} %param.13) | copy-start | bytes 6148
  93.7 8.5 %copy-start.13 = (pred[128]{0:T(512)(128)(4,1)S(1)}, pred[128]{0:T(512)(128)(4,1)}, u32[]{:S(2)}) copy-start(pred[128]{0:T(512)(128)(4,1)} %constant.72.clone.1) | copy-start | bytes 388
  97.5 116.0 %copy-start.2 = (bf16[8,16,16,128]{3,2,1,0:T(8,128)(2,1)S(1)}, bf16[8,16,16,128]{3,2,1,0:T(8,128)(2,1)}, u32[]{:S(2)}) copy-start(bf16[8,16,16,128]{3,2,1,0:T(8,128)(2,1)} %copy-done.1) | copy-start | bytes 1572868
  97.5 116.0 %copy-start.8 = (f32[8,16,16]{2,1,0:T(8,128)S(1)}, f32[8,16,16]{2,1,0:T(8,128)}, u32[]{:S(2)}) copy-start(f32[8,16,16]{2,1,0:T(8,128)} %copy-done.7) | copy-start | bytes 24580
  99.2 1.7 collective-permute-start.7
  104.5 3.4 %collective-permute-start.12 = (bf16[128,128]{1,0:T(8,128)(2,1)S(1)}, bf16[128,128]{1,0:T(8,128)(2,1)S(1)}, u32[]{:S(2)}, u32[]{:S(2)}) collective-permute-start(bf16[128,128]{1,0:T(8,128)(2,1)S(1)} %get-tuple-element.11), channel_id=1, source_target_pairs={{0,3},{1,0},{2,1},{3,2},{4,7},{5,4},{6,5},{7,6},{8,11},{9,8},{10,9... | collective-permute-start | bytes 98312 | tf_op jit(solution)/shard_map/ppermute | solution.py:20
  105.8 4.3 %collective-permute-start.13 = (bf16[128,128]{1,0:T(8,128)(2,1)S(1)}, bf16[128,128]{1,0:T(8,128)(2,1)S(1)}, u32[]{:S(2)}, u32[]{:S(2)}) collective-permute-start(bf16[128,128]{1,0:T(8,128)(2,1)S(1)} %get-tuple-element.12), channel_id=1, source_target_pairs={{0,2},{1,3},{2,0},{3,1},{4,6},{5,7},{6,4},{7,5},{8,10},{9,11},{10,... | collective-permute-start | bytes 98312 | tf_op jit(solution)/shard_map/ppermute | solution.py:20
  105.8 4.9 %collective-permute-start.14 = (bf16[128,128]{1,0:T(8,128)(2,1)S(1)}, bf16[128,128]{1,0:T(8,128)(2,1)S(1)}, u32[]{:S(2)}, u32[]{:S(2)}) collective-permute-start(bf16[128,128]{1,0:T(8,128)(2,1)S(1)} %get-tuple-element.10), channel_id=1, source_target_pairs={{0,1},{1,2},{2,3},{3,0},{4,5},{5,6},{6,7},{7,4},{8,9},{9,10},{10,1... | collective-permute-start | bytes 98312 | tf_op jit(solution)/shard_map/ppermute | solution.py:20
  186.5 38.1 %copy-start.11 = (bf16[8,128,128]{2,1,0:T(8,128)(2,1)S(1)}, bf16[8,128,128]{2,1,0:T(8,128)(2,1)}, u32[]{:S(2)}) copy-start(bf16[8,128,128]{2,1,0:T(8,128)(2,1)} %constant_dynamic-update-slice_fusion.2) | copy-start | bytes 786436
  209.4 5.6 %collective-permute-start.8 = (bf16[256,64]{1,0:T(8,128)(2,1)S(1)}, bf16[256,64]{1,0:T(8,128)(2,1)S(1)}, u32[]{:S(2)}, u32[]{:S(2)}) collective-permute-start(bf16[256,64]{1,0:T(8,128)(2,1)S(1)} %get-tuple-element.13), channel_id=1, source_target_pairs={{0,4},{4,0},{1,5},{5,1},{2,6},{6,2},{3,7},{7,3},{8,12},{12,8},{9,1... | collective-permute-start | bytes 98312 | tf_op jit(solution)/shard_map/ppermute | solution.py:201
  215.2 3.9 %collective-permute-start.9 = (bf16[256,128]{1,0:T(8,128)(2,1)S(1)}, bf16[256,128]{1,0:T(8,128)(2,1)S(1)}, u32[]{:S(2)}, u32[]{:S(2)}) collective-permute-start(bf16[256,128]{1,0:T(8,128)(2,1)S(1)} %maximum_select_fusion.2), channel_id=1, source_target_pairs={{0,3},{1,0},{2,1},{3,2},{4,7},{5,4},{6,5},{7,6},{8,11},{9,8},{10,9... | collective-permute-start | bytes 196616 | tf_op jit(solution)/shard_map/ppermute | solution.py:20
  217.7 4.7 %collective-permute-start.10 = (bf16[256,128]{1,0:T(8,128)(2,1)S(1)}, bf16[256,128]{1,0:T(8,128)(2,1)S(1)}, u32[]{:S(2)}, u32[]{:S(2)}) collective-permute-start(bf16[256,128]{1,0:T(8,128)(2,1)S(1)} %maximum_select_fusion.2), channel_id=1, source_target_pairs={{0,2},{1,3},{2,0},{3,1},{4,6},{5,7},{6,4},{7,5},{8,10},{9,11},{10,... | collective-permute-start | bytes 196616 | tf_op jit(solution)/shard_map/ppermute | solution.py:20
  218.2 6.2 %collective-permute-start.11 = (bf16[256,128]{1,0:T(8,128)(2,1)S(1)}, bf16[256,128]{1,0:T(8,128)(2,1)S(1)}, u32[]{:S(2)}, u32[]{:S(2)}) collective-permute-start(bf16[256,128]{1,0:T(8,128)(2,1)S(1)} %maximum_select_fusion.2), channel_id=1, source_target_pairs={{0,1},{1,2},{2,3},{3,0},{4,5},{5,6},{6,7},{7,4},{8,9},{9,10},{10,1... | collective-permute-start | bytes 196616 | tf_op jit(solution)/shard_map/ppermute | solution.py:20
Sparse Core Ops, SparseCore 0:
  103.8 82.7 all-gather.2

commit v6 on v5

--- a/solution.py
+++ b/solution.py
@@ -8,7 +8,7 @@
 HEADS = 8
 SPACE = ("chip", "core")
 CHUNKS_PER_STEP = 8
-GROUP = 4
+GROUP = 8
 
 
 def gather_head(piece_for):

time: 233 us -> 232 us (level)
  no operation moved by 1% of the time
where the time goes in v6:
time: 232 us
  waiting for transfers between devices  103 us (44%)
  local copies, waits for them, and re-layouts  32.2 us (14%)
  starting transfers between devices  26.6 us (11%)
  Pallas kernels  21.3 us (9%)
  matrix products  19.6 us (8%)
  between operations  14.5 us (6%)
  other arithmetic  14.3 us (6%)
    all_gather x1, waiting for transfers between devices, body(): gathered = lax.all_gather(piece[None], 'chip', axis=0, tiled=True)  72 us
    ppermute x9, waiting for transfers between devices, gather_head(): lax.ppermute(piece_for(shift), 'head', [(i, (i + shift) % count) for i in...  28.3 us
    pallas_call x1, Pallas kernels, attend(): pl.pallas_call(kernel, grid=(parts // per,), in_specs=[pl.BlockSpec(query...  21.3 us
    conv_general_dilated x2, matrix products, convolve(): lax.conv_general_dilated(rimmed[None], kernel, window_strides=(1, 1, 1),...  17.9 us
    unnamed x53, local copies, waits for them, and re-layouts  14.9 us
    ppermute x9, starting transfers between devices, gather_head(): lax.ppermute(piece_for(shift), 'head', [(i, (i + shift) % count) for i in...  10.3 us
    ppermute x2, starting transfers between devices, with_halo(): lax.ppermute(tail, axis, [(i, i + 1) for i in range(ends)])  7.83 us
    transpose x2, local copies, waits for them, and re-layouts, body(): whole = jnp.moveaxis(whole, 0, 3).reshape(features.shape[:3] + (-1,))  4.66 us
  transfers between devices with their start and end apart: 16, of which 9 were waited for; matrix products, arithmetic and copies ran while one was open for 9% of the time, Pallas kernels for 0%

profile of v6, /device:TPU:1, one launch (start us, length us, event | category | flops | bytes accessed | tf_op | source)
XLA Modules:
  0.0 231.6 jit_solution(16562029184180717208)
XLA Ops:
  7.2 3.6 %collective-permute-start = (bf16[8,16,16,32]{3,2,1,0:T(8,128)(2,1)}, bf16[8,16,16,32]{3,2,1,0:T(8,128)(2,1)S(1)}, u32[]{:S(2)}, u32[]{:S(2)}) collective-permute-start(bf16[8,16,16,32]{3,2,1,0:T(8,128)(2,1)} %param.8), channel_id=1, source_target_pairs={{0,3},{1,0},{2,1},{3,2},{4,7},{5,4},{6,5},{7,6},{8,11},{9,8},{10,9... | collective-permute-start | bytes 393224 | tf_op jit(solution)/shard_map/ppermute | solution.py:20
  11.2 0.7 collective-permute-start.2
  11.9 1.9 bitcast_dynamic-update-slice_fusion.6
  13.8 0.9 fusion.34
  14.7 18.1 %collective-permute-done = bf16[8,16,16,32]{3,2,1,0:T(8,128)(2,1)S(1)} collective-permute-done((bf16[8,16,16,32]{3,2,1,0:T(8,128)(2,1)}, bf16[8,16,16,32]{3,2,1,0:T(8,128)(2,1)S(1)}, u32[]{:S(2)}, u32[]{:S(2)}) %collective-permute-start) | collective-permute-done | bytes 131104 | tf_op jit(solution)/shard_map/ppermute | solution.py:20
  32.9 0.8 bitcast_dynamic-update-slice_fusion.4
  33.7 0.8 bitcast_dynamic-update-slice_fusion.2
  34.6 3.1 %collective-permute-done.2 = bf16[8,16,16,32]{3,2,1,0:T(8,128)(2,1)S(1)} collective-permute-done((bf16[8,16,16,32]{3,2,1,0:T(8,128)(2,1)}, bf16[8,16,16,32]{3,2,1,0:T(8,128)(2,1)S(1)}, u32[]{:S(2)}, u32[]{:S(2)}) %collective-permute-start.2) | collective-permute-done | bytes 131104 | tf_op jit(solution)/shard_map/ppermute | solution.py:20
  37.7 0.8 bitcast_dynamic-update-slice_fusion
  38.5 0.8 bitcast_dynamic-update-slice_fusion.7
  39.3 0.8 bitcast_dynamic-update-slice_fusion.5
  40.2 0.8 bitcast_dynamic-update-slice_fusion.3
  41.0 0.8 bitcast_dynamic-update-slice_fusion.1
  41.8 2.0 dynamic-slice_bitcast_fusion
  43.8 2.7 %copy.13 = bf16[8,16,16,4,32]{4,3,2,1,0:T(4,128)(2,1)S(1)} copy(bf16[8,16,16,4,32]{4,2,1,0,3:T(8,128)(2,1)S(1)} %dynamic-slice_bitcast_fusion) | data formatting | bytes 1048576 | tf_op jit(solution)/shard_map/transpose | solution.py:151
  46.5 1.8 reshape.125
  48.2 1.5 broadcast_multiply_fusion
  49.7 2.4 %collective-permute-start.4 = (bf16[1,16,16,128]{3,2,1,0:T(8,128)(2,1)S(1)}, bf16[1,16,16,128]{3,2,1,0:T(8,128)(2,1)S(1)}, u32[]{:S(2)}, u32[]{:S(2)}) collective-permute-start(bf16[1,16,16,128]{3,2,1,0:T(8,128)(2,1)S(1)} %get-tuple-element.5), channel_id=1, source_target_pairs={{4,0},{8,4},{12,8},{16,12},{20,16},{24,20},{28,24},{32,28},{36,32}... | collective-permute-start | bytes 196616 | tf_op jit(solution)/shard_map/ppermute | solution.py:114
  52.1 3.3 %collective-permute-start.3 = (bf16[1,16,16,128]{3,2,1,0:T(8,128)(2,1)S(1)}, bf16[1,16,16,128]{3,2,1,0:T(8,128)(2,1)S(1)}, u32[]{:S(2)}, u32[]{:S(2)}) collective-permute-start(bf16[1,16,16,128]{3,2,1,0:T(8,128)(2,1)S(1)} %get-tuple-element.4), channel_id=1, source_target_pairs={{0,4},{4,8},{8,12},{12,16},{16,20},{20,24},{24,28},{28,32},{32,36}... | collective-permute-start | bytes 196616 | tf_op jit(solution)/shard_map/ppermute | solution.py:112
  55.5 1.1 collective-permute-done.3
  57.6 6.2 %fusion.8 = f32[8,16,8,3,128]{4,2,3,1,0:T(8,128)S(1)} fusion(bf16[3,3,3,128,128]{4,3,2,1,0:T(8,128)(2,1)S(1)} %bitcast.96, bf16[10,16,1,7,2,128]{5,3,4,1,0,2:T(8,128)(2,1)S(1)} %slice.33, bf16[10,16,1,8,3,128]{5,3,4,1,0,2:T(8,128)(2,1)S(1)} %copy.16, pred[8,3]{0,1:T(4,128)(4,1)S(1)} %copy-done.15), kind=kOutput, calls=%fused_computation.9 | convolution fusion | flops 2609971200 | bytes 4014104 | tf_op jit(solution)/shard_map/conv_general_dilated | solution.py:123
  64.1 0.5 multiply_convert_fusion.1
  64.7 0.8 copy-done.3
  65.5 0.6 fusion.31
  66.1 1.9 collective-permute-start.6
  68.0 4.5 %collective-permute-start.5 = (bf16[1,16,16,128]{3,2,1,0:T(8,128)(2,1)}, bf16[1,16,16,128]{3,2,1,0:T(8,128)(2,1)}, u32[]{:S(2)}, u32[]{:S(2)}) collective-permute-start(bf16[1,16,16,128]{3,2,1,0:T(8,128)(2,1)} %get-tuple-element.2), channel_id=1, source_target_pairs={{0,4},{4,8},{8,12},{12,16},{16,20},{20,24},{24,28},{28,32},{32,36}... | collective-permute-start | bytes 196616 | tf_op jit(solution)/shard_map/ppermute | solution.py:112
  72.5 1.0 reshape.133
  73.5 1.0 mul.90
  74.5 0.9 mul.92
  75.4 1.7 reduce_max.9
  77.1 0.7 convert_element_type.69
  77.8 1.2 copy.22
  79.0 1.8 reshape.128
  80.8 1.2 maximum_bitcast_fusion.1
  82.0 11.7 %fusion.11 = f32[1,8,16,16,128]{4,0,3,2,1:T(1,128)S(1)} fusion(bf16[3,3,3,128,128]{4,3,2,1,0:T(8,128)(2,1)} %bitcast.97, bf16[1,10,16,16,128]{4,3,2,1,0:T(8,128)(2,1)S(1)} %maximum_bitcast_fusion.1), kind=kOutput, calls=%fused_computation.10 | convolution fusion | flops 1664090112 | bytes 2588672 | tf_op jit(solution)/shard_map/conv_general_dilated | solution.py:123
  93.7 2.5 %fusion.19 = bf16[4,8,8,2,2,2,128]{6,5,2,4,1,3,0:T(2,128)(2,1)S(1)} fusion(f32[4,2,8,2,8,2,128]{6,5,4,3,2,1,0:T(2,128)S(1)} %bitcast.83, bf16[4,2,8,2,8,2,128]{6,5,4,3,2,1,0:T(2,128)(2,1)S(1)} %copy-done.5, f32[4,2,8,2,8,2]{5,4,3,2,1,0:T(8,128)S(1)} %copy-done.6, bf16[4,2,8,2,8,2]{5,4,3,2,1,0:T(8,128)(2,1)S(1)} %copy-done.9), kind=kLoop, calls=%fused_computation.27 | loop fusion | flops 1310720 | bytes 2109440 | tf_op jit(solution)/shard_map/transpose | solution.py:136
  97.6 1.6 pad_maximum_fusion
  99.3 1.6 collective-permute-done.7
  100.9 1.1 maximum_select_fusion
  102.2 0.7 fusion.33
  102.9 0.7 fusion.25
  103.7 0.8 constant_dynamic-slice_fusion.6
  104.5 1.3 collective-permute-start.12
  105.8 0.7 collective-permute-start.14
  106.5 1.4 constant_dynamic-update-slice_fusion.9
  107.8 0.6 constant_dynamic-update-slice_fusion.8
  108.5 1.7 collective-permute-done.13
  110.1 0.6 constant_dynamic-update-slice_fusion.7
  110.7 0.6 constant_dynamic-update-slice_fusion.6
  111.4 1.4 constant_dynamic-update-slice_fusion.5
  112.7 0.6 constant_dynamic-update-slice_fusion.4
  113.3 0.6 constant_dynamic-update-slice_fusion.3
  113.9 0.6 constant_dynamic-update-slice_fusion.2
  114.6 72.0 %all-gather.3.cloned.1.call-done = bf16[16896,128]{1,0:T(8,128)(2,1)} async-done(((bf16[528,128]{1,0:T(8,128)(2,1)}), bf16[16896,128]{1,0:T(8,128)(2,1)}) %all-gather.3.cloned.1.call-update) | async-done | bytes 4325392 | tf_op jit(solution)/shard_map/all_gather | solution.py:197
  186.5 21.3 %shard_map.95 = bf16[512,64]{1,0:T(8,128)(2,1)} custom-call(bf16[512,128]{1,0:T(8,128)(2,1)} %get-tuple-element.7.refs_0_, bf16[32,528,128]{2,1,0:T(8,128)(2,1)} %bitcast.82), custom_call_target="tpu_custom_call" | custom-call | tf_op jit(solution)/shard_map/pallas_call | solution.py:88
  207.8 0.9 constant_dynamic-slice_fusion.2
  208.7 4.1 %collective-permute-start.8 = (bf16[256,64]{1,0:T(8,128)(2,1)S(1)}, bf16[256,64]{1,0:T(8,128)(2,1)S(1)}, u32[]{:S(2)}, u32[]{:S(2)}) collective-permute-start(bf16[256,64]{1,0:T(8,128)(2,1)S(1)} %get-tuple-element.13), channel_id=1, source_target_pairs={{0,4},{4,0},{1,5},{5,1},{2,6},{6,2},{3,7},{7,3},{8,12},{12,8},{9,1... | collective-permute-start | bytes 98312 | tf_op jit(solution)/shard_map/ppermute | solution.py:201
  212.8 1.5 fusion.17
  214.4 2.5 %collective-permute-start.9 = (bf16[256,128]{1,0:T(8,128)(2,1)S(1)}, bf16[256,128]{1,0:T(8,128)(2,1)S(1)}, u32[]{:S(2)}, u32[]{:S(2)}) collective-permute-start(bf16[256,128]{1,0:T(8,128)(2,1)S(1)} %maximum_select_fusion.2), channel_id=1, source_target_pairs={{0,3},{1,0},{2,1},{3,2},{4,7},{5,4},{6,5},{7,6},{8,11},{9,8},{10,9... | collective-permute-start | bytes 196616 | tf_op jit(solution)/shard_map/ppermute | solution.py:20
  217.0 0.5 collective-permute-start.10
  217.5 0.6 collective-permute-start.11
  218.3 3.3 %collective-permute-done.10 = bf16[256,128]{1,0:T(8,128)(2,1)S(1)} collective-permute-done((bf16[256,128]{1,0:T(8,128)(2,1)S(1)}, bf16[256,128]{1,0:T(8,128)(2,1)S(1)}, u32[]{:S(2)}, u32[]{:S(2)}) %collective-permute-start.10) | collective-permute-done | bytes 65568 | tf_op jit(solution)/shard_map/ppermute | solution.py:20
  221.7 2.0 collective-permute-done.11
  223.9 0.9 fusion.15
  (71 shorter events, 3.8 us)
Async XLA Ops:
  7.2 89.2 %copy-start = (bf16[8,128,512]{2,1,0:T(8,128)(2,1)S(1)}, bf16[8,128,512]{2,1,0:T(8,128)(2,1)}, u32[]{:S(2)}) copy-start(bf16[8,128,512]{2,1,0:T(8,128)(2,1)} %param.12) | copy-start | bytes 3145732
  7.2 31.3 %copy-start.4 = (bf16[8,16,16,32]{3,2,1,0:T(8,128)(2,1)S(1)}, bf16[8,16,16,32]{3,2,1,0:T(8,128)(2,1)}, u32[]{:S(2)}) copy-start(bf16[8,16,16,32]{3,2,1,0:T(8,128)(2,1)} %param.8) | copy-start | bytes 393220
  7.2 179.3 %all-gather.3.cloned.1.call-start = ((), (), s32[]{:S(2)}) async-start(), calls=%async_computation | async-start | bytes 4460544 | tf_op jit(solution)/shard_map/all_gather | solution.py:197
  7.2 25.6 %collective-permute-start = (bf16[8,16,16,32]{3,2,1,0:T(8,128)(2,1)}, bf16[8,16,16,32]{3,2,1,0:T(8,128)(2,1)S(1)}, u32[]{:S(2)}, u32[]{:S(2)}) collective-permute-start(bf16[8,16,16,32]{3,2,1,0:T(8,128)(2,1)} %param.8), channel_id=1, source_target_pairs={{0,3},{1,0},{2,1},{3,2},{4,7},{5,4},{6,5},{7,6},{8,11},{9,8},{10,9... | collective-permute-start | bytes 393224 | tf_op jit(solution)/shard_map/ppermute | solution.py:20
  10.9 22.9 %collective-permute-start.1 = (bf16[8,16,16,32]{3,2,1,0:T(8,128)(2,1)}, bf16[8,16,16,32]{3,2,1,0:T(8,128)(2,1)S(1)}, u32[]{:S(2)}, u32[]{:S(2)}) collective-permute-start(bf16[8,16,16,32]{3,2,1,0:T(8,128)(2,1)} %param.8), channel_id=1, source_target_pairs={{0,2},{1,3},{2,0},{3,1},{4,6},{5,7},{6,4},{7,5},{8,10},{9,11},{10,... | collective-permute-start | bytes 393224 | tf_op jit(solution)/shard_map/ppermute | solution.py:20
  11.2 26.4 %collective-permute-start.2 = (bf16[8,16,16,32]{3,2,1,0:T(8,128)(2,1)}, bf16[8,16,16,32]{3,2,1,0:T(8,128)(2,1)S(1)}, u32[]{:S(2)}, u32[]{:S(2)}) collective-permute-start(bf16[8,16,16,32]{3,2,1,0:T(8,128)(2,1)} %param.8), channel_id=1, source_target_pairs={{0,1},{1,2},{2,3},{3,0},{4,5},{5,6},{6,7},{7,4},{8,9},{9,10},{10,1... | collective-permute-start | bytes 393224 | tf_op jit(solution)/shard_map/ppermute | solution.py:20
  14.7 58.8 %copy-start.7 = (f32[8,16,16]{2,1,0:T(8,128)}, f32[8,16,16]{2,1,0:T(8,128)S(1)}, u32[]{:S(2)}) copy-start(f32[8,16,16]{2,1,0:T(8,128)S(1)} %get-tuple-element.15) | copy-start | bytes 24580
  48.2 9.3 %copy-start.14 = (bf16[27,128,128]{2,1,0:T(8,128)(2,1)S(1)}, bf16[27,128,128]{2,1,0:T(8,128)(2,1)}, u32[]{:S(2)}) copy-start(bf16[27,128,128]{2,1,0:T(8,128)(2,1)} %param.10) | copy-start | bytes 2654212
  48.2 9.3 %copy-start.15 = (pred[8,3]{0,1:T(4,128)(4,1)S(1)}, pred[8,3]{0,1:T(4,128)(4,1)}, u32[]{:S(2)}) copy-start(pred[8,3]{0,1:T(4,128)(4,1)} %constant.89) | copy-start | bytes 76
  49.7 6.9 %copy-start.1 = (bf16[8,16,16,128]{3,2,1,0:T(8,128)(2,1)}, bf16[8,16,16,128]{3,2,1,0:T(8,128)(2,1)S(1)}, u32[]{:S(2)}) copy-start(bf16[8,16,16,128]{3,2,1,0:T(8,128)(2,1)S(1)} %broadcast_multiply_fusion) | copy-start | bytes 1572868
  49.7 5.8 %collective-permute-start.4 = (bf16[1,16,16,128]{3,2,1,0:T(8,128)(2,1)S(1)}, bf16[1,16,16,128]{3,2,1,0:T(8,128)(2,1)S(1)}, u32[]{:S(2)}, u32[]{:S(2)}) collective-permute-start(bf16[1,16,16,128]{3,2,1,0:T(8,128)(2,1)S(1)} %get-tuple-element.5), channel_id=1, source_target_pairs={{4,0},{8,4},{12,8},{16,12},{20,16},{24,20},{28,24},{32,28},{36,32}... | collective-permute-start | bytes 196616 | tf_op jit(solution)/shard_map/ppermute | solution.py:114
  52.1 4.5 %collective-permute-start.3 = (bf16[1,16,16,128]{3,2,1,0:T(8,128)(2,1)S(1)}, bf16[1,16,16,128]{3,2,1,0:T(8,128)(2,1)S(1)}, u32[]{:S(2)}, u32[]{:S(2)}) collective-permute-start(bf16[1,16,16,128]{3,2,1,0:T(8,128)(2,1)S(1)} %get-tuple-element.4), channel_id=1, source_target_pairs={{0,4},{4,8},{8,12},{12,16},{16,20},{20,24},{24,28},{28,32},{32,36}... | collective-permute-start | bytes 196616 | tf_op jit(solution)/shard_map/ppermute | solution.py:112
  63.8 8.8 %copy-start.10 = (s32[8,16,16]{2,1,0:T(8,128)S(1)}, s32[8,16,16]{2,1,0:T(8,128)}, u32[]{:S(2)}) copy-start(s32[8,16,16]{2,1,0:T(8,128)} %param.9) | copy-start | bytes 24580
  64.7 0.8 copy-start.3
  66.1 14.7 %collective-permute-start.6 = (bf16[1,16,16,128]{3,2,1,0:T(8,128)(2,1)}, bf16[1,16,16,128]{3,2,1,0:T(8,128)(2,1)}, u32[]{:S(2)}, u32[]{:S(2)}) collective-permute-start(bf16[1,16,16,128]{3,2,1,0:T(8,128)(2,1)} %get-tuple-element.3), channel_id=1, source_target_pairs={{4,0},{8,4},{12,8},{16,12},{20,16},{24,20},{28,24},{32,28},{36,32}... | collective-permute-start | bytes 196616 | tf_op jit(solution)/shard_map/ppermute | solution.py:114
  68.0 12.7 %collective-permute-start.5 = (bf16[1,16,16,128]{3,2,1,0:T(8,128)(2,1)}, bf16[1,16,16,128]{3,2,1,0:T(8,128)(2,1)}, u32[]{:S(2)}, u32[]{:S(2)}) collective-permute-start(bf16[1,16,16,128]{3,2,1,0:T(8,128)(2,1)} %get-tuple-element.2), channel_id=1, source_target_pairs={{0,4},{4,8},{8,12},{12,16},{16,20},{20,24},{24,28},{28,32},{32,36}... | collective-permute-start | bytes 196616 | tf_op jit(solution)/shard_map/ppermute | solution.py:112
  81.9 11.8 %copy-start.5 = (bf16[4,2,8,2,8,2,128]{6,5,4,3,2,1,0:T(2,128)(2,1)S(1)}, bf16[4,2,8,2,8,2,128]{6,5,4,3,2,1,0:T(2,128)(2,1)}, u32[]{:S(2)}) copy-start(bf16[4,2,8,2,8,2,128]{6,5,4,3,2,1,0:T(2,128)(2,1)} %reshape.128) | copy-start | bytes 1572868
  81.9 11.8 %copy-start.6 = (f32[4,2,8,2,8,2]{5,4,3,2,1,0:T(8,128)S(1)}, f32[4,2,8,2,8,2]{5,4,3,2,1,0:T(8,128)}, u32[]{:S(2)}) copy-start(f32[4,2,8,2,8,2]{5,4,3,2,1,0:T(8,128)} %mul.90) | copy-start | bytes 24580
  82.0 11.8 %copy-start.9 = (bf16[4,2,8,2,8,2]{5,4,3,2,1,0:T(8,128)(2,1)S(1)}, bf16[4,2,8,2,8,2]{5,4,3,2,1,0:T(8,128)(2,1)}, u32[]{:S(2)}) copy-start(bf16[4,2,8,2,8,2]{5,4,3,2,1,0:T(8,128)(2,1)} %mul.92) | copy-start | bytes 12292
  93.7 3.2 %copy-start.12 = (f32[512]{0:T(512)S(1)}, f32[512]{0:T(512)}, u32[]{:S(2)}) copy-start(f32[512]{0:T(512)} %param.13) | copy-start | bytes 6148
  93.7 8.5 %copy-start.13 = (pred[128]{0:T(512)(128)(4,1)S(1)}, pred[128]{0:T(512)(128)(4,1)}, u32[]{:S(2)}) copy-start(pred[128]{0:T(512)(128)(4,1)} %constant.72.clone.1) | copy-start | bytes 388
  97.5 115.3 %copy-start.2 = (bf16[8,16,16,128]{3,2,1,0:T(8,128)(2,1)S(1)}, bf16[8,16,16,128]{3,2,1,0:T(8,128)(2,1)}, u32[]{:S(2)}) copy-start(bf16[8,16,16,128]{3,2,1,0:T(8,128)(2,1)} %copy-done.1) | copy-start | bytes 1572868
  97.5 115.3 %copy-start.8 = (f32[8,16,16]{2,1,0:T(8,128)S(1)}, f32[8,16,16]{2,1,0:T(8,128)}, u32[]{:S(2)}) copy-start(f32[8,16,16]{2,1,0:T(8,128)} %copy-done.7) | copy-start | bytes 24580
  99.2 1.7 collective-permute-start.7
  104.5 3.4 %collective-permute-start.12 = (bf16[128,128]{1,0:T(8,128)(2,1)S(1)}, bf16[128,128]{1,0:T(8,128)(2,1)S(1)}, u32[]{:S(2)}, u32[]{:S(2)}) collective-permute-start(bf16[128,128]{1,0:T(8,128)(2,1)S(1)} %get-tuple-element.11), channel_id=1, source_target_pairs={{0,3},{1,0},{2,1},{3,2},{4,7},{5,4},{6,5},{7,6},{8,11},{9,8},{10,9... | collective-permute-start | bytes 98312 | tf_op jit(solution)/shard_map/ppermute | solution.py:20
  105.8 4.3 %collective-permute-start.13 = (bf16[128,128]{1,0:T(8,128)(2,1)S(1)}, bf16[128,128]{1,0:T(8,128)(2,1)S(1)}, u32[]{:S(2)}, u32[]{:S(2)}) collective-permute-start(bf16[128,128]{1,0:T(8,128)(2,1)S(1)} %get-tuple-element.12), channel_id=1, source_target_pairs={{0,2},{1,3},{2,0},{3,1},{4,6},{5,7},{6,4},{7,5},{8,10},{9,11},{10,... | collective-permute-start | bytes 98312 | tf_op jit(solution)/shard_map/ppermute | solution.py:20
  105.8 4.9 %collective-permute-start.14 = (bf16[128,128]{1,0:T(8,128)(2,1)S(1)}, bf16[128,128]{1,0:T(8,128)(2,1)S(1)}, u32[]{:S(2)}, u32[]{:S(2)}) collective-permute-start(bf16[128,128]{1,0:T(8,128)(2,1)S(1)} %get-tuple-element.10), channel_id=1, source_target_pairs={{0,1},{1,2},{2,3},{3,0},{4,5},{5,6},{6,7},{7,4},{8,9},{9,10},{10,1... | collective-permute-start | bytes 98312 | tf_op jit(solution)/shard_map/ppermute | solution.py:20
  186.5 37.4 %copy-start.11 = (bf16[8,128,128]{2,1,0:T(8,128)(2,1)S(1)}, bf16[8,128,128]{2,1,0:T(8,128)(2,1)}, u32[]{:S(2)}) copy-start(bf16[8,128,128]{2,1,0:T(8,128)(2,1)} %constant_dynamic-update-slice_fusion.2) | copy-start | bytes 786436
  208.7 5.6 %collective-permute-start.8 = (bf16[256,64]{1,0:T(8,128)(2,1)S(1)}, bf16[256,64]{1,0:T(8,128)(2,1)S(1)}, u32[]{:S(2)}, u32[]{:S(2)}) collective-permute-start(bf16[256,64]{1,0:T(8,128)(2,1)S(1)} %get-tuple-element.13), channel_id=1, source_target_pairs={{0,4},{4,0},{1,5},{5,1},{2,6},{6,2},{3,7},{7,3},{8,12},{12,8},{9,1... | collective-permute-start | bytes 98312 | tf_op jit(solution)/shard_map/ppermute | solution.py:201
  214.4 3.9 %collective-permute-start.9 = (bf16[256,128]{1,0:T(8,128)(2,1)S(1)}, bf16[256,128]{1,0:T(8,128)(2,1)S(1)}, u32[]{:S(2)}, u32[]{:S(2)}) collective-permute-start(bf16[256,128]{1,0:T(8,128)(2,1)S(1)} %maximum_select_fusion.2), channel_id=1, source_target_pairs={{0,3},{1,0},{2,1},{3,2},{4,7},{5,4},{6,5},{7,6},{8,11},{9,8},{10,9... | collective-permute-start | bytes 196616 | tf_op jit(solution)/shard_map/ppermute | solution.py:20
  217.0 4.7 %collective-permute-start.10 = (bf16[256,128]{1,0:T(8,128)(2,1)S(1)}, bf16[256,128]{1,0:T(8,128)(2,1)S(1)}, u32[]{:S(2)}, u32[]{:S(2)}) collective-permute-start(bf16[256,128]{1,0:T(8,128)(2,1)S(1)} %maximum_select_fusion.2), channel_id=1, source_target_pairs={{0,2},{1,3},{2,0},{3,1},{4,6},{5,7},{6,4},{7,5},{8,10},{9,11},{10,... | collective-permute-start | bytes 196616 | tf_op jit(solution)/shard_map/ppermute | solution.py:20
  217.5 6.2 %collective-permute-start.11 = (bf16[256,128]{1,0:T(8,128)(2,1)S(1)}, bf16[256,128]{1,0:T(8,128)(2,1)S(1)}, u32[]{:S(2)}, u32[]{:S(2)}) collective-permute-start(bf16[256,128]{1,0:T(8,128)(2,1)S(1)} %maximum_select_fusion.2), channel_id=1, source_target_pairs={{0,1},{1,2},{2,3},{3,0},{4,5},{5,6},{6,7},{7,4},{8,9},{9,10},{10,1... | collective-permute-start | bytes 196616 | tf_op jit(solution)/shard_map/ppermute | solution.py:20
Sparse Core Ops, SparseCore 0:
  103.8 82.7 all-gather.2
